TPU v7x, 32 devices: a whole 2x2x4 slice. The times are simulated.
32 devices in a mesh: gx: 4 (over y, x), gy: 8 (over z, core).
Axes of the slice: x: 2, y: 2, z: 4, core: 2. Of those that a mesh axis runs over, the one named last changes fastest.
Arguments:
- basis: float32 [4, 8, 3, 32, 192], P('gx', 'gy'), may hold values from -6 to 6
- coupling: bfloat16 [4, 8, 81, 192, 192], P('gx', 'gy'), as said below
- cpl_dst: int32 [4, 8, 81], P('gx', 'gy'), may hold values from 0 to 3, as said below
- cpl_src: int32 [4, 8, 81], P('gx', 'gy'), may hold values from 0 to 26, as said below
Outputs:
- subspace: float32 [4, 8, 3, 32, 192], P('gx', 'gy')
Inputs may be any that keep to these rules, and one draw needn't show every extreme that they name: `cpl_dst`: on each column the live slots come first; a live slot holds its target block's height 0 to 2, every later slot holds 3. The columns at gx index 0 have all 81 slots live. `cpl_src`: A live slot holds (3 dx + dy) * 3 + z for a source block in the column at offsets dx - 1, dy - 1 (periodic) and height z, within one height of the target block, periodically; each source block and column offset appears at most once per target; empty slots hold 0. `coupling`: the assembled matrix is symmetric: for every live slot that couples block i to block j there is a live slot on j's column that couples j to i and holds the transposed block.
All inputs are finite; a program needn't handle non-finite values.
Results may differ from a plain program's by a relative error of at most 0.0085.
Values may be sent and summed in bfloat16 or wider, within the bound.
No kernel may reach another device: no remote copies, remote signals or barrier semaphores. Data moves between devices by JAX's collectives and lax.ppermute only.
A program may use at most 64 MiB of HBM per device.

v0:
```python
import math

import jax
import jax.numpy as jnp
from jax import lax
from jax.sharding import PartitionSpec as P

DEGREE = 8
STEPS = 2


CENTER = 5.0
HALF = 3.0
LOWEST = 0.5


def with_halo(cells, sides, width):
    for axis, dim in sides:
        count = lax.axis_size(axis)
        head = lax.slice_in_dim(cells, 0, width, axis=dim)
        tail = lax.slice_in_dim(cells, cells.shape[dim] - width, cells.shape[dim], axis=dim)
        cells = jnp.concatenate(
            [
                lax.ppermute(tail, axis, [(i, (i + 1) % count) for i in range(count)]),
                cells,
                lax.ppermute(head, axis, [((i + 1) % count, i) for i in range(count)]),
            ],
            axis=dim,
        )
    return cells


def orthonormal(filtered, rows_total):
    local_block = filtered[0, 0]
    partial_gram = jnp.einsum(
        "zvd,zwd->vw", local_block, local_block, precision=lax.Precision.HIGHEST
    )
    gram_matrix = lax.psum(partial_gram, ("gx", "gy"))
    factor = jnp.linalg.cholesky(gram_matrix)
    identity = jnp.eye(local_block.shape[1], dtype=jnp.float32)
    inverse = jax.scipy.linalg.solve_triangular(factor, identity, lower=True)
    result = jnp.einsum("vw,zwd->zvd", inverse, local_block, precision=lax.Precision.HIGHEST)
    return (result * math.sqrt(rows_total))[None, None]


def local(basis, coupling, cpl_dst, cpl_src):
    column_depth = basis.shape[2]
    vector_count = basis.shape[3]
    block_rows = basis.shape[4]
    matrices = coupling[0, 0]
    targets = cpl_dst[0, 0]
    sources = cpl_src[0, 0]
    rows_total = lax.axis_size("gx") * lax.axis_size("gy") * column_depth * block_rows
    select = (targets[None, :] == jnp.arange(column_depth, dtype=jnp.int32)[:, None]).astype(
        jnp.float32
    )

    def apply_operator(current):
        rounded = current.astype(jnp.bfloat16)
        window = with_halo(rounded, (("gx", 0), ("gy", 1)), 1)
        window_cells = window.reshape(9 * column_depth, vector_count, block_rows)
        picked = jnp.take(window_cells, sources, axis=0)
        products = jnp.einsum("kvj,kij->kvi", picked, matrices, preferred_element_type=jnp.float32)
        applied = jnp.einsum("zk,kvi->zvi", select, products, precision=lax.Precision.HIGHEST)
        return applied[None, None]

    sigma_one = HALF / (LOWEST - CENTER)
    current_basis = basis
    for outer in range(STEPS):
        previous = current_basis
        current = sigma_one / HALF * (apply_operator(previous) - CENTER * previous)
        sigma_now = sigma_one
        for inner in range(1, DEGREE):
            sigma_next = 1.0 / (2.0 / sigma_one - sigma_now)
            image = apply_operator(current)
            following = (
                2.0 * sigma_next / HALF * (image - CENTER * current)
                - sigma_now * sigma_next * previous
            )
            previous, current, sigma_now = (current, following, sigma_next)
        current_basis = orthonormal(current, rows_total)
    return current_basis


def solution(mesh):
    placed = (
        P("gx", "gy", None, None, None),
        P("gx", "gy", None, None, None),
        P("gx", "gy", None),
        P("gx", "gy", None),
    )
    return jax.shard_map(
        local,
        mesh=mesh,
        in_specs=placed,
        out_specs=P("gx", "gy", None, None, None),
        check_vma=False,
    )
```

profile of v0, /device:TPU:0, one launch (start us, length us, event | category | flops | bytes accessed | tf_op | source)
XLA Modules:
  0.0 457.6 jit_solution(3541501361220826311)
XLA Ops:
  0.9 3.9 collective-permute-start.1
  6.5 3.2 collective-permute-done
  11.5 3.7 collective-permute-done.3
  15.2 3.0 collective-permute-done.2
  19.0 5.8 %fusion.30 = f32[81,32,192]{2,1,0:T(8,128)S(1)} fusion(bf16[1,1,81,192,192]{4,3,2,1,0:T(8,128)(2,1)} %param.10, bf16[81,32,192]{2,1,0:T(8,128)(2,1)S(1)} %gather_fusion, pred[81]{0:T(512)(128)(4,1)S(1)} %compare_and_fusion), kind=kOutput, calls=%fused_computation.46 | convolution fusion | flops 191600640 | bytes 8958033 | tf_op jit(solution)/shard_map/kvj,kij->kvi/dot_general | solution.py:63
  24.9 2.6 multiply_convert_fusion
  33.4 4.6 %collective-permute-done.7 = bf16[3,1,3,32,192]{4,2,3,1,0:T(4,128)(2,1)S(1)} collective-permute-done((bf16[3,1,3,32,192]{4,2,3,1,0:T(4,128)(2,1)S(1)}, bf16[3,1,3,32,192]{4,2,3,1,0:T(4,128)(2,1)S(1)}, u32[]{:S(2)}, u32[]{:S(2)}) %collective-permute-start.7) | collective-permute-done | bytes 110624 | tf_op jit(solution)/shard_map/ppermute | solution.py:26
  41.6 5.8 %fusion.28 = f32[81,32,192]{2,1,0:T(8,128)S(1)} fusion(bf16[1,1,81,192,192]{4,3,2,1,0:T(8,128)(2,1)} %param.10, bf16[81,32,192]{2,1,0:T(8,128)(2,1)S(1)} %gather_fusion.1, pred[81]{0:T(512)(128)(4,1)S(1)} %compare_and_fusion), kind=kOutput, calls=%fused_computation.44 | convolution fusion | flops 191600640 | bytes 8958033 | tf_op jit(solution)/shard_map/kvj,kij->kvi/dot_general | solution.py:63
  47.4 2.6 fusion.269
  58.1 3.8 collective-permute-done.11
  61.9 3.1 collective-permute-done.10
  66.4 5.8 %fusion.26 = f32[81,32,192]{2,1,0:T(8,128)S(1)} fusion(bf16[1,1,81,192,192]{4,3,2,1,0:T(8,128)(2,1)} %param.10, bf16[81,32,192]{2,1,0:T(8,128)(2,1)S(1)} %gather_fusion.2, pred[81]{0:T(512)(128)(4,1)S(1)} %compare_and_fusion), kind=kOutput, calls=%fused_computation.42 | convolution fusion | flops 191600640 | bytes 8958033 | tf_op jit(solution)/shard_map/kvj,kij->kvi/dot_general | solution.py:63
  72.2 2.5 fusion.270
  81.6 4.6 %collective-permute-done.15 = bf16[3,1,3,32,192]{4,2,3,1,0:T(4,128)(2,1)S(1)} collective-permute-done((bf16[3,1,3,32,192]{4,2,3,1,0:T(4,128)(2,1)S(1)}, bf16[3,1,3,32,192]{4,2,3,1,0:T(4,128)(2,1)S(1)}, u32[]{:S(2)}, u32[]{:S(2)}) %collective-permute-start.15) | collective-permute-done | bytes 110624 | tf_op jit(solution)/shard_map/ppermute | solution.py:26
  89.4 5.8 %fusion.24 = f32[81,32,192]{2,1,0:T(8,128)S(1)} fusion(bf16[1,1,81,192,192]{4,3,2,1,0:T(8,128)(2,1)} %param.10, bf16[81,32,192]{2,1,0:T(8,128)(2,1)S(1)} %gather_fusion.3, pred[81]{0:T(512)(128)(4,1)S(1)} %compare_and_fusion), kind=kOutput, calls=%fused_computation.40 | convolution fusion | flops 191600640 | bytes 8958033 | tf_op jit(solution)/shard_map/kvj,kij->kvi/dot_general | solution.py:63
  95.2 2.5 fusion.271
  104.8 4.8 %collective-permute-done.19 = bf16[3,1,3,32,192]{4,2,3,1,0:T(4,128)(2,1)S(1)} collective-permute-done((bf16[3,1,3,32,192]{4,2,3,1,0:T(4,128)(2,1)S(1)}, bf16[3,1,3,32,192]{4,2,3,1,0:T(4,128)(2,1)S(1)}, u32[]{:S(2)}, u32[]{:S(2)}) %collective-permute-start.19) | collective-permute-done | bytes 110624 | tf_op jit(solution)/shard_map/ppermute | solution.py:26
  112.9 5.8 %fusion.22 = f32[81,32,192]{2,1,0:T(8,128)S(1)} fusion(bf16[1,1,81,192,192]{4,3,2,1,0:T(8,128)(2,1)} %param.10, bf16[81,32,192]{2,1,0:T(8,128)(2,1)S(1)} %gather_fusion.4, pred[81]{0:T(512)(128)(4,1)S(1)} %compare_and_fusion), kind=kOutput, calls=%fused_computation.38 | convolution fusion | flops 191600640 | bytes 8958033 | tf_op jit(solution)/shard_map/kvj,kij->kvi/dot_general | solution.py:63
  118.7 2.5 fusion.272
  127.5 4.6 %collective-permute-done.23 = bf16[3,1,3,32,192]{4,2,3,1,0:T(4,128)(2,1)S(1)} collective-permute-done((bf16[3,1,3,32,192]{4,2,3,1,0:T(4,128)(2,1)S(1)}, bf16[3,1,3,32,192]{4,2,3,1,0:T(4,128)(2,1)S(1)}, u32[]{:S(2)}, u32[]{:S(2)}) %collective-permute-start.23) | collective-permute-done | bytes 110624 | tf_op jit(solution)/shard_map/ppermute | solution.py:26
  135.5 5.8 %fusion.20 = f32[81,32,192]{2,1,0:T(8,128)S(1)} fusion(bf16[1,1,81,192,192]{4,3,2,1,0:T(8,128)(2,1)} %param.10, bf16[81,32,192]{2,1,0:T(8,128)(2,1)S(1)} %gather_fusion.5, pred[81]{0:T(512)(128)(4,1)S(1)} %compare_and_fusion), kind=kOutput, calls=%fused_computation.36 | convolution fusion | flops 191600640 | bytes 8958033 | tf_op jit(solution)/shard_map/kvj,kij->kvi/dot_general | solution.py:63
  141.3 2.5 fusion.273
  151.0 4.6 %collective-permute-done.27 = bf16[3,1,3,32,192]{4,2,3,1,0:T(4,128)(2,1)S(1)} collective-permute-done((bf16[3,1,3,32,192]{4,2,3,1,0:T(4,128)(2,1)S(1)}, bf16[3,1,3,32,192]{4,2,3,1,0:T(4,128)(2,1)S(1)}, u32[]{:S(2)}, u32[]{:S(2)}) %collective-permute-start.27) | collective-permute-done | bytes 110624 | tf_op jit(solution)/shard_map/ppermute | solution.py:26
  159.0 5.8 %fusion.18 = f32[81,32,192]{2,1,0:T(8,128)S(1)} fusion(bf16[1,1,81,192,192]{4,3,2,1,0:T(8,128)(2,1)} %param.10, bf16[81,32,192]{2,1,0:T(8,128)(2,1)S(1)} %gather_fusion.6, pred[81]{0:T(512)(128)(4,1)S(1)} %compare_and_fusion), kind=kOutput, calls=%fused_computation.34 | convolution fusion | flops 191600640 | bytes 8958033 | tf_op jit(solution)/shard_map/kvj,kij->kvi/dot_general | solution.py:63
  164.8 2.5 fusion.274
  174.2 4.6 %collective-permute-done.31 = bf16[3,1,3,32,192]{4,2,3,1,0:T(4,128)(2,1)S(1)} collective-permute-done((bf16[3,1,3,32,192]{4,2,3,1,0:T(4,128)(2,1)S(1)}, bf16[3,1,3,32,192]{4,2,3,1,0:T(4,128)(2,1)S(1)}, u32[]{:S(2)}, u32[]{:S(2)}) %collective-permute-start.31) | collective-permute-done | bytes 110624 | tf_op jit(solution)/shard_map/ppermute | solution.py:26
  182.2 5.8 %fusion.16 = f32[81,32,192]{2,1,0:T(8,128)S(1)} fusion(bf16[1,1,81,192,192]{4,3,2,1,0:T(8,128)(2,1)} %param.10, bf16[81,32,192]{2,1,0:T(8,128)(2,1)S(1)} %gather_fusion.7, pred[81]{0:T(512)(128)(4,1)S(1)} %compare_and_fusion), kind=kOutput, calls=%fused_computation.32 | convolution fusion | flops 191600640 | bytes 8958033 | tf_op jit(solution)/shard_map/kvj,kij->kvi/dot_general | solution.py:63
  188.0 2.5 fusion.130
  190.8 38.4 %psum.14 = f32[32,32]{0,1:T(8,128)S(1)} all-reduce(f32[32,32]{0,1:T(8,128)S(1)} %convolution_bitcast_fusion.3), channel_id=1, replica_groups=mesh['gx'=4,'gy'=8] {'gx','gy'}, use_global_device_ids=true, to_apply=%region_0.0 | all-reduce | flops 1024 | bytes 8192 | tf_op jit(solution)/shard_map/psum | solution.py:38
  229.2 2.9 cholesky.44
  233.5 2.4 custom-call.6
  241.2 2.6 collective-permute-done.32
  246.5 3.9 collective-permute-done.34
  251.2 5.8 %fusion.14 = f32[81,32,192]{2,1,0:T(8,128)S(1)} fusion(bf16[1,1,81,192,192]{4,3,2,1,0:T(8,128)(2,1)} %param.10, bf16[81,32,192]{2,1,0:T(8,128)(2,1)S(1)} %gather_fusion.8, pred[81]{0:T(512)(128)(4,1)S(1)} %compare_and_fusion), kind=kOutput, calls=%fused_computation.30 | convolution fusion | flops 191600640 | bytes 8958033 | tf_op jit(solution)/shard_map/kvj,kij->kvi/dot_general | solution.py:63
  257.1 2.5 fusion.46
  265.8 3.7 collective-permute-done.39
  272.5 5.8 %fusion.12 = f32[81,32,192]{2,1,0:T(8,128)S(1)} fusion(bf16[1,1,81,192,192]{4,3,2,1,0:T(8,128)(2,1)} %param.10, bf16[81,32,192]{2,1,0:T(8,128)(2,1)S(1)} %gather_fusion.9, pred[81]{0:T(512)(128)(4,1)S(1)} %compare_and_fusion), kind=kOutput, calls=%fused_computation.28 | convolution fusion | flops 191600640 | bytes 8958033 | tf_op jit(solution)/shard_map/kvj,kij->kvi/dot_general | solution.py:63
  278.3 2.5 fusion.44
  288.1 3.6 collective-permute-done.43
  291.7 2.4 collective-permute-done.42
  294.9 5.8 %fusion.10 = f32[81,32,192]{2,1,0:T(8,128)S(1)} fusion(bf16[1,1,81,192,192]{4,3,2,1,0:T(8,128)(2,1)} %param.10, bf16[81,32,192]{2,1,0:T(8,128)(2,1)S(1)} %gather_fusion.10, pred[81]{0:T(512)(128)(4,1)S(1)} %compare_and_fusion), kind=kOutput, calls=%fused_computation.26 | convolution fusion | flops 191600640 | bytes 8958033 | tf_op jit(solution)/shard_map/kvj,kij->kvi/dot_general | solution.py:63
  300.7 2.5 fusion.42
  309.5 3.6 collective-permute-done.47
  313.1 2.4 collective-permute-done.46
  316.2 5.8 %fusion.8 = f32[81,32,192]{2,1,0:T(8,128)S(1)} fusion(bf16[1,1,81,192,192]{4,3,2,1,0:T(8,128)(2,1)} %param.10, bf16[81,32,192]{2,1,0:T(8,128)(2,1)S(1)} %gather_fusion.11, pred[81]{0:T(512)(128)(4,1)S(1)} %compare_and_fusion), kind=kOutput, calls=%fused_computation.24 | convolution fusion | flops 191600640 | bytes 8958033 | tf_op jit(solution)/shard_map/kvj,kij->kvi/dot_general | solution.py:63
  322.0 2.5 fusion.40
  331.2 3.5 collective-permute-done.51
  334.8 2.4 collective-permute-done.50
  338.0 5.8 %fusion.6 = f32[81,32,192]{2,1,0:T(8,128)S(1)} fusion(bf16[1,1,81,192,192]{4,3,2,1,0:T(8,128)(2,1)} %param.10, bf16[81,32,192]{2,1,0:T(8,128)(2,1)S(1)} %gather_fusion.12, pred[81]{0:T(512)(128)(4,1)S(1)} %compare_and_fusion), kind=kOutput, calls=%fused_computation.22 | convolution fusion | flops 191600640 | bytes 8958033 | tf_op jit(solution)/shard_map/kvj,kij->kvi/dot_general | solution.py:63
  343.8 2.5 fusion.38
  353.0 3.6 collective-permute-done.55
  356.6 2.4 collective-permute-done.54
  359.7 5.8 %fusion.4 = f32[81,32,192]{2,1,0:T(8,128)S(1)} fusion(bf16[1,1,81,192,192]{4,3,2,1,0:T(8,128)(2,1)} %param.10, bf16[81,32,192]{2,1,0:T(8,128)(2,1)S(1)} %gather_fusion.13, pred[81]{0:T(512)(128)(4,1)S(1)} %compare_and_fusion), kind=kOutput, calls=%fused_computation.20 | convolution fusion | flops 191600640 | bytes 8958033 | tf_op jit(solution)/shard_map/kvj,kij->kvi/dot_general | solution.py:63
  365.5 2.5 fusion.36
  374.8 3.5 collective-permute-done.59
  378.2 2.5 collective-permute-done.58
  381.5 5.8 %fusion.2 = f32[81,32,192]{2,1,0:T(8,128)S(1)} fusion(bf16[1,1,81,192,192]{4,3,2,1,0:T(8,128)(2,1)} %param.10, bf16[81,32,192]{2,1,0:T(8,128)(2,1)S(1)} %gather_fusion.14, pred[81]{0:T(512)(128)(4,1)S(1)} %compare_and_fusion), kind=kOutput, calls=%fused_computation.18 | convolution fusion | flops 191600640 | bytes 8958033 | tf_op jit(solution)/shard_map/kvj,kij->kvi/dot_general | solution.py:63
  387.3 2.5 fusion.34
  396.2 3.6 collective-permute-done.63
  402.9 5.8 %fusion = f32[81,32,192]{2,1,0:T(8,128)S(1)} fusion(bf16[1,1,81,192,192]{4,3,2,1,0:T(8,128)(2,1)} %param.10, bf16[81,32,192]{2,1,0:T(8,128)(2,1)S(1)} %gather_fusion.15, pred[81]{0:T(512)(128)(4,1)S(1)} %compare_and_fusion), kind=kOutput, calls=%fused_computation.16 | convolution fusion | flops 191600640 | bytes 8958033 | tf_op jit(solution)/shard_map/kvj,kij->kvi/dot_general | solution.py:63
  408.7 2.5 fusion.32
  411.6 37.7 %psum.15 = f32[32,32]{0,1:T(8,128)S(1)} all-reduce(f32[32,32]{0,1:T(8,128)S(1)} %convolution_bitcast_fusion.1), channel_id=1, replica_groups=mesh['gx'=4,'gy'=8] {'gx','gy'}, use_global_device_ids=true, to_apply=%region_3.7 | all-reduce | flops 1024 | bytes 8192 | tf_op jit(solution)/shard_map/psum | solution.py:38
  449.4 2.9 cholesky.55
  453.6 2.4 custom-call.7
  (190 shorter events, 144.1 us)
Async XLA Ops:
  0.9 5.6 %collective-permute-start.1 = (bf16[1,1,3,32,192]{4,3,2,1,0:T(8,128)(2,1)S(1)}, bf16[1,1,3,32,192]{4,3,2,1,0:T(8,128)(2,1)S(1)}, u32[]{:S(2)}, u32[]{:S(2)}) collective-permute-start(bf16[1,1,3,32,192]{4,3,2,1,0:T(8,128)(2,1)S(1)} %convert_element_type.82), channel_id=1, source_target_pairs={{8,0},{16,8},{24,16},{0,24},{9,1},{17,9},{25,17},{1,25},{10,2},{18... | collective-permute-start | bytes 110600 | tf_op jit(solution)/shard_map/ppermute | solution.py:26
  4.8 5.0 %collective-permute-start = (bf16[1,1,3,32,192]{4,3,2,1,0:T(8,128)(2,1)S(1)}, bf16[1,1,3,32,192]{4,3,2,1,0:T(8,128)(2,1)S(1)}, u32[]{:S(2)}, u32[]{:S(2)}) collective-permute-start(bf16[1,1,3,32,192]{4,3,2,1,0:T(8,128)(2,1)S(1)} %convert_element_type.82), channel_id=1, source_target_pairs={{0,8},{8,16},{16,24},{24,0},{1,9},{9,17},{17,25},{25,1},{2,10},{10... | collective-permute-start | bytes 110600 | tf_op jit(solution)/shard_map/ppermute | solution.py:24
  9.8 5.4 %collective-permute-start.3 = (bf16[3,1,3,32,192]{4,3,2,1,0:T(8,128)(2,1)S(1)}, bf16[3,1,3,32,192]{4,3,2,1,0:T(8,128)(2,1)S(1)}, u32[]{:S(2)}, u32[]{:S(2)}) collective-permute-start(bf16[3,1,3,32,192]{4,3,2,1,0:T(8,128)(2,1)S(1)} %pad_maximum_fusion.23), channel_id=1, source_target_pairs={{1,0},{2,1},{3,2},{4,3},{5,4},{6,5},{7,6},{0,7},{9,8},{10,9},{11,1... | collective-permute-start | bytes 331784 | tf_op jit(solution)/shard_map/ppermute | solution.py:26
  11.5 6.7 %collective-permute-start.2 = (bf16[3,1,3,32,192]{4,3,2,1,0:T(8,128)(2,1)S(1)}, bf16[3,1,3,32,192]{4,3,2,1,0:T(8,128)(2,1)S(1)}, u32[]{:S(2)}, u32[]{:S(2)}) collective-permute-start(bf16[3,1,3,32,192]{4,3,2,1,0:T(8,128)(2,1)S(1)} %pad_maximum_fusion.23), channel_id=1, source_target_pairs={{0,1},{1,2},{2,3},{3,4},{4,5},{5,6},{6,7},{7,0},{8,9},{9,10},{10,1... | collective-permute-start | bytes 331784 | tf_op jit(solution)/shard_map/ppermute | solution.py:24
  27.4 4.3 collective-permute-start.5
  27.5 5.2 %collective-permute-start.4 = (bf16[1,1,3,32,192]{4,2,3,1,0:T(4,128)(2,1)S(1)}, bf16[1,1,3,32,192]{4,2,3,1,0:T(4,128)(2,1)S(1)}, u32[]{:S(2)}, u32[]{:S(2)}) collective-permute-start(bf16[1,1,3,32,192]{4,2,3,1,0:T(4,128)(2,1)S(1)} %get-tuple-element.18), channel_id=1, source_target_pairs={{0,8},{8,16},{16,24},{24,0},{1,9},{9,17},{17,25},{25,1},{2,10},{10... | collective-permute-start | bytes 110600 | tf_op jit(solution)/shard_map/ppermute | solution.py:24
  32.9 5.2 %collective-permute-start.7 = (bf16[3,1,3,32,192]{4,2,3,1,0:T(4,128)(2,1)S(1)}, bf16[3,1,3,32,192]{4,2,3,1,0:T(4,128)(2,1)S(1)}, u32[]{:S(2)}, u32[]{:S(2)}) collective-permute-start(bf16[3,1,3,32,192]{4,2,3,1,0:T(4,128)(2,1)S(1)} %pad_maximum_fusion.16), channel_id=1, source_target_pairs={{1,0},{2,1},{3,2},{4,3},{5,4},{6,5},{7,6},{0,7},{9,8},{10,9},{11,1... | collective-permute-start | bytes 331784 | tf_op jit(solution)/shard_map/ppermute | solution.py:26
  32.9 7.3 %collective-permute-start.6 = (bf16[3,1,3,32,192]{4,2,3,1,0:T(4,128)(2,1)S(1)}, bf16[3,1,3,32,192]{4,2,3,1,0:T(4,128)(2,1)S(1)}, u32[]{:S(2)}, u32[]{:S(2)}) collective-permute-start(bf16[3,1,3,32,192]{4,2,3,1,0:T(4,128)(2,1)S(1)} %pad_maximum_fusion.16), channel_id=1, source_target_pairs={{0,1},{1,2},{2,3},{3,4},{4,5},{5,6},{6,7},{7,0},{8,9},{9,10},{10,1... | collective-permute-start | bytes 331784 | tf_op jit(solution)/shard_map/ppermute | solution.py:24
  50.0 4.3 collective-permute-start.9
  50.9 5.2 %collective-permute-start.8 = (bf16[1,1,3,32,192]{4,2,3,1,0:T(4,128)(2,1)S(1)}, bf16[1,1,3,32,192]{4,2,3,1,0:T(4,128)(2,1)S(1)}, u32[]{:S(2)}, u32[]{:S(2)}) collective-permute-start(bf16[1,1,3,32,192]{4,2,3,1,0:T(4,128)(2,1)S(1)} %get-tuple-element.20), channel_id=1, source_target_pairs={{0,8},{8,16},{16,24},{24,0},{1,9},{9,17},{17,25},{25,1},{2,10},{10... | collective-permute-start | bytes 110600 | tf_op jit(solution)/shard_map/ppermute | solution.py:24
  56.3 5.6 %collective-permute-start.11 = (bf16[3,1,3,32,192]{4,2,3,1,0:T(4,128)(2,1)S(1)}, bf16[3,1,3,32,192]{4,2,3,1,0:T(4,128)(2,1)S(1)}, u32[]{:S(2)}, u32[]{:S(2)}) collective-permute-start(bf16[3,1,3,32,192]{4,2,3,1,0:T(4,128)(2,1)S(1)} %pad_maximum_fusion.17), channel_id=1, source_target_pairs={{1,0},{2,1},{3,2},{4,3},{5,4},{6,5},{7,6},{0,7},{9,8},{10,9},{11,1... | collective-permute-start | bytes 331784 | tf_op jit(solution)/shard_map/ppermute | solution.py:26
  57.7 7.3 %collective-permute-start.10 = (bf16[3,1,3,32,192]{4,2,3,1,0:T(4,128)(2,1)S(1)}, bf16[3,1,3,32,192]{4,2,3,1,0:T(4,128)(2,1)S(1)}, u32[]{:S(2)}, u32[]{:S(2)}) collective-permute-start(bf16[3,1,3,32,192]{4,2,3,1,0:T(4,128)(2,1)S(1)} %pad_maximum_fusion.17), channel_id=1, source_target_pairs={{0,1},{1,2},{2,3},{3,4},{4,5},{5,6},{6,7},{7,0},{8,9},{9,10},{10,1... | collective-permute-start | bytes 331784 | tf_op jit(solution)/shard_map/ppermute | solution.py:24
  74.7 4.3 collective-permute-start.13
  75.7 5.2 %collective-permute-start.12 = (bf16[1,1,3,32,192]{4,2,3,1,0:T(4,128)(2,1)S(1)}, bf16[1,1,3,32,192]{4,2,3,1,0:T(4,128)(2,1)S(1)}, u32[]{:S(2)}, u32[]{:S(2)}) collective-permute-start(bf16[1,1,3,32,192]{4,2,3,1,0:T(4,128)(2,1)S(1)} %get-tuple-element.22), channel_id=1, source_target_pairs={{0,8},{8,16},{16,24},{24,0},{1,9},{9,17},{17,25},{25,1},{2,10},{10... | collective-permute-start | bytes 110600 | tf_op jit(solution)/shard_map/ppermute | solution.py:24
  81.1 5.2 %collective-permute-start.15 = (bf16[3,1,3,32,192]{4,2,3,1,0:T(4,128)(2,1)S(1)}, bf16[3,1,3,32,192]{4,2,3,1,0:T(4,128)(2,1)S(1)}, u32[]{:S(2)}, u32[]{:S(2)}) collective-permute-start(bf16[3,1,3,32,192]{4,2,3,1,0:T(4,128)(2,1)S(1)} %pad_maximum_fusion.18), channel_id=1, source_target_pairs={{1,0},{2,1},{3,2},{4,3},{5,4},{6,5},{7,6},{0,7},{9,8},{10,9},{11,1... | collective-permute-start | bytes 331784 | tf_op jit(solution)/shard_map/ppermute | solution.py:26
  81.1 6.9 %collective-permute-start.14 = (bf16[3,1,3,32,192]{4,2,3,1,0:T(4,128)(2,1)S(1)}, bf16[3,1,3,32,192]{4,2,3,1,0:T(4,128)(2,1)S(1)}, u32[]{:S(2)}, u32[]{:S(2)}) collective-permute-start(bf16[3,1,3,32,192]{4,2,3,1,0:T(4,128)(2,1)S(1)} %pad_maximum_fusion.18), channel_id=1, source_target_pairs={{0,1},{1,2},{2,3},{3,4},{4,5},{5,6},{6,7},{7,0},{8,9},{9,10},{10,1... | collective-permute-start | bytes 331784 | tf_op jit(solution)/shard_map/ppermute | solution.py:24
  97.8 4.3 collective-permute-start.17
  98.7 5.2 %collective-permute-start.16 = (bf16[1,1,3,32,192]{4,2,3,1,0:T(4,128)(2,1)S(1)}, bf16[1,1,3,32,192]{4,2,3,1,0:T(4,128)(2,1)S(1)}, u32[]{:S(2)}, u32[]{:S(2)}) collective-permute-start(bf16[1,1,3,32,192]{4,2,3,1,0:T(4,128)(2,1)S(1)} %get-tuple-element.24), channel_id=1, source_target_pairs={{0,8},{8,16},{16,24},{24,0},{1,9},{9,17},{17,25},{25,1},{2,10},{10... | collective-permute-start | bytes 110600 | tf_op jit(solution)/shard_map/ppermute | solution.py:24
  104.0 5.5 %collective-permute-start.19 = (bf16[3,1,3,32,192]{4,2,3,1,0:T(4,128)(2,1)S(1)}, bf16[3,1,3,32,192]{4,2,3,1,0:T(4,128)(2,1)S(1)}, u32[]{:S(2)}, u32[]{:S(2)}) collective-permute-start(bf16[3,1,3,32,192]{4,2,3,1,0:T(4,128)(2,1)S(1)} %pad_maximum_fusion.19), channel_id=1, source_target_pairs={{1,0},{2,1},{3,2},{4,3},{5,4},{6,5},{7,6},{0,7},{9,8},{10,9},{11,1... | collective-permute-start | bytes 331784 | tf_op jit(solution)/shard_map/ppermute | solution.py:26
  104.5 7.0 %collective-permute-start.18 = (bf16[3,1,3,32,192]{4,2,3,1,0:T(4,128)(2,1)S(1)}, bf16[3,1,3,32,192]{4,2,3,1,0:T(4,128)(2,1)S(1)}, u32[]{:S(2)}, u32[]{:S(2)}) collective-permute-start(bf16[3,1,3,32,192]{4,2,3,1,0:T(4,128)(2,1)S(1)} %pad_maximum_fusion.19), channel_id=1, source_target_pairs={{0,1},{1,2},{2,3},{3,4},{4,5},{5,6},{6,7},{7,0},{8,9},{9,10},{10,1... | collective-permute-start | bytes 331784 | tf_op jit(solution)/shard_map/ppermute | solution.py:24
  121.3 4.3 collective-permute-start.21
  121.6 5.2 %collective-permute-start.20 = (bf16[1,1,3,32,192]{4,2,3,1,0:T(4,128)(2,1)S(1)}, bf16[1,1,3,32,192]{4,2,3,1,0:T(4,128)(2,1)S(1)}, u32[]{:S(2)}, u32[]{:S(2)}) collective-permute-start(bf16[1,1,3,32,192]{4,2,3,1,0:T(4,128)(2,1)S(1)} %get-tuple-element.26), channel_id=1, source_target_pairs={{0,8},{8,16},{16,24},{24,0},{1,9},{9,17},{17,25},{25,1},{2,10},{10... | collective-permute-start | bytes 110600 | tf_op jit(solution)/shard_map/ppermute | solution.py:24
  127.0 5.2 %collective-permute-start.23 = (bf16[3,1,3,32,192]{4,2,3,1,0:T(4,128)(2,1)S(1)}, bf16[3,1,3,32,192]{4,2,3,1,0:T(4,128)(2,1)S(1)}, u32[]{:S(2)}, u32[]{:S(2)}) collective-permute-start(bf16[3,1,3,32,192]{4,2,3,1,0:T(4,128)(2,1)S(1)} %pad_maximum_fusion.20), channel_id=1, source_target_pairs={{1,0},{2,1},{3,2},{4,3},{5,4},{6,5},{7,6},{0,7},{9,8},{10,9},{11,1... | collective-permute-start | bytes 331784 | tf_op jit(solution)/shard_map/ppermute | solution.py:26
  127.3 6.9 %collective-permute-start.22 = (bf16[3,1,3,32,192]{4,2,3,1,0:T(4,128)(2,1)S(1)}, bf16[3,1,3,32,192]{4,2,3,1,0:T(4,128)(2,1)S(1)}, u32[]{:S(2)}, u32[]{:S(2)}) collective-permute-start(bf16[3,1,3,32,192]{4,2,3,1,0:T(4,128)(2,1)S(1)} %pad_maximum_fusion.20), channel_id=1, source_target_pairs={{0,1},{1,2},{2,3},{3,4},{4,5},{5,6},{6,7},{7,0},{8,9},{9,10},{10,1... | collective-permute-start | bytes 331784 | tf_op jit(solution)/shard_map/ppermute | solution.py:24
  143.9 4.3 collective-permute-start.25
  144.9 5.2 %collective-permute-start.24 = (bf16[1,1,3,32,192]{4,2,3,1,0:T(4,128)(2,1)S(1)}, bf16[1,1,3,32,192]{4,2,3,1,0:T(4,128)(2,1)S(1)}, u32[]{:S(2)}, u32[]{:S(2)}) collective-permute-start(bf16[1,1,3,32,192]{4,2,3,1,0:T(4,128)(2,1)S(1)} %get-tuple-element.28), channel_id=1, source_target_pairs={{0,8},{8,16},{16,24},{24,0},{1,9},{9,17},{17,25},{25,1},{2,10},{10... | collective-permute-start | bytes 110600 | tf_op jit(solution)/shard_map/ppermute | solution.py:24
  150.2 5.4 %collective-permute-start.27 = (bf16[3,1,3,32,192]{4,2,3,1,0:T(4,128)(2,1)S(1)}, bf16[3,1,3,32,192]{4,2,3,1,0:T(4,128)(2,1)S(1)}, u32[]{:S(2)}, u32[]{:S(2)}) collective-permute-start(bf16[3,1,3,32,192]{4,2,3,1,0:T(4,128)(2,1)S(1)} %pad_maximum_fusion.21), channel_id=1, source_target_pairs={{1,0},{2,1},{3,2},{4,3},{5,4},{6,5},{7,6},{0,7},{9,8},{10,9},{11,1... | collective-permute-start | bytes 331784 | tf_op jit(solution)/shard_map/ppermute | solution.py:26
  150.6 7.1 %collective-permute-start.26 = (bf16[3,1,3,32,192]{4,2,3,1,0:T(4,128)(2,1)S(1)}, bf16[3,1,3,32,192]{4,2,3,1,0:T(4,128)(2,1)S(1)}, u32[]{:S(2)}, u32[]{:S(2)}) collective-permute-start(bf16[3,1,3,32,192]{4,2,3,1,0:T(4,128)(2,1)S(1)} %pad_maximum_fusion.21), channel_id=1, source_target_pairs={{0,1},{1,2},{2,3},{3,4},{4,5},{5,6},{6,7},{7,0},{8,9},{9,10},{10,1... | collective-permute-start | bytes 331784 | tf_op jit(solution)/shard_map/ppermute | solution.py:24
  167.3 4.3 collective-permute-start.29
  168.3 5.2 %collective-permute-start.28 = (bf16[1,1,3,32,192]{4,2,3,1,0:T(4,128)(2,1)S(1)}, bf16[1,1,3,32,192]{4,2,3,1,0:T(4,128)(2,1)S(1)}, u32[]{:S(2)}, u32[]{:S(2)}) collective-permute-start(bf16[1,1,3,32,192]{4,2,3,1,0:T(4,128)(2,1)S(1)} %get-tuple-element.30), channel_id=1, source_target_pairs={{0,8},{8,16},{16,24},{24,0},{1,9},{9,17},{17,25},{25,1},{2,10},{10... | collective-permute-start | bytes 110600 | tf_op jit(solution)/shard_map/ppermute | solution.py:24
  173.7 5.2 %collective-permute-start.31 = (bf16[3,1,3,32,192]{4,2,3,1,0:T(4,128)(2,1)S(1)}, bf16[3,1,3,32,192]{4,2,3,1,0:T(4,128)(2,1)S(1)}, u32[]{:S(2)}, u32[]{:S(2)}) collective-permute-start(bf16[3,1,3,32,192]{4,2,3,1,0:T(4,128)(2,1)S(1)} %pad_maximum_fusion.22), channel_id=1, source_target_pairs={{1,0},{2,1},{3,2},{4,3},{5,4},{6,5},{7,6},{0,7},{9,8},{10,9},{11,1... | collective-permute-start | bytes 331784 | tf_op jit(solution)/shard_map/ppermute | solution.py:26
  173.9 6.9 %collective-permute-start.30 = (bf16[3,1,3,32,192]{4,2,3,1,0:T(4,128)(2,1)S(1)}, bf16[3,1,3,32,192]{4,2,3,1,0:T(4,128)(2,1)S(1)}, u32[]{:S(2)}, u32[]{:S(2)}) collective-permute-start(bf16[3,1,3,32,192]{4,2,3,1,0:T(4,128)(2,1)S(1)} %pad_maximum_fusion.22), channel_id=1, source_target_pairs={{0,1},{1,2},{2,3},{3,4},{4,5},{5,6},{6,7},{7,0},{8,9},{9,10},{10,1... | collective-permute-start | bytes 331784 | tf_op jit(solution)/shard_map/ppermute | solution.py:24
  236.4 4.7 %collective-permute-start.33 = (bf16[1,1,3,32,192]{4,3,2,1,0:T(8,128)(2,1)S(1)}, bf16[1,1,3,32,192]{4,3,2,1,0:T(8,128)(2,1)S(1)}, u32[]{:S(2)}, u32[]{:S(2)}) collective-permute-start(bf16[1,1,3,32,192]{4,3,2,1,0:T(8,128)(2,1)S(1)} %fusion.222), channel_id=1, source_target_pairs={{8,0},{16,8},{24,16},{0,24},{9,1},{17,9},{25,17},{1,25},{10,2},{18... | collective-permute-start | bytes 110600 | tf_op jit(solution)/shard_map/ppermute | solution.py:26
  238.8 5.0 %collective-permute-start.32 = (bf16[1,1,3,32,192]{4,3,2,1,0:T(8,128)(2,1)S(1)}, bf16[1,1,3,32,192]{4,3,2,1,0:T(8,128)(2,1)S(1)}, u32[]{:S(2)}, u32[]{:S(2)}) collective-permute-start(bf16[1,1,3,32,192]{4,3,2,1,0:T(8,128)(2,1)S(1)} %fusion.222), channel_id=1, source_target_pairs={{0,8},{8,16},{16,24},{24,0},{1,9},{9,17},{17,25},{25,1},{2,10},{10... | collective-permute-start | bytes 110600 | tf_op jit(solution)/shard_map/ppermute | solution.py:24
  243.8 2.7 collective-permute-start.35
  243.9 6.6 %collective-permute-start.34 = (bf16[3,1,3,32,192]{4,3,2,1,0:T(8,128)(2,1)S(1)}, bf16[3,1,3,32,192]{4,3,2,1,0:T(8,128)(2,1)S(1)}, u32[]{:S(2)}, u32[]{:S(2)}) collective-permute-start(bf16[3,1,3,32,192]{4,3,2,1,0:T(8,128)(2,1)S(1)} %pad_maximum_fusion.24), channel_id=1, source_target_pairs={{0,1},{1,2},{2,3},{3,4},{4,5},{5,6},{6,7},{7,0},{8,9},{9,10},{10,1... | collective-permute-start | bytes 331784 | tf_op jit(solution)/shard_map/ppermute | solution.py:24
  259.6 4.2 collective-permute-start.37
  260.2 5.0 %collective-permute-start.36 = (bf16[1,1,3,32,192]{4,3,2,1,0:T(8,128)(2,1)S(1)}, bf16[1,1,3,32,192]{4,3,2,1,0:T(8,128)(2,1)S(1)}, u32[]{:S(2)}, u32[]{:S(2)}) collective-permute-start(bf16[1,1,3,32,192]{4,3,2,1,0:T(8,128)(2,1)S(1)} %fusion.223), channel_id=1, source_target_pairs={{0,8},{8,16},{16,24},{24,0},{1,9},{9,17},{17,25},{25,1},{2,10},{10... | collective-permute-start | bytes 110600 | tf_op jit(solution)/shard_map/ppermute | solution.py:24
  265.2 4.3 collective-permute-start.39
  265.3 6.4 %collective-permute-start.38 = (bf16[3,1,3,32,192]{4,3,2,1,0:T(8,128)(2,1)S(1)}, bf16[3,1,3,32,192]{4,3,2,1,0:T(8,128)(2,1)S(1)}, u32[]{:S(2)}, u32[]{:S(2)}) collective-permute-start(bf16[3,1,3,32,192]{4,3,2,1,0:T(8,128)(2,1)S(1)} %pad_maximum_fusion.25), channel_id=1, source_target_pairs={{0,1},{1,2},{2,3},{3,4},{4,5},{5,6},{6,7},{7,0},{8,9},{9,10},{10,1... | collective-permute-start | bytes 331784 | tf_op jit(solution)/shard_map/ppermute | solution.py:24
  280.9 4.1 collective-permute-start.41
  282.4 5.0 %collective-permute-start.40 = (bf16[1,1,3,32,192]{4,3,2,1,0:T(8,128)(2,1)S(1)}, bf16[1,1,3,32,192]{4,3,2,1,0:T(8,128)(2,1)S(1)}, u32[]{:S(2)}, u32[]{:S(2)}) collective-permute-start(bf16[1,1,3,32,192]{4,3,2,1,0:T(8,128)(2,1)S(1)} %get-tuple-element.16), channel_id=1, source_target_pairs={{0,8},{8,16},{16,24},{24,0},{1,9},{9,17},{17,25},{25,1},{2,10},{10... | collective-permute-start | bytes 110600 | tf_op jit(solution)/shard_map/ppermute | solution.py:24
  287.4 4.3 collective-permute-start.43
  287.6 6.5 %collective-permute-start.42 = (bf16[3,1,3,32,192]{4,3,2,1,0:T(8,128)(2,1)S(1)}, bf16[3,1,3,32,192]{4,3,2,1,0:T(8,128)(2,1)S(1)}, u32[]{:S(2)}, u32[]{:S(2)}) collective-permute-start(bf16[3,1,3,32,192]{4,3,2,1,0:T(8,128)(2,1)S(1)} %pad_maximum_fusion.26), channel_id=1, source_target_pairs={{0,1},{1,2},{2,3},{3,4},{4,5},{5,6},{6,7},{7,0},{8,9},{9,10},{10,1... | collective-permute-start | bytes 331784 | tf_op jit(solution)/shard_map/ppermute | solution.py:24
  303.3 4.1 collective-permute-start.45
  303.9 5.0 %collective-permute-start.44 = (bf16[1,1,3,32,192]{4,3,2,1,0:T(8,128)(2,1)S(1)}, bf16[1,1,3,32,192]{4,3,2,1,0:T(8,128)(2,1)S(1)}, u32[]{:S(2)}, u32[]{:S(2)}) collective-permute-start(bf16[1,1,3,32,192]{4,3,2,1,0:T(8,128)(2,1)S(1)} %get-tuple-element.14), channel_id=1, source_target_pairs={{0,8},{8,16},{16,24},{24,0},{1,9},{9,17},{17,25},{25,1},{2,10},{10... | collective-permute-start | bytes 110600 | tf_op jit(solution)/shard_map/ppermute | solution.py:24
  309.0 4.1 collective-permute-start.47
  309.0 6.4 %collective-permute-start.46 = (bf16[3,1,3,32,192]{4,3,2,1,0:T(8,128)(2,1)S(1)}, bf16[3,1,3,32,192]{4,3,2,1,0:T(8,128)(2,1)S(1)}, u32[]{:S(2)}, u32[]{:S(2)}) collective-permute-start(bf16[3,1,3,32,192]{4,3,2,1,0:T(8,128)(2,1)S(1)} %pad_maximum_fusion.27), channel_id=1, source_target_pairs={{0,1},{1,2},{2,3},{3,4},{4,5},{5,6},{6,7},{7,0},{8,9},{9,10},{10,1... | collective-permute-start | bytes 331784 | tf_op jit(solution)/shard_map/ppermute | solution.py:24
  324.6 4.1 collective-permute-start.49
  325.5 5.0 %collective-permute-start.48 = (bf16[1,1,3,32,192]{4,3,2,1,0:T(8,128)(2,1)S(1)}, bf16[1,1,3,32,192]{4,3,2,1,0:T(8,128)(2,1)S(1)}, u32[]{:S(2)}, u32[]{:S(2)}) collective-permute-start(bf16[1,1,3,32,192]{4,3,2,1,0:T(8,128)(2,1)S(1)} %get-tuple-element.12), channel_id=1, source_target_pairs={{0,8},{8,16},{16,24},{24,0},{1,9},{9,17},{17,25},{25,1},{2,10},{10... | collective-permute-start | bytes 110600 | tf_op jit(solution)/shard_map/ppermute | solution.py:24
  330.5 4.3 collective-permute-start.51
  330.6 6.6 %collective-permute-start.50 = (bf16[3,1,3,32,192]{4,3,2,1,0:T(8,128)(2,1)S(1)}, bf16[3,1,3,32,192]{4,3,2,1,0:T(8,128)(2,1)S(1)}, u32[]{:S(2)}, u32[]{:S(2)}) collective-permute-start(bf16[3,1,3,32,192]{4,3,2,1,0:T(8,128)(2,1)S(1)} %pad_maximum_fusion.28), channel_id=1, source_target_pairs={{0,1},{1,2},{2,3},{3,4},{4,5},{5,6},{6,7},{7,0},{8,9},{9,10},{10,1... | collective-permute-start | bytes 331784 | tf_op jit(solution)/shard_map/ppermute | solution.py:24
  346.4 4.1 collective-permute-start.53
  347.4 5.0 %collective-permute-start.52 = (bf16[1,1,3,32,192]{4,3,2,1,0:T(8,128)(2,1)S(1)}, bf16[1,1,3,32,192]{4,3,2,1,0:T(8,128)(2,1)S(1)}, u32[]{:S(2)}, u32[]{:S(2)}) collective-permute-start(bf16[1,1,3,32,192]{4,3,2,1,0:T(8,128)(2,1)S(1)} %get-tuple-element.10), channel_id=1, source_target_pairs={{0,8},{8,16},{16,24},{24,0},{1,9},{9,17},{17,25},{25,1},{2,10},{10... | collective-permute-start | bytes 110600 | tf_op jit(solution)/shard_map/ppermute | solution.py:24
  352.4 4.1 collective-permute-start.55
  352.5 6.4 %collective-permute-start.54 = (bf16[3,1,3,32,192]{4,3,2,1,0:T(8,128)(2,1)S(1)}, bf16[3,1,3,32,192]{4,3,2,1,0:T(8,128)(2,1)S(1)}, u32[]{:S(2)}, u32[]{:S(2)}) collective-permute-start(bf16[3,1,3,32,192]{4,3,2,1,0:T(8,128)(2,1)S(1)} %pad_maximum_fusion.29), channel_id=1, source_target_pairs={{0,1},{1,2},{2,3},{3,4},{4,5},{5,6},{6,7},{7,0},{8,9},{9,10},{10,1... | collective-permute-start | bytes 331784 | tf_op jit(solution)/shard_map/ppermute | solution.py:24
  368.1 4.1 collective-permute-start.57
  369.0 5.0 %collective-permute-start.56 = (bf16[1,1,3,32,192]{4,3,2,1,0:T(8,128)(2,1)S(1)}, bf16[1,1,3,32,192]{4,3,2,1,0:T(8,128)(2,1)S(1)}, u32[]{:S(2)}, u32[]{:S(2)}) collective-permute-start(bf16[1,1,3,32,192]{4,3,2,1,0:T(8,128)(2,1)S(1)} %get-tuple-element.6), channel_id=1, source_target_pairs={{0,8},{8,16},{16,24},{24,0},{1,9},{9,17},{17,25},{25,1},{2,10},{10... | collective-permute-start | bytes 110600 | tf_op jit(solution)/shard_map/ppermute | solution.py:24
  374.0 4.2 collective-permute-start.59
  374.0 6.7 %collective-permute-start.58 = (bf16[3,1,3,32,192]{4,3,2,1,0:T(8,128)(2,1)S(1)}, bf16[3,1,3,32,192]{4,3,2,1,0:T(8,128)(2,1)S(1)}, u32[]{:S(2)}, u32[]{:S(2)}) collective-permute-start(bf16[3,1,3,32,192]{4,3,2,1,0:T(8,128)(2,1)S(1)} %pad_maximum_fusion.30), channel_id=1, source_target_pairs={{0,1},{1,2},{2,3},{3,4},{4,5},{5,6},{6,7},{7,0},{8,9},{9,10},{10,1... | collective-permute-start | bytes 331784 | tf_op jit(solution)/shard_map/ppermute | solution.py:24
  389.9 4.1 collective-permute-start.61
  390.6 5.0 %collective-permute-start.60 = (bf16[1,1,3,32,192]{4,3,2,1,0:T(8,128)(2,1)S(1)}, bf16[1,1,3,32,192]{4,3,2,1,0:T(8,128)(2,1)S(1)}, u32[]{:S(2)}, u32[]{:S(2)}) collective-permute-start(bf16[1,1,3,32,192]{4,3,2,1,0:T(8,128)(2,1)S(1)} %convert_bitcast_fusion), channel_id=1, source_target_pairs={{0,8},{8,16},{16,24},{24,0},{1,9},{9,17},{17,25},{25,1},{2,10},{10... | collective-permute-start | bytes 110600 | tf_op jit(solution)/shard_map/ppermute | solution.py:24
  395.6 4.1 collective-permute-start.63
  395.7 6.4 %collective-permute-start.62 = (bf16[3,1,3,32,192]{4,3,2,1,0:T(8,128)(2,1)S(1)}, bf16[3,1,3,32,192]{4,3,2,1,0:T(8,128)(2,1)S(1)}, u32[]{:S(2)}, u32[]{:S(2)}) collective-permute-start(bf16[3,1,3,32,192]{4,3,2,1,0:T(8,128)(2,1)S(1)} %pad_maximum_fusion.31), channel_id=1, source_target_pairs={{0,1},{1,2},{2,3},{3,4},{4,5},{5,6},{6,7},{7,0},{8,9},{9,10},{10,1... | collective-permute-start | bytes 331784 | tf_op jit(solution)/shard_map/ppermute | solution.py:24
  (2 other events, 11.7 us)
where the time goes:
time: 466 us; the launch traced here: 458 us
  waiting for transfers between devices  163 us (35%)
  matrix products  136 us (29%)
  blocking collectives  76.1 us (16%)
  starting transfers between devices  47.6 us (10%)
  other arithmetic  22.3 us (5%)
  local copies, waits for them, and re-layouts  11.6 us (2%)
    ppermute x32, waiting for transfers between devices, with_halo(): lax.ppermute(head, axis, [((i + 1) % count, i) for i in range(count)])  95.3 us
    dot_general x16, matrix products, apply_operator(): jnp.einsum('kvj,kij->kvi', picked, matrices, preferred_element_type=jnp.f...  92.9 us
    psum x2, blocking collectives, orthonormal(): gram_matrix = lax.psum(partial_gram, ('gx', 'gy'))  76.1 us
    ppermute x32, waiting for transfers between devices, with_halo(): lax.ppermute(tail, axis, [(i, (i + 1) % count) for i in range(count)])  68 us
    dot_general x16, matrix products, apply_operator(): jnp.einsum('zk,kvi->zvi', select, products, precision=lax.Precision.HIGHEST)  40.6 us
    ppermute x32, starting transfers between devices, with_halo(): lax.ppermute(tail, axis, [(i, (i + 1) % count) for i in range(count)])  24.7 us
    ppermute x32, starting transfers between devices, with_halo(): lax.ppermute(head, axis, [((i + 1) % count, i) for i in range(count)])  22.9 us
    gather x16, local copies, waits for them, and re-layouts, apply_operator(): picked = jnp.take(window_cells, sources, axis=0)  10.9 us
  transfers between devices with their start and end apart: 64, of which 64 were waited for; matrix products, arithmetic and copies ran while one was open for 0% of the time, Pallas kernels for 0%

commit v1 on v0

v1 whole, which is shorter than its diff:
```python
import math

import jax
import jax.numpy as jnp
from jax import lax
from jax.experimental import pallas as pl
from jax.experimental.pallas import tpu as pltpu
from jax.sharding import PartitionSpec as P

DEGREE = 8
STEPS = 2


CENTER = 5.0
HALF = 3.0
LOWEST = 0.5

CHUNK = 9


def gather_window(rounded):
    nx = lax.axis_size("gx")
    ny = lax.axis_size("gy")
    cells = []
    for dx in range(3):
        for dy in range(3):
            if dx == 1 and dy == 1:
                cells.append(rounded)
                continue
            pairs = []
            for a in range(nx):
                for b in range(ny):
                    src = a * ny + b
                    dst = ((a - dx + 1) % nx) * ny + (b - dy + 1) % ny
                    pairs.append((src, dst))
            cells.append(lax.ppermute(rounded, ("gx", "gy"), pairs))
    return cells


def apply_kernel(src_ref, dst_ref, coef_ref, *refs):
    cells = refs[:9]
    cur_ref, prev_ref, cpl_hbm = refs[9:12]
    out_ref, out_bf_ref = refs[12:14]
    win, cpl, acc, sems = refs[14:]
    slots = cpl.shape[0]
    chunks = slots // CHUNK
    depth = cur_ref.shape[0]

    copies = []
    for c in range(chunks):
        cp = pltpu.make_async_copy(
            cpl_hbm.at[pl.ds(c * CHUNK, CHUNK)], cpl.at[pl.ds(c * CHUNK, CHUNK)], sems.at[c]
        )
        cp.start()
        copies.append(cp)

    for c in range(9):
        win[pl.ds(c * depth, depth)] = cells[c][...]
    acc[...] = jnp.zeros_like(acc)

    for c in range(chunks):
        copies[c].wait()

        def body(i, carry, c=c):
            s = c * CHUNK + i
            y = win[src_ref[s]]
            prod = lax.dot_general(
                y, cpl[s], (((1,), (1,)), ((), ())), preferred_element_type=jnp.float32
            )
            t = dst_ref[s]
            acc[t] = acc[t] + prod
            return carry

        lax.fori_loop(0, CHUNK, body, 0)

    alpha = coef_ref[0]
    beta = coef_ref[1]
    for z in range(depth):
        cur = cur_ref[z]
        nxt = alpha * (acc[z] - CENTER * cur) - beta * prev_ref[z]
        out_ref[z] = nxt
        out_bf_ref[z] = nxt.astype(jnp.bfloat16)


def apply_step(cells, cur, prev, matrices, sources, targets, coef):
    depth, vectors, dof = cur.shape
    slots = matrices.shape[0]
    vmem = pltpu.MemorySpace.VMEM
    smem = pltpu.MemorySpace.SMEM
    in_specs = (
        [pl.BlockSpec(memory_space=smem)] * 3
        + [pl.BlockSpec(memory_space=vmem)] * 11
        + [pl.BlockSpec(memory_space=pl.ANY)]
    )
    flops = 2 * slots * vectors * dof * dof
    bytes_accessed = slots * dof * dof * 2 + 9 * cur.size * 2 + 4 * cur.size * 4
    return pl.pallas_call(
        apply_kernel,
        out_shape=(
            jax.ShapeDtypeStruct(cur.shape, jnp.float32),
            jax.ShapeDtypeStruct(cur.shape, jnp.bfloat16),
        ),
        in_specs=in_specs,
        out_specs=(pl.BlockSpec(memory_space=vmem), pl.BlockSpec(memory_space=vmem)),
        scratch_shapes=[
            pltpu.VMEM((9 * depth, vectors, dof), jnp.bfloat16),
            pltpu.VMEM((slots, dof, dof), jnp.bfloat16),
            pltpu.VMEM((depth + 1, vectors, dof), jnp.float32),
            pltpu.SemaphoreType.DMA((slots // CHUNK,)),
        ],
        cost_estimate=pl.CostEstimate(flops=flops, bytes_accessed=bytes_accessed, transcendentals=0),
        compiler_params=pltpu.CompilerParams(vmem_limit_bytes=32 * 1024 * 1024),
    )(sources, targets, coef, *cells, cur, prev, matrices)


def orthonormal(filtered, rows_total):
    partial_gram = jnp.einsum(
        "zvd,zwd->vw", filtered, filtered, precision=lax.Precision.HIGHEST
    )
    gram_matrix = lax.psum(partial_gram, ("gx", "gy"))
    factor = jnp.linalg.cholesky(gram_matrix)
    identity = jnp.eye(filtered.shape[1], dtype=jnp.float32)
    inverse = jax.scipy.linalg.solve_triangular(factor, identity, lower=True)
    result = jnp.einsum("vw,zwd->zvd", inverse, filtered, precision=lax.Precision.HIGHEST)
    return result * math.sqrt(rows_total)


def local(basis, coupling, cpl_dst, cpl_src):
    column_depth = basis.shape[2]
    block_rows = basis.shape[4]
    matrices = coupling[0, 0]
    targets = cpl_dst[0, 0]
    sources = cpl_src[0, 0]
    rows_total = lax.axis_size("gx") * lax.axis_size("gy") * column_depth * block_rows

    def coefs(alpha, beta):
        return jnp.array([alpha, beta], dtype=jnp.float32)

    sigma_one = HALF / (LOWEST - CENTER)
    current = basis[0, 0]
    for outer in range(STEPS):
        previous = current
        rounded = current.astype(jnp.bfloat16)
        cells = gather_window(rounded)
        current, rounded = apply_step(
            cells, current, previous, matrices, sources, targets,
            coefs(sigma_one / HALF, 0.0),
        )
        sigma_now = sigma_one
        for inner in range(1, DEGREE):
            sigma_next = 1.0 / (2.0 / sigma_one - sigma_now)
            cells = gather_window(rounded)
            following, rounded = apply_step(
                cells, current, previous, matrices, sources, targets,
                coefs(2.0 * sigma_next / HALF, sigma_now * sigma_next),
            )
            previous, current, sigma_now = (current, following, sigma_next)
        current = orthonormal(current, rows_total)
    return current[None, None]


def solution(mesh):
    placed = (
        P("gx", "gy", None, None, None),
        P("gx", "gy", None, None, None),
        P("gx", "gy", None),
        P("gx", "gy", None),
    )
    return jax.shard_map(
        local,
        mesh=mesh,
        in_specs=placed,
        out_specs=P("gx", "gy", None, None, None),
        check_vma=False,
    )
```

time: 466 us -> 659 us (1.41); the launches traced: 458 us -> 658 us
  Pallas kernels: 0 us -> 255 us
  starting transfers between devices: 47.6 us -> 185 us
  matrix products: 136 us -> 2.03 us
  waiting for transfers between devices: 163 us -> 114 us
  other arithmetic: 22.3 us -> 14.3 us
    pallas_call x0 -> x16, Pallas kernels: none -> 255 us  [apply_step(): pl.pallas_call(apply_kernel, out_shape=(jax.ShapeDtypeStruct(cur.shape, j...]
    ppermute x64 -> x128, starting transfers between devices: 47.6 us -> 185 us  [gather_window(): cells.append(lax.ppermute(rounded, ('gx', 'gy'), pairs))]
    dot_general x36 -> x4, matrix products: 135 us -> 1.56 us  [the longest x2 1.11 us: orthonormal(): jnp.einsum('vw,zwd->zvd', inverse, filtered, precision=lax.Precision.HIGH...]
    ppermute x64 -> x128, waiting for transfers between devices: 163 us -> 114 us  [gather_window(): cells.append(lax.ppermute(rounded, ('gx', 'gy'), pairs))]
    unnamed x4 -> x36, local copies, waits for them, and re-layouts: 0.01 us -> 12.7 us
    gather x16 -> x0, local copies, waits for them, and re-layouts: 10.9 us -> none  [apply_operator(): picked = jnp.take(window_cells, sources, axis=0)]
  transfers between devices with their start and end apart: 64 -> 128, of which waited for: 64 -> 32; matrix products, arithmetic and copies ran while one was open for 0% -> 0% of each run, Pallas kernels for 0% -> 0%
where the time goes in v1:
time: 659 us; the launch traced here: 658 us
  Pallas kernels  255 us (39%)
  starting transfers between devices  185 us (28%)
  waiting for transfers between devices  114 us (17%)
  blocking collectives  74.1 us (11%)
  other arithmetic  14.3 us (2%)
  local copies, waits for them, and re-layouts  12.8 us (2%)
    pallas_call x16, Pallas kernels, apply_step(): pl.pallas_call(apply_kernel, out_shape=(jax.ShapeDtypeStruct(cur.shape, j...  255 us
    ppermute x128, starting transfers between devices, gather_window(): cells.append(lax.ppermute(rounded, ('gx', 'gy'), pairs))  185 us
    ppermute x128, waiting for transfers between devices, gather_window(): cells.append(lax.ppermute(rounded, ('gx', 'gy'), pairs))  114 us
    psum x2, blocking collectives, orthonormal(): gram_matrix = lax.psum(partial_gram, ('gx', 'gy'))  74.1 us
  transfers between devices with their start and end apart: 128, of which 32 were waited for; matrix products, arithmetic and copies ran while one was open for 0% of the time, Pallas kernels for 0%

profile of v1, /device:TPU:0, one launch (start us, length us, event | category | flops | bytes accessed | tf_op | source)
XLA Modules:
  0.0 658.2 jit_solution(8854734198639349047)
XLA Ops:
  0.9 6.4 collective-permute-start.7
  7.8 4.4 collective-permute-start.4
  12.2 3.6 collective-permute-start.2
  20.8 4.5 collective-permute-done.refs_0_
  25.3 3.3 copy-done
  31.4 15.9 %shard_map.190 = (f32[3,32,192]{2,1,0:T(8,128)S(1)}, bf16[3,32,192]{2,1,0:T(8,128)(2,1)S(1)}) custom-call(s32[81]{0:T(128)S(1)} %bitcast.64, s32[81]{0:T(128)S(1)} %bitcast.80, f32[2]{0:T(128)S(1)} %copy-done.16, bf16[3,32,192]{2,1,0:T(8,128)(2,1)S(1)} %collective-permute-done.refs_0_, bf16[3,32,192]{2,1,0:T(8,128)(2,1)S(1)} %collective-permute-done.1.refs_1_, ...), custom_call_target="tpu_custom_call" | custom-call | flops 191102976 | bytes 6598656 | tf_op jit(solution)/shard_map/pallas_call | solution.py:97
  49.1 3.3 collective-permute-start.12
  52.4 3.1 collective-permute-start.10
  60.5 5.0 collective-permute-done.8.refs_0_
  65.5 15.9 %shard_map.191 = (f32[3,32,192]{2,1,0:T(8,128)S(1)}, bf16[3,32,192]{2,1,0:T(8,128)(2,1)S(1)}) custom-call(s32[81]{0:T(128)S(1)} %bitcast.65, s32[81]{0:T(128)S(1)} %bitcast.81, f32[2]{0:T(128)S(1)} %copy-done.15, bf16[3,32,192]{2,1,0:T(8,128)(2,1)S(1)} %collective-permute-done.8.refs_0_, bf16[3,32,192]{2,1,0:T(8,128)(2,1)S(1)} %collective-permute-done.9.refs_1_, ...), custom_call_target="tpu_custom_call" | custom-call | flops 191102976 | bytes 6598656 | tf_op jit(solution)/shard_map/pallas_call | solution.py:97
  83.2 3.3 collective-permute-start.20
  86.5 3.1 collective-permute-start.18
  94.6 5.0 collective-permute-done.16.refs_0_
  99.5 15.9 %shard_map.192 = (f32[3,32,192]{2,1,0:T(8,128)S(1)}, bf16[3,32,192]{2,1,0:T(8,128)(2,1)S(1)}) custom-call(s32[81]{0:T(128)S(1)} %bitcast.66, s32[81]{0:T(128)S(1)} %bitcast.82, f32[2]{0:T(128)S(1)} %copy-done.14, bf16[3,32,192]{2,1,0:T(8,128)(2,1)S(1)} %collective-permute-done.16.refs_0_, bf16[3,32,192]{2,1,0:T(8,128)(2,1)S(1)} %collective-permute-done.17.refs_1_, ...), custom_call_target="tpu_custom_call" | custom-call | flops 191102976 | bytes 6598656 | tf_op jit(solution)/shard_map/pallas_call | solution.py:97
  117.2 3.3 collective-permute-start.28
  120.5 3.1 collective-permute-start.26
  128.6 5.0 collective-permute-done.24.refs_0_
  133.6 15.9 %shard_map.193 = (f32[3,32,192]{2,1,0:T(8,128)S(1)}, bf16[3,32,192]{2,1,0:T(8,128)(2,1)S(1)}) custom-call(s32[81]{0:T(128)S(1)} %bitcast.67, s32[81]{0:T(128)S(1)} %bitcast.83, f32[2]{0:T(128)S(1)} %copy-done.13, bf16[3,32,192]{2,1,0:T(8,128)(2,1)S(1)} %collective-permute-done.24.refs_0_, bf16[3,32,192]{2,1,0:T(8,128)(2,1)S(1)} %collective-permute-done.25.refs_1_, ...), custom_call_target="tpu_custom_call" | custom-call | flops 191102976 | bytes 6598656 | tf_op jit(solution)/shard_map/pallas_call | solution.py:97
  151.3 3.3 collective-permute-start.36
  154.6 3.1 collective-permute-start.34
  162.7 5.0 collective-permute-done.32.refs_0_
  167.6 15.9 %shard_map.194 = (f32[3,32,192]{2,1,0:T(8,128)S(1)}, bf16[3,32,192]{2,1,0:T(8,128)(2,1)S(1)}) custom-call(s32[81]{0:T(128)S(1)} %bitcast.68, s32[81]{0:T(128)S(1)} %bitcast.84, f32[2]{0:T(128)S(1)} %copy-done.12, bf16[3,32,192]{2,1,0:T(8,128)(2,1)S(1)} %collective-permute-done.32.refs_0_, bf16[3,32,192]{2,1,0:T(8,128)(2,1)S(1)} %collective-permute-done.33.refs_1_, ...), custom_call_target="tpu_custom_call" | custom-call | flops 191102976 | bytes 6598656 | tf_op jit(solution)/shard_map/pallas_call | solution.py:97
  185.3 3.3 collective-permute-start.44
  188.6 3.1 collective-permute-start.42
  196.7 5.0 collective-permute-done.40.refs_0_
  201.7 15.9 %shard_map.195 = (f32[3,32,192]{2,1,0:T(8,128)S(1)}, bf16[3,32,192]{2,1,0:T(8,128)(2,1)S(1)}) custom-call(s32[81]{0:T(128)S(1)} %bitcast.69, s32[81]{0:T(128)S(1)} %bitcast.85, f32[2]{0:T(128)S(1)} %copy-done.11, bf16[3,32,192]{2,1,0:T(8,128)(2,1)S(1)} %collective-permute-done.40.refs_0_, bf16[3,32,192]{2,1,0:T(8,128)(2,1)S(1)} %collective-permute-done.41.refs_1_, ...), custom_call_target="tpu_custom_call" | custom-call | flops 191102976 | bytes 6598656 | tf_op jit(solution)/shard_map/pallas_call | solution.py:97
  219.4 3.3 collective-permute-start.52
  222.7 3.1 collective-permute-start.50
  230.8 5.0 collective-permute-done.48.refs_0_
  235.8 15.9 %shard_map.196 = (f32[3,32,192]{2,1,0:T(8,128)S(1)}, bf16[3,32,192]{2,1,0:T(8,128)(2,1)S(1)}) custom-call(s32[81]{0:T(128)S(1)} %bitcast.70, s32[81]{0:T(128)S(1)} %bitcast.86, f32[2]{0:T(128)S(1)} %copy-done.10, bf16[3,32,192]{2,1,0:T(8,128)(2,1)S(1)} %collective-permute-done.48.refs_0_, bf16[3,32,192]{2,1,0:T(8,128)(2,1)S(1)} %collective-permute-done.49.refs_1_, ...), custom_call_target="tpu_custom_call" | custom-call | flops 191102976 | bytes 6598656 | tf_op jit(solution)/shard_map/pallas_call | solution.py:97
  253.4 3.3 collective-permute-start.60
  256.7 3.1 collective-permute-start.58
  264.8 5.0 collective-permute-done.56.refs_0_
  269.8 16.5 %shard_map.197 = (f32[3,32,192]{2,1,0:T(8,128)S(1)}, bf16[3,32,192]{2,1,0:T(8,128)(2,1)}) custom-call(s32[81]{0:T(128)S(1)} %bitcast.71, s32[81]{0:T(128)S(1)} %bitcast.87, f32[2]{0:T(128)S(1)} %copy-done.9, bf16[3,32,192]{2,1,0:T(8,128)(2,1)S(1)} %collective-permute-done.56.refs_0_, bf16[3,32,192]{2,1,0:T(8,128)(2,1)S(1)} %collective-permute-done.57.refs_1_, ...), custom_call_target="tpu_custom_call" | custom-call | flops 191102976 | bytes 6598656 | tf_op jit(solution)/shard_map/pallas_call | solution.py:97
  286.6 37.2 %psum.14 = f32[32,32]{0,1:T(8,128)S(1)} all-reduce(f32[32,32]{0,1:T(8,128)S(1)} %convolution_bitcast_fusion.3), channel_id=1, replica_groups=mesh['gx'=4,'gy'=8] {'gx','gy'}, use_global_device_ids=true, to_apply=%region_0.0 | all-reduce | flops 1024 | bytes 8192 | tf_op jit(solution)/shard_map/psum | solution.py:120
  338.6 3.5 collective-permute-start.66
  347.1 4.5 collective-permute-done.64.refs_0_
  351.7 3.3 copy-done.2
  355.0 15.9 %shard_map.198 = (f32[3,32,192]{2,1,0:T(8,128)S(1)}, bf16[3,32,192]{2,1,0:T(8,128)(2,1)S(1)}) custom-call(s32[81]{0:T(128)S(1)} %bitcast.72, s32[81]{0:T(128)S(1)} %bitcast.88, f32[2]{0:T(128)S(1)} %copy-done.17, bf16[3,32,192]{2,1,0:T(8,128)(2,1)S(1)} %collective-permute-done.64.refs_0_, bf16[3,32,192]{2,1,0:T(8,128)(2,1)S(1)} %collective-permute-done.65.refs_1_, ...), custom_call_target="tpu_custom_call" | custom-call | flops 191102976 | bytes 6598656 | tf_op jit(solution)/shard_map/pallas_call | solution.py:97
  372.6 3.3 collective-permute-start.76
  375.9 3.1 collective-permute-start.74
  384.0 5.0 collective-permute-done.72.refs_0_
  389.0 3.3 copy-done.3
  392.3 15.9 %shard_map.199 = (f32[3,32,192]{2,1,0:T(8,128)S(1)}, bf16[3,32,192]{2,1,0:T(8,128)(2,1)S(1)}) custom-call(s32[81]{0:T(128)S(1)} %bitcast.73, s32[81]{0:T(128)S(1)} %bitcast.89, f32[2]{0:T(128)S(1)} %copy-done.15, bf16[3,32,192]{2,1,0:T(8,128)(2,1)S(1)} %collective-permute-done.72.refs_0_, bf16[3,32,192]{2,1,0:T(8,128)(2,1)S(1)} %collective-permute-done.73.refs_1_, ...), custom_call_target="tpu_custom_call" | custom-call | flops 191102976 | bytes 6598656 | tf_op jit(solution)/shard_map/pallas_call | solution.py:97
  409.9 3.3 collective-permute-start.84
  421.3 5.0 collective-permute-done.80.refs_0_
  426.3 15.9 %shard_map.200 = (f32[3,32,192]{2,1,0:T(8,128)S(1)}, bf16[3,32,192]{2,1,0:T(8,128)(2,1)S(1)}) custom-call(s32[81]{0:T(128)S(1)} %bitcast.74, s32[81]{0:T(128)S(1)} %bitcast.90, f32[2]{0:T(128)S(1)} %copy-done.14, bf16[3,32,192]{2,1,0:T(8,128)(2,1)S(1)} %collective-permute-done.80.refs_0_, bf16[3,32,192]{2,1,0:T(8,128)(2,1)S(1)} %collective-permute-done.81.refs_1_, ...), custom_call_target="tpu_custom_call" | custom-call | flops 191102976 | bytes 6598656 | tf_op jit(solution)/shard_map/pallas_call | solution.py:97
  444.0 3.3 collective-permute-start.92
  447.3 3.1 collective-permute-start.90
  455.4 5.0 collective-permute-done.88.refs_0_
  460.4 15.9 %shard_map.201 = (f32[3,32,192]{2,1,0:T(8,128)S(1)}, bf16[3,32,192]{2,1,0:T(8,128)(2,1)S(1)}) custom-call(s32[81]{0:T(128)S(1)} %bitcast.75, s32[81]{0:T(128)S(1)} %bitcast.91, f32[2]{0:T(128)S(1)} %copy-done.13, bf16[3,32,192]{2,1,0:T(8,128)(2,1)S(1)} %collective-permute-done.88.refs_0_, bf16[3,32,192]{2,1,0:T(8,128)(2,1)S(1)} %collective-permute-done.89.refs_1_, ...), custom_call_target="tpu_custom_call" | custom-call | flops 191102976 | bytes 6598656 | tf_op jit(solution)/shard_map/pallas_call | solution.py:97
  478.0 3.3 collective-permute-start.100
  489.4 5.0 collective-permute-done.96.refs_0_
  494.4 15.9 %shard_map.202 = (f32[3,32,192]{2,1,0:T(8,128)S(1)}, bf16[3,32,192]{2,1,0:T(8,128)(2,1)S(1)}) custom-call(s32[81]{0:T(128)S(1)} %bitcast.76, s32[81]{0:T(128)S(1)} %bitcast.92, f32[2]{0:T(128)S(1)} %copy-done.12, bf16[3,32,192]{2,1,0:T(8,128)(2,1)S(1)} %collective-permute-done.96.refs_0_, bf16[3,32,192]{2,1,0:T(8,128)(2,1)S(1)} %collective-permute-done.97.refs_1_, ...), custom_call_target="tpu_custom_call" | custom-call | flops 191102976 | bytes 6598656 | tf_op jit(solution)/shard_map/pallas_call | solution.py:97
  512.1 3.3 collective-permute-start.108
  523.5 5.0 collective-permute-done.104.refs_0_
  528.5 15.9 %shard_map.203 = (f32[3,32,192]{2,1,0:T(8,128)S(1)}, bf16[3,32,192]{2,1,0:T(8,128)(2,1)S(1)}) custom-call(s32[81]{0:T(128)S(1)} %bitcast.77, s32[81]{0:T(128)S(1)} %bitcast.93, f32[2]{0:T(128)S(1)} %copy-done.11, bf16[3,32,192]{2,1,0:T(8,128)(2,1)S(1)} %collective-permute-done.104.refs_0_, bf16[3,32,192]{2,1,0:T(8,128)(2,1)S(1)} %collective-permute-done.105.refs_1_, ...), custom_call_target="tpu_custom_call" | custom-call | flops 191102976 | bytes 6598656 | tf_op jit(solution)/shard_map/pallas_call | solution.py:97
  546.1 3.3 collective-permute-start.116
  557.5 5.0 collective-permute-done.112.refs_0_
  562.5 15.9 %shard_map.204 = (f32[3,32,192]{2,1,0:T(8,128)S(1)}, bf16[3,32,192]{2,1,0:T(8,128)(2,1)S(1)}) custom-call(s32[81]{0:T(128)S(1)} %bitcast.78, s32[81]{0:T(128)S(1)} %bitcast.94, f32[2]{0:T(128)S(1)} %copy-done.10, bf16[3,32,192]{2,1,0:T(8,128)(2,1)S(1)} %collective-permute-done.112.refs_0_, bf16[3,32,192]{2,1,0:T(8,128)(2,1)S(1)} %collective-permute-done.113.refs_1_, ...), custom_call_target="tpu_custom_call" | custom-call | flops 191102976 | bytes 6598656 | tf_op jit(solution)/shard_map/pallas_call | solution.py:97
  580.2 3.3 collective-permute-start.124
  591.6 5.0 collective-permute-done.120.refs_0_
  596.5 16.5 %shard_map.205 = (f32[3,32,192]{2,1,0:T(8,128)S(1)}, bf16[3,32,192]{2,1,0:T(8,128)(2,1)}) custom-call(s32[81]{0:T(128)S(1)} %bitcast.79, s32[81]{0:T(128)S(1)} %bitcast.95, f32[2]{0:T(128)S(1)} %copy-done.9, bf16[3,32,192]{2,1,0:T(8,128)(2,1)S(1)} %collective-permute-done.120.refs_0_, bf16[3,32,192]{2,1,0:T(8,128)(2,1)S(1)} %collective-permute-done.121.refs_1_, ...), custom_call_target="tpu_custom_call" | custom-call | flops 191102976 | bytes 6598656 | tf_op jit(solution)/shard_map/pallas_call | solution.py:97
  613.3 37.0 %psum.15 = f32[32,32]{0,1:T(8,128)S(1)} all-reduce(f32[32,32]{0,1:T(8,128)S(1)} %convolution_bitcast_fusion.1), channel_id=1, replica_groups=mesh['gx'=4,'gy'=8] {'gx','gy'}, use_global_device_ids=true, to_apply=%region_3.6 | all-reduce | flops 1024 | bytes 8192 | tf_op jit(solution)/shard_map/psum | solution.py:120
  (267 shorter events, 147.3 us)
Async XLA Ops:
  0.9 11.3 %collective-permute-start.7 = (bf16[3,32,192]{2,1,0:T(8,128)(2,1)S(1)}, bf16[3,32,192]{2,1,0:T(8,128)(2,1)S(1)}, u32[]{:S(2)}, u32[]{:S(2)}) collective-permute-start(bf16[3,32,192]{2,1,0:T(8,128)(2,1)S(1)} %bitcast_convert_fusion.refs_4_), channel_id=1, source_target_pairs={{0,31},{1,24},{2,25},{3,26},{4,27},{5,28},{6,29},{7,30},{8,7},{9,0... | collective-permute-start | bytes 110600 | tf_op jit(solution)/shard_map/ppermute | solution.py:36
  7.3 8.5 %collective-permute-start.6 = (bf16[3,32,192]{2,1,0:T(8,128)(2,1)S(1)}, bf16[3,32,192]{2,1,0:T(8,128)(2,1)S(1)}, u32[]{:S(2)}, u32[]{:S(2)}) collective-permute-start(bf16[3,32,192]{2,1,0:T(8,128)(2,1)S(1)} %bitcast_convert_fusion.refs_4_), channel_id=1, source_target_pairs={{0,24},{1,25},{2,26},{3,27},{4,28},{5,29},{6,30},{7,31},{8,0},{9,1... | collective-permute-start | bytes 110600 | tf_op jit(solution)/shard_map/ppermute | solution.py:36
  7.8 10.4 %collective-permute-start.5 = (bf16[3,32,192]{2,1,0:T(8,128)(2,1)S(1)}, bf16[3,32,192]{2,1,0:T(8,128)(2,1)S(1)}, u32[]{:S(2)}, u32[]{:S(2)}) collective-permute-start(bf16[3,32,192]{2,1,0:T(8,128)(2,1)S(1)} %bitcast_convert_fusion.refs_4_), channel_id=1, source_target_pairs={{0,25},{1,26},{2,27},{3,28},{4,29},{5,30},{6,31},{7,24},{8,1},{9,2... | collective-permute-start | bytes 110600 | tf_op jit(solution)/shard_map/ppermute | solution.py:36
  7.8 10.4 %collective-permute-start.4 = (bf16[3,32,192]{2,1,0:T(8,128)(2,1)S(1)}, bf16[3,32,192]{2,1,0:T(8,128)(2,1)S(1)}, u32[]{:S(2)}, u32[]{:S(2)}) collective-permute-start(bf16[3,32,192]{2,1,0:T(8,128)(2,1)S(1)} %bitcast_convert_fusion.refs_4_), channel_id=1, source_target_pairs={{0,7},{1,0},{2,1},{3,2},{4,3},{5,4},{6,5},{7,6},{8,15},{9,8},{10,9... | collective-permute-start | bytes 110600 | tf_op jit(solution)/shard_map/ppermute | solution.py:36
  18.2 7.1 %collective-permute-start = (bf16[3,32,192]{2,1,0:T(8,128)(2,1)S(1)}, bf16[3,32,192]{2,1,0:T(8,128)(2,1)S(1)}, u32[]{:S(2)}, u32[]{:S(2)}) collective-permute-start(bf16[3,32,192]{2,1,0:T(8,128)(2,1)S(1)} %bitcast_convert_fusion.refs_4_), channel_id=1, source_target_pairs={{0,9},{1,10},{2,11},{3,12},{4,13},{5,14},{6,15},{7,8},{8,17},{9,18... | collective-permute-start | bytes 110600 | tf_op jit(solution)/shard_map/ppermute | solution.py:36
  47.4 8.1 %collective-permute-start.14 = (bf16[3,32,192]{2,1,0:T(8,128)(2,1)S(1)}, bf16[3,32,192]{2,1,0:T(8,128)(2,1)S(1)}, u32[]{:S(2)}, u32[]{:S(2)}) collective-permute-start(bf16[3,32,192]{2,1,0:T(8,128)(2,1)S(1)} %get-tuple-element.37.refs_4_), channel_id=1, source_target_pairs={{0,24},{1,25},{2,26},{3,27},{4,28},{5,29},{6,30},{7,31},{8,0},{9,1... | collective-permute-start | bytes 110600 | tf_op jit(solution)/shard_map/ppermute | solution.py:36
  47.5 10.9 %collective-permute-start.13 = (bf16[3,32,192]{2,1,0:T(8,128)(2,1)S(1)}, bf16[3,32,192]{2,1,0:T(8,128)(2,1)S(1)}, u32[]{:S(2)}, u32[]{:S(2)}) collective-permute-start(bf16[3,32,192]{2,1,0:T(8,128)(2,1)S(1)} %get-tuple-element.37.refs_4_), channel_id=1, source_target_pairs={{0,25},{1,26},{2,27},{3,28},{4,29},{5,30},{6,31},{7,24},{8,1},{9,2... | collective-permute-start | bytes 110600 | tf_op jit(solution)/shard_map/ppermute | solution.py:36
  49.1 9.3 %collective-permute-start.12 = (bf16[3,32,192]{2,1,0:T(8,128)(2,1)S(1)}, bf16[3,32,192]{2,1,0:T(8,128)(2,1)S(1)}, u32[]{:S(2)}, u32[]{:S(2)}) collective-permute-start(bf16[3,32,192]{2,1,0:T(8,128)(2,1)S(1)} %get-tuple-element.37.refs_4_), channel_id=1, source_target_pairs={{0,7},{1,0},{2,1},{3,2},{4,3},{5,4},{6,5},{7,6},{8,15},{9,8},{10,9... | collective-permute-start | bytes 110600 | tf_op jit(solution)/shard_map/ppermute | solution.py:36
  81.4 8.1 %collective-permute-start.22 = (bf16[3,32,192]{2,1,0:T(8,128)(2,1)S(1)}, bf16[3,32,192]{2,1,0:T(8,128)(2,1)S(1)}, u32[]{:S(2)}, u32[]{:S(2)}) collective-permute-start(bf16[3,32,192]{2,1,0:T(8,128)(2,1)S(1)} %get-tuple-element.39.refs_4_), channel_id=1, source_target_pairs={{0,24},{1,25},{2,26},{3,27},{4,28},{5,29},{6,30},{7,31},{8,0},{9,1... | collective-permute-start | bytes 110600 | tf_op jit(solution)/shard_map/ppermute | solution.py:36
  81.5 10.9 %collective-permute-start.21 = (bf16[3,32,192]{2,1,0:T(8,128)(2,1)S(1)}, bf16[3,32,192]{2,1,0:T(8,128)(2,1)S(1)}, u32[]{:S(2)}, u32[]{:S(2)}) collective-permute-start(bf16[3,32,192]{2,1,0:T(8,128)(2,1)S(1)} %get-tuple-element.39.refs_4_), channel_id=1, source_target_pairs={{0,25},{1,26},{2,27},{3,28},{4,29},{5,30},{6,31},{7,24},{8,1},{9,2... | collective-permute-start | bytes 110600 | tf_op jit(solution)/shard_map/ppermute | solution.py:36
  83.2 9.3 %collective-permute-start.20 = (bf16[3,32,192]{2,1,0:T(8,128)(2,1)S(1)}, bf16[3,32,192]{2,1,0:T(8,128)(2,1)S(1)}, u32[]{:S(2)}, u32[]{:S(2)}) collective-permute-start(bf16[3,32,192]{2,1,0:T(8,128)(2,1)S(1)} %get-tuple-element.39.refs_4_), channel_id=1, source_target_pairs={{0,7},{1,0},{2,1},{3,2},{4,3},{5,4},{6,5},{7,6},{8,15},{9,8},{10,9... | collective-permute-start | bytes 110600 | tf_op jit(solution)/shard_map/ppermute | solution.py:36
  92.4 7.1 %collective-permute-start.16 = (bf16[3,32,192]{2,1,0:T(8,128)(2,1)S(1)}, bf16[3,32,192]{2,1,0:T(8,128)(2,1)S(1)}, u32[]{:S(2)}, u32[]{:S(2)}) collective-permute-start(bf16[3,32,192]{2,1,0:T(8,128)(2,1)S(1)} %get-tuple-element.39.refs_4_), channel_id=1, source_target_pairs={{0,9},{1,10},{2,11},{3,12},{4,13},{5,14},{6,15},{7,8},{8,17},{9,18... | collective-permute-start | bytes 110600 | tf_op jit(solution)/shard_map/ppermute | solution.py:36
  115.5 8.1 %collective-permute-start.30 = (bf16[3,32,192]{2,1,0:T(8,128)(2,1)S(1)}, bf16[3,32,192]{2,1,0:T(8,128)(2,1)S(1)}, u32[]{:S(2)}, u32[]{:S(2)}) collective-permute-start(bf16[3,32,192]{2,1,0:T(8,128)(2,1)S(1)} %get-tuple-element.41.refs_4_), channel_id=1, source_target_pairs={{0,24},{1,25},{2,26},{3,27},{4,28},{5,29},{6,30},{7,31},{8,0},{9,1... | collective-permute-start | bytes 110600 | tf_op jit(solution)/shard_map/ppermute | solution.py:36
  115.6 10.9 %collective-permute-start.29 = (bf16[3,32,192]{2,1,0:T(8,128)(2,1)S(1)}, bf16[3,32,192]{2,1,0:T(8,128)(2,1)S(1)}, u32[]{:S(2)}, u32[]{:S(2)}) collective-permute-start(bf16[3,32,192]{2,1,0:T(8,128)(2,1)S(1)} %get-tuple-element.41.refs_4_), channel_id=1, source_target_pairs={{0,25},{1,26},{2,27},{3,28},{4,29},{5,30},{6,31},{7,24},{8,1},{9,2... | collective-permute-start | bytes 110600 | tf_op jit(solution)/shard_map/ppermute | solution.py:36
  117.2 9.3 %collective-permute-start.28 = (bf16[3,32,192]{2,1,0:T(8,128)(2,1)S(1)}, bf16[3,32,192]{2,1,0:T(8,128)(2,1)S(1)}, u32[]{:S(2)}, u32[]{:S(2)}) collective-permute-start(bf16[3,32,192]{2,1,0:T(8,128)(2,1)S(1)} %get-tuple-element.41.refs_4_), channel_id=1, source_target_pairs={{0,7},{1,0},{2,1},{3,2},{4,3},{5,4},{6,5},{7,6},{8,15},{9,8},{10,9... | collective-permute-start | bytes 110600 | tf_op jit(solution)/shard_map/ppermute | solution.py:36
  126.5 7.1 %collective-permute-start.24 = (bf16[3,32,192]{2,1,0:T(8,128)(2,1)S(1)}, bf16[3,32,192]{2,1,0:T(8,128)(2,1)S(1)}, u32[]{:S(2)}, u32[]{:S(2)}) collective-permute-start(bf16[3,32,192]{2,1,0:T(8,128)(2,1)S(1)} %get-tuple-element.41.refs_4_), channel_id=1, source_target_pairs={{0,9},{1,10},{2,11},{3,12},{4,13},{5,14},{6,15},{7,8},{8,17},{9,18... | collective-permute-start | bytes 110600 | tf_op jit(solution)/shard_map/ppermute | solution.py:36
  149.6 8.1 %collective-permute-start.38 = (bf16[3,32,192]{2,1,0:T(8,128)(2,1)S(1)}, bf16[3,32,192]{2,1,0:T(8,128)(2,1)S(1)}, u32[]{:S(2)}, u32[]{:S(2)}) collective-permute-start(bf16[3,32,192]{2,1,0:T(8,128)(2,1)S(1)} %get-tuple-element.43.refs_4_), channel_id=1, source_target_pairs={{0,24},{1,25},{2,26},{3,27},{4,28},{5,29},{6,30},{7,31},{8,0},{9,1... | collective-permute-start | bytes 110600 | tf_op jit(solution)/shard_map/ppermute | solution.py:36
  149.6 10.9 %collective-permute-start.37 = (bf16[3,32,192]{2,1,0:T(8,128)(2,1)S(1)}, bf16[3,32,192]{2,1,0:T(8,128)(2,1)S(1)}, u32[]{:S(2)}, u32[]{:S(2)}) collective-permute-start(bf16[3,32,192]{2,1,0:T(8,128)(2,1)S(1)} %get-tuple-element.43.refs_4_), channel_id=1, source_target_pairs={{0,25},{1,26},{2,27},{3,28},{4,29},{5,30},{6,31},{7,24},{8,1},{9,2... | collective-permute-start | bytes 110600 | tf_op jit(solution)/shard_map/ppermute | solution.py:36
  151.3 9.3 %collective-permute-start.36 = (bf16[3,32,192]{2,1,0:T(8,128)(2,1)S(1)}, bf16[3,32,192]{2,1,0:T(8,128)(2,1)S(1)}, u32[]{:S(2)}, u32[]{:S(2)}) collective-permute-start(bf16[3,32,192]{2,1,0:T(8,128)(2,1)S(1)} %get-tuple-element.43.refs_4_), channel_id=1, source_target_pairs={{0,7},{1,0},{2,1},{3,2},{4,3},{5,4},{6,5},{7,6},{8,15},{9,8},{10,9... | collective-permute-start | bytes 110600 | tf_op jit(solution)/shard_map/ppermute | solution.py:36
  160.5 7.1 %collective-permute-start.32 = (bf16[3,32,192]{2,1,0:T(8,128)(2,1)S(1)}, bf16[3,32,192]{2,1,0:T(8,128)(2,1)S(1)}, u32[]{:S(2)}, u32[]{:S(2)}) collective-permute-start(bf16[3,32,192]{2,1,0:T(8,128)(2,1)S(1)} %get-tuple-element.43.refs_4_), channel_id=1, source_target_pairs={{0,9},{1,10},{2,11},{3,12},{4,13},{5,14},{6,15},{7,8},{8,17},{9,18... | collective-permute-start | bytes 110600 | tf_op jit(solution)/shard_map/ppermute | solution.py:36
  183.6 8.1 %collective-permute-start.46 = (bf16[3,32,192]{2,1,0:T(8,128)(2,1)S(1)}, bf16[3,32,192]{2,1,0:T(8,128)(2,1)S(1)}, u32[]{:S(2)}, u32[]{:S(2)}) collective-permute-start(bf16[3,32,192]{2,1,0:T(8,128)(2,1)S(1)} %get-tuple-element.45.refs_4_), channel_id=1, source_target_pairs={{0,24},{1,25},{2,26},{3,27},{4,28},{5,29},{6,30},{7,31},{8,0},{9,1... | collective-permute-start | bytes 110600 | tf_op jit(solution)/shard_map/ppermute | solution.py:36
  183.7 10.9 %collective-permute-start.45 = (bf16[3,32,192]{2,1,0:T(8,128)(2,1)S(1)}, bf16[3,32,192]{2,1,0:T(8,128)(2,1)S(1)}, u32[]{:S(2)}, u32[]{:S(2)}) collective-permute-start(bf16[3,32,192]{2,1,0:T(8,128)(2,1)S(1)} %get-tuple-element.45.refs_4_), channel_id=1, source_target_pairs={{0,25},{1,26},{2,27},{3,28},{4,29},{5,30},{6,31},{7,24},{8,1},{9,2... | collective-permute-start | bytes 110600 | tf_op jit(solution)/shard_map/ppermute | solution.py:36
  185.3 9.3 %collective-permute-start.44 = (bf16[3,32,192]{2,1,0:T(8,128)(2,1)S(1)}, bf16[3,32,192]{2,1,0:T(8,128)(2,1)S(1)}, u32[]{:S(2)}, u32[]{:S(2)}) collective-permute-start(bf16[3,32,192]{2,1,0:T(8,128)(2,1)S(1)} %get-tuple-element.45.refs_4_), channel_id=1, source_target_pairs={{0,7},{1,0},{2,1},{3,2},{4,3},{5,4},{6,5},{7,6},{8,15},{9,8},{10,9... | collective-permute-start | bytes 110600 | tf_op jit(solution)/shard_map/ppermute | solution.py:36
  194.6 7.1 %collective-permute-start.40 = (bf16[3,32,192]{2,1,0:T(8,128)(2,1)S(1)}, bf16[3,32,192]{2,1,0:T(8,128)(2,1)S(1)}, u32[]{:S(2)}, u32[]{:S(2)}) collective-permute-start(bf16[3,32,192]{2,1,0:T(8,128)(2,1)S(1)} %get-tuple-element.45.refs_4_), channel_id=1, source_target_pairs={{0,9},{1,10},{2,11},{3,12},{4,13},{5,14},{6,15},{7,8},{8,17},{9,18... | collective-permute-start | bytes 110600 | tf_op jit(solution)/shard_map/ppermute | solution.py:36
  217.7 8.1 %collective-permute-start.54 = (bf16[3,32,192]{2,1,0:T(8,128)(2,1)S(1)}, bf16[3,32,192]{2,1,0:T(8,128)(2,1)S(1)}, u32[]{:S(2)}, u32[]{:S(2)}) collective-permute-start(bf16[3,32,192]{2,1,0:T(8,128)(2,1)S(1)} %get-tuple-element.47.refs_4_), channel_id=1, source_target_pairs={{0,24},{1,25},{2,26},{3,27},{4,28},{5,29},{6,30},{7,31},{8,0},{9,1... | collective-permute-start | bytes 110600 | tf_op jit(solution)/shard_map/ppermute | solution.py:36
  217.7 10.9 %collective-permute-start.53 = (bf16[3,32,192]{2,1,0:T(8,128)(2,1)S(1)}, bf16[3,32,192]{2,1,0:T(8,128)(2,1)S(1)}, u32[]{:S(2)}, u32[]{:S(2)}) collective-permute-start(bf16[3,32,192]{2,1,0:T(8,128)(2,1)S(1)} %get-tuple-element.47.refs_4_), channel_id=1, source_target_pairs={{0,25},{1,26},{2,27},{3,28},{4,29},{5,30},{6,31},{7,24},{8,1},{9,2... | collective-permute-start | bytes 110600 | tf_op jit(solution)/shard_map/ppermute | solution.py:36
  219.4 9.3 %collective-permute-start.52 = (bf16[3,32,192]{2,1,0:T(8,128)(2,1)S(1)}, bf16[3,32,192]{2,1,0:T(8,128)(2,1)S(1)}, u32[]{:S(2)}, u32[]{:S(2)}) collective-permute-start(bf16[3,32,192]{2,1,0:T(8,128)(2,1)S(1)} %get-tuple-element.47.refs_4_), channel_id=1, source_target_pairs={{0,7},{1,0},{2,1},{3,2},{4,3},{5,4},{6,5},{7,6},{8,15},{9,8},{10,9... | collective-permute-start | bytes 110600 | tf_op jit(solution)/shard_map/ppermute | solution.py:36
  228.6 7.1 %collective-permute-start.48 = (bf16[3,32,192]{2,1,0:T(8,128)(2,1)S(1)}, bf16[3,32,192]{2,1,0:T(8,128)(2,1)S(1)}, u32[]{:S(2)}, u32[]{:S(2)}) collective-permute-start(bf16[3,32,192]{2,1,0:T(8,128)(2,1)S(1)} %get-tuple-element.47.refs_4_), channel_id=1, source_target_pairs={{0,9},{1,10},{2,11},{3,12},{4,13},{5,14},{6,15},{7,8},{8,17},{9,18... | collective-permute-start | bytes 110600 | tf_op jit(solution)/shard_map/ppermute | solution.py:36
  251.7 8.1 %collective-permute-start.62 = (bf16[3,32,192]{2,1,0:T(8,128)(2,1)S(1)}, bf16[3,32,192]{2,1,0:T(8,128)(2,1)S(1)}, u32[]{:S(2)}, u32[]{:S(2)}) collective-permute-start(bf16[3,32,192]{2,1,0:T(8,128)(2,1)S(1)} %get-tuple-element.49.refs_4_), channel_id=1, source_target_pairs={{0,24},{1,25},{2,26},{3,27},{4,28},{5,29},{6,30},{7,31},{8,0},{9,1... | collective-permute-start | bytes 110600 | tf_op jit(solution)/shard_map/ppermute | solution.py:36
  251.8 10.9 %collective-permute-start.61 = (bf16[3,32,192]{2,1,0:T(8,128)(2,1)S(1)}, bf16[3,32,192]{2,1,0:T(8,128)(2,1)S(1)}, u32[]{:S(2)}, u32[]{:S(2)}) collective-permute-start(bf16[3,32,192]{2,1,0:T(8,128)(2,1)S(1)} %get-tuple-element.49.refs_4_), channel_id=1, source_target_pairs={{0,25},{1,26},{2,27},{3,28},{4,29},{5,30},{6,31},{7,24},{8,1},{9,2... | collective-permute-start | bytes 110600 | tf_op jit(solution)/shard_map/ppermute | solution.py:36
  253.4 9.3 %collective-permute-start.60 = (bf16[3,32,192]{2,1,0:T(8,128)(2,1)S(1)}, bf16[3,32,192]{2,1,0:T(8,128)(2,1)S(1)}, u32[]{:S(2)}, u32[]{:S(2)}) collective-permute-start(bf16[3,32,192]{2,1,0:T(8,128)(2,1)S(1)} %get-tuple-element.49.refs_4_), channel_id=1, source_target_pairs={{0,7},{1,0},{2,1},{3,2},{4,3},{5,4},{6,5},{7,6},{8,15},{9,8},{10,9... | collective-permute-start | bytes 110600 | tf_op jit(solution)/shard_map/ppermute | solution.py:36
  262.7 7.1 %collective-permute-start.56 = (bf16[3,32,192]{2,1,0:T(8,128)(2,1)S(1)}, bf16[3,32,192]{2,1,0:T(8,128)(2,1)S(1)}, u32[]{:S(2)}, u32[]{:S(2)}) collective-permute-start(bf16[3,32,192]{2,1,0:T(8,128)(2,1)S(1)} %get-tuple-element.49.refs_4_), channel_id=1, source_target_pairs={{0,9},{1,10},{2,11},{3,12},{4,13},{5,14},{6,15},{7,8},{8,17},{9,18... | collective-permute-start | bytes 110600 | tf_op jit(solution)/shard_map/ppermute | solution.py:36
  331.0 7.6 %collective-permute-start.71 = (bf16[3,32,192]{2,1,0:T(8,128)(2,1)S(1)}, bf16[3,32,192]{2,1,0:T(8,128)(2,1)S(1)}, u32[]{:S(2)}, u32[]{:S(2)}) collective-permute-start(bf16[3,32,192]{2,1,0:T(8,128)(2,1)S(1)} %get-tuple-element.67.refs_4_), channel_id=1, source_target_pairs={{0,31},{1,24},{2,25},{3,26},{4,27},{5,28},{6,29},{7,30},{8,7},{9,0... | collective-permute-start | bytes 110600 | tf_op jit(solution)/shard_map/ppermute | solution.py:36
  333.6 8.5 %collective-permute-start.70 = (bf16[3,32,192]{2,1,0:T(8,128)(2,1)S(1)}, bf16[3,32,192]{2,1,0:T(8,128)(2,1)S(1)}, u32[]{:S(2)}, u32[]{:S(2)}) collective-permute-start(bf16[3,32,192]{2,1,0:T(8,128)(2,1)S(1)} %get-tuple-element.67.refs_4_), channel_id=1, source_target_pairs={{0,24},{1,25},{2,26},{3,27},{4,28},{5,29},{6,30},{7,31},{8,0},{9,1... | collective-permute-start | bytes 110600 | tf_op jit(solution)/shard_map/ppermute | solution.py:36
  334.2 10.4 %collective-permute-start.69 = (bf16[3,32,192]{2,1,0:T(8,128)(2,1)S(1)}, bf16[3,32,192]{2,1,0:T(8,128)(2,1)S(1)}, u32[]{:S(2)}, u32[]{:S(2)}) collective-permute-start(bf16[3,32,192]{2,1,0:T(8,128)(2,1)S(1)} %get-tuple-element.67.refs_4_), channel_id=1, source_target_pairs={{0,25},{1,26},{2,27},{3,28},{4,29},{5,30},{6,31},{7,24},{8,1},{9,2... | collective-permute-start | bytes 110600 | tf_op jit(solution)/shard_map/ppermute | solution.py:36
  335.7 8.9 %collective-permute-start.68 = (bf16[3,32,192]{2,1,0:T(8,128)(2,1)S(1)}, bf16[3,32,192]{2,1,0:T(8,128)(2,1)S(1)}, u32[]{:S(2)}, u32[]{:S(2)}) collective-permute-start(bf16[3,32,192]{2,1,0:T(8,128)(2,1)S(1)} %get-tuple-element.67.refs_4_), channel_id=1, source_target_pairs={{0,7},{1,0},{2,1},{3,2},{4,3},{5,4},{6,5},{7,6},{8,15},{9,8},{10,9... | collective-permute-start | bytes 110600 | tf_op jit(solution)/shard_map/ppermute | solution.py:36
  344.6 7.1 %collective-permute-start.64 = (bf16[3,32,192]{2,1,0:T(8,128)(2,1)S(1)}, bf16[3,32,192]{2,1,0:T(8,128)(2,1)S(1)}, u32[]{:S(2)}, u32[]{:S(2)}) collective-permute-start(bf16[3,32,192]{2,1,0:T(8,128)(2,1)S(1)} %get-tuple-element.67.refs_4_), channel_id=1, source_target_pairs={{0,9},{1,10},{2,11},{3,12},{4,13},{5,14},{6,15},{7,8},{8,17},{9,18... | collective-permute-start | bytes 110600 | tf_op jit(solution)/shard_map/ppermute | solution.py:36
  370.9 8.1 %collective-permute-start.78 = (bf16[3,32,192]{2,1,0:T(8,128)(2,1)S(1)}, bf16[3,32,192]{2,1,0:T(8,128)(2,1)S(1)}, u32[]{:S(2)}, u32[]{:S(2)}) collective-permute-start(bf16[3,32,192]{2,1,0:T(8,128)(2,1)S(1)} %get-tuple-element.52.refs_4_), channel_id=1, source_target_pairs={{0,24},{1,25},{2,26},{3,27},{4,28},{5,29},{6,30},{7,31},{8,0},{9,1... | collective-permute-start | bytes 110600 | tf_op jit(solution)/shard_map/ppermute | solution.py:36
  371.0 10.9 %collective-permute-start.77 = (bf16[3,32,192]{2,1,0:T(8,128)(2,1)S(1)}, bf16[3,32,192]{2,1,0:T(8,128)(2,1)S(1)}, u32[]{:S(2)}, u32[]{:S(2)}) collective-permute-start(bf16[3,32,192]{2,1,0:T(8,128)(2,1)S(1)} %get-tuple-element.52.refs_4_), channel_id=1, source_target_pairs={{0,25},{1,26},{2,27},{3,28},{4,29},{5,30},{6,31},{7,24},{8,1},{9,2... | collective-permute-start | bytes 110600 | tf_op jit(solution)/shard_map/ppermute | solution.py:36
  372.6 9.3 %collective-permute-start.76 = (bf16[3,32,192]{2,1,0:T(8,128)(2,1)S(1)}, bf16[3,32,192]{2,1,0:T(8,128)(2,1)S(1)}, u32[]{:S(2)}, u32[]{:S(2)}) collective-permute-start(bf16[3,32,192]{2,1,0:T(8,128)(2,1)S(1)} %get-tuple-element.52.refs_4_), channel_id=1, source_target_pairs={{0,7},{1,0},{2,1},{3,2},{4,3},{5,4},{6,5},{7,6},{8,15},{9,8},{10,9... | collective-permute-start | bytes 110600 | tf_op jit(solution)/shard_map/ppermute | solution.py:36
  381.9 7.1 %collective-permute-start.72 = (bf16[3,32,192]{2,1,0:T(8,128)(2,1)S(1)}, bf16[3,32,192]{2,1,0:T(8,128)(2,1)S(1)}, u32[]{:S(2)}, u32[]{:S(2)}) collective-permute-start(bf16[3,32,192]{2,1,0:T(8,128)(2,1)S(1)} %get-tuple-element.52.refs_4_), channel_id=1, source_target_pairs={{0,9},{1,10},{2,11},{3,12},{4,13},{5,14},{6,15},{7,8},{8,17},{9,18... | collective-permute-start | bytes 110600 | tf_op jit(solution)/shard_map/ppermute | solution.py:36
  408.2 8.1 %collective-permute-start.86 = (bf16[3,32,192]{2,1,0:T(8,128)(2,1)S(1)}, bf16[3,32,192]{2,1,0:T(8,128)(2,1)S(1)}, u32[]{:S(2)}, u32[]{:S(2)}) collective-permute-start(bf16[3,32,192]{2,1,0:T(8,128)(2,1)S(1)} %get-tuple-element.54.refs_4_), channel_id=1, source_target_pairs={{0,24},{1,25},{2,26},{3,27},{4,28},{5,29},{6,30},{7,31},{8,0},{9,1... | collective-permute-start | bytes 110600 | tf_op jit(solution)/shard_map/ppermute | solution.py:36
  408.3 10.9 %collective-permute-start.85 = (bf16[3,32,192]{2,1,0:T(8,128)(2,1)S(1)}, bf16[3,32,192]{2,1,0:T(8,128)(2,1)S(1)}, u32[]{:S(2)}, u32[]{:S(2)}) collective-permute-start(bf16[3,32,192]{2,1,0:T(8,128)(2,1)S(1)} %get-tuple-element.54.refs_4_), channel_id=1, source_target_pairs={{0,25},{1,26},{2,27},{3,28},{4,29},{5,30},{6,31},{7,24},{8,1},{9,2... | collective-permute-start | bytes 110600 | tf_op jit(solution)/shard_map/ppermute | solution.py:36
  409.9 9.3 %collective-permute-start.84 = (bf16[3,32,192]{2,1,0:T(8,128)(2,1)S(1)}, bf16[3,32,192]{2,1,0:T(8,128)(2,1)S(1)}, u32[]{:S(2)}, u32[]{:S(2)}) collective-permute-start(bf16[3,32,192]{2,1,0:T(8,128)(2,1)S(1)} %get-tuple-element.54.refs_4_), channel_id=1, source_target_pairs={{0,7},{1,0},{2,1},{3,2},{4,3},{5,4},{6,5},{7,6},{8,15},{9,8},{10,9... | collective-permute-start | bytes 110600 | tf_op jit(solution)/shard_map/ppermute | solution.py:36
  419.2 7.1 %collective-permute-start.80 = (bf16[3,32,192]{2,1,0:T(8,128)(2,1)S(1)}, bf16[3,32,192]{2,1,0:T(8,128)(2,1)S(1)}, u32[]{:S(2)}, u32[]{:S(2)}) collective-permute-start(bf16[3,32,192]{2,1,0:T(8,128)(2,1)S(1)} %get-tuple-element.54.refs_4_), channel_id=1, source_target_pairs={{0,9},{1,10},{2,11},{3,12},{4,13},{5,14},{6,15},{7,8},{8,17},{9,18... | collective-permute-start | bytes 110600 | tf_op jit(solution)/shard_map/ppermute | solution.py:36
  442.3 8.1 %collective-permute-start.94 = (bf16[3,32,192]{2,1,0:T(8,128)(2,1)S(1)}, bf16[3,32,192]{2,1,0:T(8,128)(2,1)S(1)}, u32[]{:S(2)}, u32[]{:S(2)}) collective-permute-start(bf16[3,32,192]{2,1,0:T(8,128)(2,1)S(1)} %get-tuple-element.56.refs_4_), channel_id=1, source_target_pairs={{0,24},{1,25},{2,26},{3,27},{4,28},{5,29},{6,30},{7,31},{8,0},{9,1... | collective-permute-start | bytes 110600 | tf_op jit(solution)/shard_map/ppermute | solution.py:36
  442.3 10.9 %collective-permute-start.93 = (bf16[3,32,192]{2,1,0:T(8,128)(2,1)S(1)}, bf16[3,32,192]{2,1,0:T(8,128)(2,1)S(1)}, u32[]{:S(2)}, u32[]{:S(2)}) collective-permute-start(bf16[3,32,192]{2,1,0:T(8,128)(2,1)S(1)} %get-tuple-element.56.refs_4_), channel_id=1, source_target_pairs={{0,25},{1,26},{2,27},{3,28},{4,29},{5,30},{6,31},{7,24},{8,1},{9,2... | collective-permute-start | bytes 110600 | tf_op jit(solution)/shard_map/ppermute | solution.py:36
  444.0 9.3 %collective-permute-start.92 = (bf16[3,32,192]{2,1,0:T(8,128)(2,1)S(1)}, bf16[3,32,192]{2,1,0:T(8,128)(2,1)S(1)}, u32[]{:S(2)}, u32[]{:S(2)}) collective-permute-start(bf16[3,32,192]{2,1,0:T(8,128)(2,1)S(1)} %get-tuple-element.56.refs_4_), channel_id=1, source_target_pairs={{0,7},{1,0},{2,1},{3,2},{4,3},{5,4},{6,5},{7,6},{8,15},{9,8},{10,9... | collective-permute-start | bytes 110600 | tf_op jit(solution)/shard_map/ppermute | solution.py:36
  453.2 7.1 %collective-permute-start.88 = (bf16[3,32,192]{2,1,0:T(8,128)(2,1)S(1)}, bf16[3,32,192]{2,1,0:T(8,128)(2,1)S(1)}, u32[]{:S(2)}, u32[]{:S(2)}) collective-permute-start(bf16[3,32,192]{2,1,0:T(8,128)(2,1)S(1)} %get-tuple-element.56.refs_4_), channel_id=1, source_target_pairs={{0,9},{1,10},{2,11},{3,12},{4,13},{5,14},{6,15},{7,8},{8,17},{9,18... | collective-permute-start | bytes 110600 | tf_op jit(solution)/shard_map/ppermute | solution.py:36
  476.3 8.1 %collective-permute-start.102 = (bf16[3,32,192]{2,1,0:T(8,128)(2,1)S(1)}, bf16[3,32,192]{2,1,0:T(8,128)(2,1)S(1)}, u32[]{:S(2)}, u32[]{:S(2)}) collective-permute-start(bf16[3,32,192]{2,1,0:T(8,128)(2,1)S(1)} %get-tuple-element.58.refs_4_), channel_id=1, source_target_pairs={{0,24},{1,25},{2,26},{3,27},{4,28},{5,29},{6,30},{7,31},{8,0},{9,1... | collective-permute-start | bytes 110600 | tf_op jit(solution)/shard_map/ppermute | solution.py:36
  476.4 10.9 %collective-permute-start.101 = (bf16[3,32,192]{2,1,0:T(8,128)(2,1)S(1)}, bf16[3,32,192]{2,1,0:T(8,128)(2,1)S(1)}, u32[]{:S(2)}, u32[]{:S(2)}) collective-permute-start(bf16[3,32,192]{2,1,0:T(8,128)(2,1)S(1)} %get-tuple-element.58.refs_4_), channel_id=1, source_target_pairs={{0,25},{1,26},{2,27},{3,28},{4,29},{5,30},{6,31},{7,24},{8,1},{9,2... | collective-permute-start | bytes 110600 | tf_op jit(solution)/shard_map/ppermute | solution.py:36
  478.0 9.3 %collective-permute-start.100 = (bf16[3,32,192]{2,1,0:T(8,128)(2,1)S(1)}, bf16[3,32,192]{2,1,0:T(8,128)(2,1)S(1)}, u32[]{:S(2)}, u32[]{:S(2)}) collective-permute-start(bf16[3,32,192]{2,1,0:T(8,128)(2,1)S(1)} %get-tuple-element.58.refs_4_), channel_id=1, source_target_pairs={{0,7},{1,0},{2,1},{3,2},{4,3},{5,4},{6,5},{7,6},{8,15},{9,8},{10,9... | collective-permute-start | bytes 110600 | tf_op jit(solution)/shard_map/ppermute | solution.py:36
  487.3 7.1 %collective-permute-start.96 = (bf16[3,32,192]{2,1,0:T(8,128)(2,1)S(1)}, bf16[3,32,192]{2,1,0:T(8,128)(2,1)S(1)}, u32[]{:S(2)}, u32[]{:S(2)}) collective-permute-start(bf16[3,32,192]{2,1,0:T(8,128)(2,1)S(1)} %get-tuple-element.58.refs_4_), channel_id=1, source_target_pairs={{0,9},{1,10},{2,11},{3,12},{4,13},{5,14},{6,15},{7,8},{8,17},{9,18... | collective-permute-start | bytes 110600 | tf_op jit(solution)/shard_map/ppermute | solution.py:36
  510.4 8.1 %collective-permute-start.110 = (bf16[3,32,192]{2,1,0:T(8,128)(2,1)S(1)}, bf16[3,32,192]{2,1,0:T(8,128)(2,1)S(1)}, u32[]{:S(2)}, u32[]{:S(2)}) collective-permute-start(bf16[3,32,192]{2,1,0:T(8,128)(2,1)S(1)} %get-tuple-element.60.refs_4_), channel_id=1, source_target_pairs={{0,24},{1,25},{2,26},{3,27},{4,28},{5,29},{6,30},{7,31},{8,0},{9,1... | collective-permute-start | bytes 110600 | tf_op jit(solution)/shard_map/ppermute | solution.py:36
  510.4 10.9 %collective-permute-start.109 = (bf16[3,32,192]{2,1,0:T(8,128)(2,1)S(1)}, bf16[3,32,192]{2,1,0:T(8,128)(2,1)S(1)}, u32[]{:S(2)}, u32[]{:S(2)}) collective-permute-start(bf16[3,32,192]{2,1,0:T(8,128)(2,1)S(1)} %get-tuple-element.60.refs_4_), channel_id=1, source_target_pairs={{0,25},{1,26},{2,27},{3,28},{4,29},{5,30},{6,31},{7,24},{8,1},{9,2... | collective-permute-start | bytes 110600 | tf_op jit(solution)/shard_map/ppermute | solution.py:36
  512.1 9.3 %collective-permute-start.108 = (bf16[3,32,192]{2,1,0:T(8,128)(2,1)S(1)}, bf16[3,32,192]{2,1,0:T(8,128)(2,1)S(1)}, u32[]{:S(2)}, u32[]{:S(2)}) collective-permute-start(bf16[3,32,192]{2,1,0:T(8,128)(2,1)S(1)} %get-tuple-element.60.refs_4_), channel_id=1, source_target_pairs={{0,7},{1,0},{2,1},{3,2},{4,3},{5,4},{6,5},{7,6},{8,15},{9,8},{10,9... | collective-permute-start | bytes 110600 | tf_op jit(solution)/shard_map/ppermute | solution.py:36
  521.3 7.1 %collective-permute-start.104 = (bf16[3,32,192]{2,1,0:T(8,128)(2,1)S(1)}, bf16[3,32,192]{2,1,0:T(8,128)(2,1)S(1)}, u32[]{:S(2)}, u32[]{:S(2)}) collective-permute-start(bf16[3,32,192]{2,1,0:T(8,128)(2,1)S(1)} %get-tuple-element.60.refs_4_), channel_id=1, source_target_pairs={{0,9},{1,10},{2,11},{3,12},{4,13},{5,14},{6,15},{7,8},{8,17},{9,18... | collective-permute-start | bytes 110600 | tf_op jit(solution)/shard_map/ppermute | solution.py:36
  544.4 8.1 %collective-permute-start.118 = (bf16[3,32,192]{2,1,0:T(8,128)(2,1)S(1)}, bf16[3,32,192]{2,1,0:T(8,128)(2,1)S(1)}, u32[]{:S(2)}, u32[]{:S(2)}) collective-permute-start(bf16[3,32,192]{2,1,0:T(8,128)(2,1)S(1)} %get-tuple-element.62.refs_4_), channel_id=1, source_target_pairs={{0,24},{1,25},{2,26},{3,27},{4,28},{5,29},{6,30},{7,31},{8,0},{9,1... | collective-permute-start | bytes 110600 | tf_op jit(solution)/shard_map/ppermute | solution.py:36
  544.5 10.9 %collective-permute-start.117 = (bf16[3,32,192]{2,1,0:T(8,128)(2,1)S(1)}, bf16[3,32,192]{2,1,0:T(8,128)(2,1)S(1)}, u32[]{:S(2)}, u32[]{:S(2)}) collective-permute-start(bf16[3,32,192]{2,1,0:T(8,128)(2,1)S(1)} %get-tuple-element.62.refs_4_), channel_id=1, source_target_pairs={{0,25},{1,26},{2,27},{3,28},{4,29},{5,30},{6,31},{7,24},{8,1},{9,2... | collective-permute-start | bytes 110600 | tf_op jit(solution)/shard_map/ppermute | solution.py:36
  546.1 9.3 %collective-permute-start.116 = (bf16[3,32,192]{2,1,0:T(8,128)(2,1)S(1)}, bf16[3,32,192]{2,1,0:T(8,128)(2,1)S(1)}, u32[]{:S(2)}, u32[]{:S(2)}) collective-permute-start(bf16[3,32,192]{2,1,0:T(8,128)(2,1)S(1)} %get-tuple-element.62.refs_4_), channel_id=1, source_target_pairs={{0,7},{1,0},{2,1},{3,2},{4,3},{5,4},{6,5},{7,6},{8,15},{9,8},{10,9... | collective-permute-start | bytes 110600 | tf_op jit(solution)/shard_map/ppermute | solution.py:36
  555.4 7.1 %collective-permute-start.112 = (bf16[3,32,192]{2,1,0:T(8,128)(2,1)S(1)}, bf16[3,32,192]{2,1,0:T(8,128)(2,1)S(1)}, u32[]{:S(2)}, u32[]{:S(2)}) collective-permute-start(bf16[3,32,192]{2,1,0:T(8,128)(2,1)S(1)} %get-tuple-element.62.refs_4_), channel_id=1, source_target_pairs={{0,9},{1,10},{2,11},{3,12},{4,13},{5,14},{6,15},{7,8},{8,17},{9,18... | collective-permute-start | bytes 110600 | tf_op jit(solution)/shard_map/ppermute | solution.py:36
  578.5 8.1 %collective-permute-start.126 = (bf16[3,32,192]{2,1,0:T(8,128)(2,1)S(1)}, bf16[3,32,192]{2,1,0:T(8,128)(2,1)S(1)}, u32[]{:S(2)}, u32[]{:S(2)}) collective-permute-start(bf16[3,32,192]{2,1,0:T(8,128)(2,1)S(1)} %get-tuple-element.64.refs_4_), channel_id=1, source_target_pairs={{0,24},{1,25},{2,26},{3,27},{4,28},{5,29},{6,30},{7,31},{8,0},{9,1... | collective-permute-start | bytes 110600 | tf_op jit(solution)/shard_map/ppermute | solution.py:36
  578.5 10.9 %collective-permute-start.125 = (bf16[3,32,192]{2,1,0:T(8,128)(2,1)S(1)}, bf16[3,32,192]{2,1,0:T(8,128)(2,1)S(1)}, u32[]{:S(2)}, u32[]{:S(2)}) collective-permute-start(bf16[3,32,192]{2,1,0:T(8,128)(2,1)S(1)} %get-tuple-element.64.refs_4_), channel_id=1, source_target_pairs={{0,25},{1,26},{2,27},{3,28},{4,29},{5,30},{6,31},{7,24},{8,1},{9,2... | collective-permute-start | bytes 110600 | tf_op jit(solution)/shard_map/ppermute | solution.py:36
  580.2 9.3 %collective-permute-start.124 = (bf16[3,32,192]{2,1,0:T(8,128)(2,1)S(1)}, bf16[3,32,192]{2,1,0:T(8,128)(2,1)S(1)}, u32[]{:S(2)}, u32[]{:S(2)}) collective-permute-start(bf16[3,32,192]{2,1,0:T(8,128)(2,1)S(1)} %get-tuple-element.64.refs_4_), channel_id=1, source_target_pairs={{0,7},{1,0},{2,1},{3,2},{4,3},{5,4},{6,5},{7,6},{8,15},{9,8},{10,9... | collective-permute-start | bytes 110600 | tf_op jit(solution)/shard_map/ppermute | solution.py:36
  (82 other events, 989.5 us)

commit v2 on v0

--- a/solution.py
+++ b/solution.py
@@ -30,42 +30,48 @@
     return cells
 
 
+def dense_coupling(matrices, targets, sources, depth, cells):
+    slots = matrices.shape[0]
+    match = (targets[:, None, None] == jnp.arange(depth, dtype=jnp.int32)[None, :, None]) & (
+        sources[:, None, None] == jnp.arange(cells, dtype=jnp.int32)[None, None, :]
+    )
+    slot_ids = jnp.arange(slots, dtype=jnp.int32)[:, None, None]
+    index = jnp.sum(jnp.where(match, slot_ids, 0), axis=0)
+    present = jnp.any(match, axis=0)
+    blocks = jnp.take(matrices, index.reshape(-1), axis=0).reshape(
+        depth, cells, matrices.shape[1], matrices.shape[2]
+    )
+    blocks = jnp.where(present[:, :, None, None], blocks, jnp.zeros((), matrices.dtype))
+    return jnp.transpose(blocks, (0, 2, 1, 3))
+
+
 def orthonormal(filtered, rows_total):
-    local_block = filtered[0, 0]
     partial_gram = jnp.einsum(
-        "zvd,zwd->vw", local_block, local_block, precision=lax.Precision.HIGHEST
+        "zvd,zwd->vw", filtered, filtered, precision=lax.Precision.HIGHEST
     )
     gram_matrix = lax.psum(partial_gram, ("gx", "gy"))
     factor = jnp.linalg.cholesky(gram_matrix)
-    identity = jnp.eye(local_block.shape[1], dtype=jnp.float32)
+    identity = jnp.eye(filtered.shape[1], dtype=jnp.float32)
     inverse = jax.scipy.linalg.solve_triangular(factor, identity, lower=True)
-    result = jnp.einsum("vw,zwd->zvd", inverse, local_block, precision=lax.Precision.HIGHEST)
-    return (result * math.sqrt(rows_total))[None, None]
+    result = jnp.einsum("vw,zwd->zvd", inverse, filtered, precision=lax.Precision.HIGHEST)
+    return result * math.sqrt(rows_total)
 
 
 def local(basis, coupling, cpl_dst, cpl_src):
     column_depth = basis.shape[2]
     vector_count = basis.shape[3]
     block_rows = basis.shape[4]
-    matrices = coupling[0, 0]
-    targets = cpl_dst[0, 0]
-    sources = cpl_src[0, 0]
     rows_total = lax.axis_size("gx") * lax.axis_size("gy") * column_depth * block_rows
-    select = (targets[None, :] == jnp.arange(column_depth, dtype=jnp.int32)[:, None]).astype(
-        jnp.float32
-    )
+    dense = dense_coupling(coupling[0, 0], cpl_dst[0, 0], cpl_src[0, 0], column_depth, 9 * column_depth)
 
     def apply_operator(current):
-        rounded = current.astype(jnp.bfloat16)
+        rounded = current.astype(jnp.bfloat16)[None, None]
         window = with_halo(rounded, (("gx", 0), ("gy", 1)), 1)
         window_cells = window.reshape(9 * column_depth, vector_count, block_rows)
-        picked = jnp.take(window_cells, sources, axis=0)
-        products = jnp.einsum("kvj,kij->kvi", picked, matrices, preferred_element_type=jnp.float32)
-        applied = jnp.einsum("zk,kvi->zvi", select, products, precision=lax.Precision.HIGHEST)
-        return applied[None, None]
+        return jnp.einsum("kvj,tikj->tvi", window_cells, dense, preferred_element_type=jnp.float32)
 
     sigma_one = HALF / (LOWEST - CENTER)
-    current_basis = basis
+    current_basis = basis[0, 0]
     for outer in range(STEPS):
         previous = current_basis
         current = sigma_one / HALF * (apply_operator(previous) - CENTER * previous)
@@ -79,7 +85,7 @@
             )
             previous, current, sigma_now = (current, following, sigma_next)
         current_basis = orthonormal(current, rows_total)
-    return current_basis
+    return current_basis[None, None]
 
 
 def solution(mesh):

time: 466 us -> 366 us (0.79); the launches traced: 458 us -> 365 us
  matrix products: 136 us -> 57.8 us
  waiting for transfers between devices: 163 us -> 155 us
    dot_general x36 -> x20, matrix products: 135 us -> 57.3 us  [the longest x16 55.7 us: apply_operator(): jnp.einsum('kvj,tikj->tvi', window_cells, dense, preferred_element_type=j...]
    ppermute x32, waiting for transfers between devices: 95.3 us -> 84.9 us  [with_halo(): lax.ppermute(head, axis, [((i + 1) % count, i) for i in range(count)])]
    gather x16 -> x1, local copies, waits for them, and re-layouts: 10.9 us -> 10.3 us  [dense_coupling(): jnp.take(matrices, index.reshape(-1), axis=0)]
  transfers between devices with their start and end apart: 64 -> 64, of which waited for: 64 -> 62; matrix products, arithmetic and copies ran while one was open for 0% -> 3% of each run, Pallas kernels for 0% -> 0%
where the time goes in v2:
time: 366 us; the launch traced here: 365 us
  waiting for transfers between devices  155 us (42%)
  blocking collectives  75.1 us (21%)
  matrix products  57.8 us (16%)
  starting transfers between devices  48.1 us (13%)
  other arithmetic  18.4 us (5%)
  local copies, waits for them, and re-layouts  10.5 us (3%)
    ppermute x32, waiting for transfers between devices, with_halo(): lax.ppermute(head, axis, [((i + 1) % count, i) for i in range(count)])  84.9 us
    psum x2, blocking collectives, orthonormal(): gram_matrix = lax.psum(partial_gram, ('gx', 'gy'))  75.1 us
    ppermute x32, waiting for transfers between devices, with_halo(): lax.ppermute(tail, axis, [(i, (i + 1) % count) for i in range(count)])  69.7 us
    dot_general x16, matrix products, apply_operator(): jnp.einsum('kvj,tikj->tvi', window_cells, dense, preferred_element_type=j...  55.7 us
    ppermute x32, starting transfers between devices, with_halo(): lax.ppermute(head, axis, [((i + 1) % count, i) for i in range(count)])  24.8 us
    ppermute x32, starting transfers between devices, with_halo(): lax.ppermute(tail, axis, [(i, (i + 1) % count) for i in range(count)])  23.2 us
    gather x1, local copies, waits for them, and re-layouts, dense_coupling(): jnp.take(matrices, index.reshape(-1), axis=0)  10.3 us
  transfers between devices with their start and end apart: 64, of which 62 were waited for; matrix products, arithmetic and copies ran while one was open for 3% of the time, Pallas kernels for 0%

profile of v2, /device:TPU:0, one launch (start us, length us, event | category | flops | bytes accessed | tf_op | source)
XLA Modules:
  0.0 365.2 jit_solution(5078331061172338378)
XLA Ops:
  0.9 3.9 %collective-permute-start.1 = (bf16[1,1,3,32,192]{4,3,2,1,0:T(8,128)(2,1)S(1)}, bf16[1,1,3,32,192]{4,3,2,1,0:T(8,128)(2,1)S(1)}, u32[]{:S(2)}, u32[]{:S(2)}) collective-permute-start(bf16[1,1,3,32,192]{4,3,2,1,0:T(8,128)(2,1)S(1)} %convert_element_type.61), channel_id=1, source_target_pairs={{8,0},{16,8},{24,16},{0,24},{9,1},{17,9},{25,17},{1,25},{10,2},{18... | collective-permute-start | bytes 110600 | tf_op jit(solution)/shard_map/ppermute | solution.py:26
  6.4 10.3 %gather_fusion = bf16[81,192,192]{2,1,0:T(8,128)(2,1)} fusion(bf16[81,192,192]{2,1,0:T(8,128)(2,1)} %bitcast.477, s32[1024]{0:T(1024)S(1)} %pad_clamp_fusion), kind=kCustom, calls=%fused_computation | custom fusion | bytes 11944260 | tf_op jit(solution)/shard_map/jit(_take)/gather | solution.py:41
  16.7 2.8 collective-permute-start.3
  19.7 2.5 collective-permute-done.3
  22.2 3.7 %collective-permute-done.2 = bf16[3,1,3,32,192]{4,3,2,1,0:T(8,128)(2,1)S(1)} collective-permute-done((bf16[3,1,3,32,192]{4,3,2,1,0:T(8,128)(2,1)S(1)}, bf16[3,1,3,32,192]{4,3,2,1,0:T(8,128)(2,1)S(1)}, u32[]{:S(2)}, u32[]{:S(2)}) %collective-permute-start.2) | collective-permute-done | bytes 110624 | tf_op jit(solution)/shard_map/ppermute | solution.py:24
  26.0 5.3 %fusion.171 = f32[3,32,192]{2,1,0:T(8,128)S(1)} fusion(bf16[27,32,192,1]{2,1,0,3:T(8,128)(2,1)S(1)} %bitcast.511, f32[1,1,3,32,192]{4,3,2,1,0:T(8,128)S(1)} %copy-done, bf16[3,27,192,192]{3,2,1,0:T(8,128)(2,1)} %bitcast.478, pred[3,27]{1,0:T(4,128)(4,1)S(1)} %compare_and_fusion, pred[3,27]{1,0:T(4,128)(4,1)S(1)} %and_reduce_fusion), kind=kOutput, calls=%fused_computation.82 | convolution fusion | flops 197111808 | bytes 6451362 | tf_op jit(solution)/shard_map/kvj,tikj->tvi/dot_general | solution.py:71
  31.4 2.7 collective-permute-start.5
  35.8 3.2 collective-permute-done.4
  39.6 3.6 collective-permute-done.7
  43.2 2.4 collective-permute-done.6
  45.7 3.1 fusion.174
  54.5 3.6 collective-permute-done.11
  58.0 2.5 collective-permute-done.10
  60.6 3.1 fusion.177
  70.3 3.6 collective-permute-done.15
  73.8 2.4 collective-permute-done.14
  76.3 3.1 fusion.180
  85.8 3.6 collective-permute-done.19
  89.3 2.4 collective-permute-done.18
  91.8 3.1 fusion.183
  99.0 2.3 collective-permute-done.20
  101.9 3.6 collective-permute-done.23
  105.5 2.4 collective-permute-done.22
  107.9 3.1 fusion.186
  116.9 3.6 collective-permute-done.27
  120.4 2.4 collective-permute-done.26
  122.9 3.1 fusion.189
  132.5 3.6 collective-permute-done.31
  136.1 2.5 collective-permute-done.30
  138.7 3.1 fusion.192
  142.1 37.6 %psum.14 = f32[32,32]{0,1:T(8,128)S(1)} all-reduce(f32[32,32]{0,1:T(8,128)S(1)} %convolution_bitcast_fusion.3), channel_id=1, replica_groups=mesh['gx'=4,'gy'=8] {'gx','gy'}, use_global_device_ids=true, to_apply=%region_2.3 | all-reduce | flops 1024 | bytes 8192 | tf_op jit(solution)/shard_map/psum | solution.py:52
  179.7 2.9 cholesky.44
  184.0 2.4 custom-call.6
  186.9 3.3 collective-permute-start.33
  192.0 3.2 collective-permute-done.32
  198.0 3.9 %collective-permute-done.34 = bf16[3,1,3,32,192]{4,3,2,1,0:T(8,128)(2,1)S(1)} collective-permute-done((bf16[3,1,3,32,192]{4,3,2,1,0:T(8,128)(2,1)S(1)}, bf16[3,1,3,32,192]{4,3,2,1,0:T(8,128)(2,1)S(1)}, u32[]{:S(2)}, u32[]{:S(2)}) %collective-permute-start.34) | collective-permute-done | bytes 110624 | tf_op jit(solution)/shard_map/ppermute | solution.py:24
  202.0 5.3 %fusion.126 = f32[3,192,32]{1,2,0:T(8,128)S(1)} fusion(bf16[27,32,192,1]{2,1,0,3:T(8,128)(2,1)S(1)} %bitcast.513, f32[3,192,32]{1,2,0:T(8,128)S(1)} %fusion.229, bf16[3,27,192,192]{3,2,1,0:T(8,128)(2,1)} %bitcast.479, pred[3,27]{1,0:T(4,128)(4,1)S(1)} %compare_and_fusion, pred[3,27]{1,0:T(4,128)(4,1)S(1)} %and_reduce_fusion), kind=kOutput, calls=%fused_computation.67 | convolution fusion | flops 197111808 | bytes 6451362 | tf_op jit(solution)/shard_map/kvj,tikj->tvi/dot_general | solution.py:71
  209.4 2.4 collective-permute-done.37
  213.0 3.4 collective-permute-done.39
  216.4 2.6 collective-permute-done.38
  219.1 5.3 %fusion.195 = f32[3,192,32]{1,2,0:T(8,128)S(1)} fusion(bf16[27,32,192,1]{2,1,0,3:T(8,128)(2,1)S(1)} %bitcast.505, f32[3,192,32]{1,2,0:T(8,128)S(1)} %fusion.229, f32[3,192,32]{1,2,0:T(8,128)S(1)} %fusion.126, bf16[3,27,192,192]{3,2,1,0:T(8,128)(2,1)} %bitcast.480, pred[3,27]{1,0:T(4,128)(4,1)S(1)} %compare_and_fusion, pred[3,27]{1,0:T(4,128)(4,1)S(1)} %and_reduce_fusion), kind=kOutput, calls=%fused_computation.90 | convolution fusion | flops 197167104 | bytes 6525090 | tf_op jit(solution)/shard_map/kvj,tikj->tvi/dot_general | solution.py:71
  231.1 3.6 collective-permute-done.43
  234.6 2.4 collective-permute-done.42
  237.1 3.1 fusion.198
  244.4 2.8 collective-permute-done.44
  247.8 3.6 collective-permute-done.47
  251.3 2.4 collective-permute-done.46
  253.8 3.1 fusion.201
  263.0 3.6 collective-permute-done.51
  266.6 2.4 collective-permute-done.50
  269.1 3.1 fusion.204
  278.3 3.6 collective-permute-done.55
  281.9 2.4 collective-permute-done.54
  284.3 3.1 fusion.207
  293.9 3.6 collective-permute-done.59
  297.5 2.5 collective-permute-done.58
  300.1 3.1 fusion.210
  307.3 2.3 collective-permute-done.60
  310.2 3.6 collective-permute-done.63
  313.7 2.6 collective-permute-done.62
  316.4 3.1 fusion.213
  319.8 37.6 %psum.15 = f32[32,32]{0,1:T(8,128)S(1)} all-reduce(f32[32,32]{0,1:T(8,128)S(1)} %convolution_bitcast_fusion.1), channel_id=1, replica_groups=mesh['gx'=4,'gy'=8] {'gx','gy'}, use_global_device_ids=true, to_apply=%region_5.8 | all-reduce | flops 1024 | bytes 8192 | tf_op jit(solution)/shard_map/psum | solution.py:52
  357.4 2.9 cholesky.55
  361.7 2.4 custom-call.7
  (171 shorter events, 90.0 us)
Async XLA Ops:
  0.9 15.8 %collective-permute-start.1 = (bf16[1,1,3,32,192]{4,3,2,1,0:T(8,128)(2,1)S(1)}, bf16[1,1,3,32,192]{4,3,2,1,0:T(8,128)(2,1)S(1)}, u32[]{:S(2)}, u32[]{:S(2)}) collective-permute-start(bf16[1,1,3,32,192]{4,3,2,1,0:T(8,128)(2,1)S(1)} %convert_element_type.61), channel_id=1, source_target_pairs={{8,0},{16,8},{24,16},{0,24},{9,1},{17,9},{25,17},{1,25},{10,2},{18... | collective-permute-start | bytes 110600 | tf_op jit(solution)/shard_map/ppermute | solution.py:26
  4.8 11.9 %collective-permute-start = (bf16[1,1,3,32,192]{4,3,2,1,0:T(8,128)(2,1)S(1)}, bf16[1,1,3,32,192]{4,3,2,1,0:T(8,128)(2,1)S(1)}, u32[]{:S(2)}, u32[]{:S(2)}) collective-permute-start(bf16[1,1,3,32,192]{4,3,2,1,0:T(8,128)(2,1)S(1)} %convert_element_type.61), channel_id=1, source_target_pairs={{0,8},{8,16},{16,24},{24,0},{1,9},{9,17},{17,25},{25,1},{2,10},{10... | collective-permute-start | bytes 110600 | tf_op jit(solution)/shard_map/ppermute | solution.py:24
  16.7 5.5 %collective-permute-start.3 = (bf16[3,1,3,32,192]{4,3,2,1,0:T(8,128)(2,1)S(1)}, bf16[3,1,3,32,192]{4,3,2,1,0:T(8,128)(2,1)S(1)}, u32[]{:S(2)}, u32[]{:S(2)}) collective-permute-start(bf16[3,1,3,32,192]{4,3,2,1,0:T(8,128)(2,1)S(1)} %pad_maximum_fusion.16), channel_id=1, source_target_pairs={{1,0},{2,1},{3,2},{4,3},{5,4},{6,5},{7,6},{0,7},{9,8},{10,9},{11,1... | collective-permute-start | bytes 331784 | tf_op jit(solution)/shard_map/ppermute | solution.py:26
  19.5 6.4 %collective-permute-start.2 = (bf16[3,1,3,32,192]{4,3,2,1,0:T(8,128)(2,1)S(1)}, bf16[3,1,3,32,192]{4,3,2,1,0:T(8,128)(2,1)S(1)}, u32[]{:S(2)}, u32[]{:S(2)}) collective-permute-start(bf16[3,1,3,32,192]{4,3,2,1,0:T(8,128)(2,1)S(1)} %pad_maximum_fusion.16), channel_id=1, source_target_pairs={{0,1},{1,2},{2,3},{3,4},{4,5},{5,6},{6,7},{7,0},{8,9},{9,10},{10,1... | collective-permute-start | bytes 331784 | tf_op jit(solution)/shard_map/ppermute | solution.py:24
  31.4 4.4 %collective-permute-start.5 = (bf16[1,1,3,32,192]{4,3,2,1,0:T(8,128)(2,1)S(1)}, bf16[1,1,3,32,192]{4,3,2,1,0:T(8,128)(2,1)S(1)}, u32[]{:S(2)}, u32[]{:S(2)}) collective-permute-start(bf16[1,1,3,32,192]{4,3,2,1,0:T(8,128)(2,1)S(1)} %fusion.217), channel_id=1, source_target_pairs={{8,0},{16,8},{24,16},{0,24},{9,1},{17,9},{25,17},{1,25},{10,2},{18... | collective-permute-start | bytes 110600 | tf_op jit(solution)/shard_map/ppermute | solution.py:26
  34.0 5.0 %collective-permute-start.4 = (bf16[1,1,3,32,192]{4,3,2,1,0:T(8,128)(2,1)S(1)}, bf16[1,1,3,32,192]{4,3,2,1,0:T(8,128)(2,1)S(1)}, u32[]{:S(2)}, u32[]{:S(2)}) collective-permute-start(bf16[1,1,3,32,192]{4,3,2,1,0:T(8,128)(2,1)S(1)} %fusion.217), channel_id=1, source_target_pairs={{0,8},{8,16},{16,24},{24,0},{1,9},{9,17},{17,25},{25,1},{2,10},{10... | collective-permute-start | bytes 110600 | tf_op jit(solution)/shard_map/ppermute | solution.py:24
  39.1 4.1 %collective-permute-start.7 = (bf16[3,1,3,32,192]{4,3,2,1,0:T(8,128)(2,1)S(1)}, bf16[3,1,3,32,192]{4,3,2,1,0:T(8,128)(2,1)S(1)}, u32[]{:S(2)}, u32[]{:S(2)}) collective-permute-start(bf16[3,1,3,32,192]{4,3,2,1,0:T(8,128)(2,1)S(1)} %pad_maximum_fusion.17), channel_id=1, source_target_pairs={{1,0},{2,1},{3,2},{4,3},{5,4},{6,5},{7,6},{0,7},{9,8},{10,9},{11,1... | collective-permute-start | bytes 331784 | tf_op jit(solution)/shard_map/ppermute | solution.py:26
  39.1 6.4 %collective-permute-start.6 = (bf16[3,1,3,32,192]{4,3,2,1,0:T(8,128)(2,1)S(1)}, bf16[3,1,3,32,192]{4,3,2,1,0:T(8,128)(2,1)S(1)}, u32[]{:S(2)}, u32[]{:S(2)}) collective-permute-start(bf16[3,1,3,32,192]{4,3,2,1,0:T(8,128)(2,1)S(1)} %pad_maximum_fusion.17), channel_id=1, source_target_pairs={{0,1},{1,2},{2,3},{3,4},{4,5},{5,6},{6,7},{7,0},{8,9},{9,10},{10,1... | collective-permute-start | bytes 331784 | tf_op jit(solution)/shard_map/ppermute | solution.py:24
  48.8 4.1 %collective-permute-start.9 = (bf16[1,1,3,32,192]{4,3,2,1,0:T(8,128)(2,1)S(1)}, bf16[1,1,3,32,192]{4,3,2,1,0:T(8,128)(2,1)S(1)}, u32[]{:S(2)}, u32[]{:S(2)}) collective-permute-start(bf16[1,1,3,32,192]{4,3,2,1,0:T(8,128)(2,1)S(1)} %convert_bitcast_fusion.11), channel_id=1, source_target_pairs={{8,0},{16,8},{24,16},{0,24},{9,1},{17,9},{25,17},{1,25},{10,2},{18... | collective-permute-start | bytes 110600 | tf_op jit(solution)/shard_map/ppermute | solution.py:26
  48.8 5.0 %collective-permute-start.8 = (bf16[1,1,3,32,192]{4,3,2,1,0:T(8,128)(2,1)S(1)}, bf16[1,1,3,32,192]{4,3,2,1,0:T(8,128)(2,1)S(1)}, u32[]{:S(2)}, u32[]{:S(2)}) collective-permute-start(bf16[1,1,3,32,192]{4,3,2,1,0:T(8,128)(2,1)S(1)} %convert_bitcast_fusion.11), channel_id=1, source_target_pairs={{0,8},{8,16},{16,24},{24,0},{1,9},{9,17},{17,25},{25,1},{2,10},{10... | collective-permute-start | bytes 110600 | tf_op jit(solution)/shard_map/ppermute | solution.py:24
  53.9 4.1 %collective-permute-start.11 = (bf16[3,1,3,32,192]{4,3,2,1,0:T(8,128)(2,1)S(1)}, bf16[3,1,3,32,192]{4,3,2,1,0:T(8,128)(2,1)S(1)}, u32[]{:S(2)}, u32[]{:S(2)}) collective-permute-start(bf16[3,1,3,32,192]{4,3,2,1,0:T(8,128)(2,1)S(1)} %pad_maximum_fusion.18), channel_id=1, source_target_pairs={{1,0},{2,1},{3,2},{4,3},{5,4},{6,5},{7,6},{0,7},{9,8},{10,9},{11,1... | collective-permute-start | bytes 331784 | tf_op jit(solution)/shard_map/ppermute | solution.py:26
  54.2 6.4 %collective-permute-start.10 = (bf16[3,1,3,32,192]{4,3,2,1,0:T(8,128)(2,1)S(1)}, bf16[3,1,3,32,192]{4,3,2,1,0:T(8,128)(2,1)S(1)}, u32[]{:S(2)}, u32[]{:S(2)}) collective-permute-start(bf16[3,1,3,32,192]{4,3,2,1,0:T(8,128)(2,1)S(1)} %pad_maximum_fusion.18), channel_id=1, source_target_pairs={{0,1},{1,2},{2,3},{3,4},{4,5},{5,6},{6,7},{7,0},{8,9},{9,10},{10,1... | collective-permute-start | bytes 331784 | tf_op jit(solution)/shard_map/ppermute | solution.py:24
  63.8 4.1 %collective-permute-start.13 = (bf16[1,1,3,32,192]{4,3,2,1,0:T(8,128)(2,1)S(1)}, bf16[1,1,3,32,192]{4,3,2,1,0:T(8,128)(2,1)S(1)}, u32[]{:S(2)}, u32[]{:S(2)}) collective-permute-start(bf16[1,1,3,32,192]{4,3,2,1,0:T(8,128)(2,1)S(1)} %convert_bitcast_fusion.10), channel_id=1, source_target_pairs={{8,0},{16,8},{24,16},{0,24},{9,1},{17,9},{25,17},{1,25},{10,2},{18... | collective-permute-start | bytes 110600 | tf_op jit(solution)/shard_map/ppermute | solution.py:26
  64.7 5.0 %collective-permute-start.12 = (bf16[1,1,3,32,192]{4,3,2,1,0:T(8,128)(2,1)S(1)}, bf16[1,1,3,32,192]{4,3,2,1,0:T(8,128)(2,1)S(1)}, u32[]{:S(2)}, u32[]{:S(2)}) collective-permute-start(bf16[1,1,3,32,192]{4,3,2,1,0:T(8,128)(2,1)S(1)} %convert_bitcast_fusion.10), channel_id=1, source_target_pairs={{0,8},{8,16},{16,24},{24,0},{1,9},{9,17},{17,25},{25,1},{2,10},{10... | collective-permute-start | bytes 110600 | tf_op jit(solution)/shard_map/ppermute | solution.py:24
  69.7 4.1 %collective-permute-start.15 = (bf16[3,1,3,32,192]{4,3,2,1,0:T(8,128)(2,1)S(1)}, bf16[3,1,3,32,192]{4,3,2,1,0:T(8,128)(2,1)S(1)}, u32[]{:S(2)}, u32[]{:S(2)}) collective-permute-start(bf16[3,1,3,32,192]{4,3,2,1,0:T(8,128)(2,1)S(1)} %pad_maximum_fusion.19), channel_id=1, source_target_pairs={{1,0},{2,1},{3,2},{4,3},{5,4},{6,5},{7,6},{0,7},{9,8},{10,9},{11,1... | collective-permute-start | bytes 331784 | tf_op jit(solution)/shard_map/ppermute | solution.py:26
  69.8 6.4 %collective-permute-start.14 = (bf16[3,1,3,32,192]{4,3,2,1,0:T(8,128)(2,1)S(1)}, bf16[3,1,3,32,192]{4,3,2,1,0:T(8,128)(2,1)S(1)}, u32[]{:S(2)}, u32[]{:S(2)}) collective-permute-start(bf16[3,1,3,32,192]{4,3,2,1,0:T(8,128)(2,1)S(1)} %pad_maximum_fusion.19), channel_id=1, source_target_pairs={{0,1},{1,2},{2,3},{3,4},{4,5},{5,6},{6,7},{7,0},{8,9},{9,10},{10,1... | collective-permute-start | bytes 331784 | tf_op jit(solution)/shard_map/ppermute | solution.py:24
  79.4 4.1 %collective-permute-start.17 = (bf16[1,1,3,32,192]{4,3,2,1,0:T(8,128)(2,1)S(1)}, bf16[1,1,3,32,192]{4,3,2,1,0:T(8,128)(2,1)S(1)}, u32[]{:S(2)}, u32[]{:S(2)}) collective-permute-start(bf16[1,1,3,32,192]{4,3,2,1,0:T(8,128)(2,1)S(1)} %convert_bitcast_fusion.9), channel_id=1, source_target_pairs={{8,0},{16,8},{24,16},{0,24},{9,1},{17,9},{25,17},{1,25},{10,2},{18... | collective-permute-start | bytes 110600 | tf_op jit(solution)/shard_map/ppermute | solution.py:26
  80.2 5.0 %collective-permute-start.16 = (bf16[1,1,3,32,192]{4,3,2,1,0:T(8,128)(2,1)S(1)}, bf16[1,1,3,32,192]{4,3,2,1,0:T(8,128)(2,1)S(1)}, u32[]{:S(2)}, u32[]{:S(2)}) collective-permute-start(bf16[1,1,3,32,192]{4,3,2,1,0:T(8,128)(2,1)S(1)} %convert_bitcast_fusion.9), channel_id=1, source_target_pairs={{0,8},{8,16},{16,24},{24,0},{1,9},{9,17},{17,25},{25,1},{2,10},{10... | collective-permute-start | bytes 110600 | tf_op jit(solution)/shard_map/ppermute | solution.py:24
  85.2 4.1 %collective-permute-start.19 = (bf16[3,1,3,32,192]{4,3,2,1,0:T(8,128)(2,1)S(1)}, bf16[3,1,3,32,192]{4,3,2,1,0:T(8,128)(2,1)S(1)}, u32[]{:S(2)}, u32[]{:S(2)}) collective-permute-start(bf16[3,1,3,32,192]{4,3,2,1,0:T(8,128)(2,1)S(1)} %pad_maximum_fusion.20), channel_id=1, source_target_pairs={{1,0},{2,1},{3,2},{4,3},{5,4},{6,5},{7,6},{0,7},{9,8},{10,9},{11,1... | collective-permute-start | bytes 331784 | tf_op jit(solution)/shard_map/ppermute | solution.py:26
  85.3 6.4 %collective-permute-start.18 = (bf16[3,1,3,32,192]{4,3,2,1,0:T(8,128)(2,1)S(1)}, bf16[3,1,3,32,192]{4,3,2,1,0:T(8,128)(2,1)S(1)}, u32[]{:S(2)}, u32[]{:S(2)}) collective-permute-start(bf16[3,1,3,32,192]{4,3,2,1,0:T(8,128)(2,1)S(1)} %pad_maximum_fusion.20), channel_id=1, source_target_pairs={{0,1},{1,2},{2,3},{3,4},{4,5},{5,6},{6,7},{7,0},{8,9},{9,10},{10,1... | collective-permute-start | bytes 331784 | tf_op jit(solution)/shard_map/ppermute | solution.py:24
  94.9 4.1 %collective-permute-start.21 = (bf16[1,1,3,32,192]{4,3,2,1,0:T(8,128)(2,1)S(1)}, bf16[1,1,3,32,192]{4,3,2,1,0:T(8,128)(2,1)S(1)}, u32[]{:S(2)}, u32[]{:S(2)}) collective-permute-start(bf16[1,1,3,32,192]{4,3,2,1,0:T(8,128)(2,1)S(1)} %convert_bitcast_fusion.8), channel_id=1, source_target_pairs={{8,0},{16,8},{24,16},{0,24},{9,1},{17,9},{25,17},{1,25},{10,2},{18... | collective-permute-start | bytes 110600 | tf_op jit(solution)/shard_map/ppermute | solution.py:26
  96.3 5.0 %collective-permute-start.20 = (bf16[1,1,3,32,192]{4,3,2,1,0:T(8,128)(2,1)S(1)}, bf16[1,1,3,32,192]{4,3,2,1,0:T(8,128)(2,1)S(1)}, u32[]{:S(2)}, u32[]{:S(2)}) collective-permute-start(bf16[1,1,3,32,192]{4,3,2,1,0:T(8,128)(2,1)S(1)} %convert_bitcast_fusion.8), channel_id=1, source_target_pairs={{0,8},{8,16},{16,24},{24,0},{1,9},{9,17},{17,25},{25,1},{2,10},{10... | collective-permute-start | bytes 110600 | tf_op jit(solution)/shard_map/ppermute | solution.py:24
  101.3 4.1 %collective-permute-start.23 = (bf16[3,1,3,32,192]{4,3,2,1,0:T(8,128)(2,1)S(1)}, bf16[3,1,3,32,192]{4,3,2,1,0:T(8,128)(2,1)S(1)}, u32[]{:S(2)}, u32[]{:S(2)}) collective-permute-start(bf16[3,1,3,32,192]{4,3,2,1,0:T(8,128)(2,1)S(1)} %pad_maximum_fusion.21), channel_id=1, source_target_pairs={{1,0},{2,1},{3,2},{4,3},{5,4},{6,5},{7,6},{0,7},{9,8},{10,9},{11,1... | collective-permute-start | bytes 331784 | tf_op jit(solution)/shard_map/ppermute | solution.py:26
  101.4 6.4 %collective-permute-start.22 = (bf16[3,1,3,32,192]{4,3,2,1,0:T(8,128)(2,1)S(1)}, bf16[3,1,3,32,192]{4,3,2,1,0:T(8,128)(2,1)S(1)}, u32[]{:S(2)}, u32[]{:S(2)}) collective-permute-start(bf16[3,1,3,32,192]{4,3,2,1,0:T(8,128)(2,1)S(1)} %pad_maximum_fusion.21), channel_id=1, source_target_pairs={{0,1},{1,2},{2,3},{3,4},{4,5},{5,6},{6,7},{7,0},{8,9},{9,10},{10,1... | collective-permute-start | bytes 331784 | tf_op jit(solution)/shard_map/ppermute | solution.py:24
  111.0 4.1 %collective-permute-start.25 = (bf16[1,1,3,32,192]{4,3,2,1,0:T(8,128)(2,1)S(1)}, bf16[1,1,3,32,192]{4,3,2,1,0:T(8,128)(2,1)S(1)}, u32[]{:S(2)}, u32[]{:S(2)}) collective-permute-start(bf16[1,1,3,32,192]{4,3,2,1,0:T(8,128)(2,1)S(1)} %convert_bitcast_fusion.7), channel_id=1, source_target_pairs={{8,0},{16,8},{24,16},{0,24},{9,1},{17,9},{25,17},{1,25},{10,2},{18... | collective-permute-start | bytes 110600 | tf_op jit(solution)/shard_map/ppermute | solution.py:26
  111.3 5.0 %collective-permute-start.24 = (bf16[1,1,3,32,192]{4,3,2,1,0:T(8,128)(2,1)S(1)}, bf16[1,1,3,32,192]{4,3,2,1,0:T(8,128)(2,1)S(1)}, u32[]{:S(2)}, u32[]{:S(2)}) collective-permute-start(bf16[1,1,3,32,192]{4,3,2,1,0:T(8,128)(2,1)S(1)} %convert_bitcast_fusion.7), channel_id=1, source_target_pairs={{0,8},{8,16},{16,24},{24,0},{1,9},{9,17},{17,25},{25,1},{2,10},{10... | collective-permute-start | bytes 110600 | tf_op jit(solution)/shard_map/ppermute | solution.py:24
  116.3 4.1 %collective-permute-start.27 = (bf16[3,1,3,32,192]{4,3,2,1,0:T(8,128)(2,1)S(1)}, bf16[3,1,3,32,192]{4,3,2,1,0:T(8,128)(2,1)S(1)}, u32[]{:S(2)}, u32[]{:S(2)}) collective-permute-start(bf16[3,1,3,32,192]{4,3,2,1,0:T(8,128)(2,1)S(1)} %pad_maximum_fusion.22), channel_id=1, source_target_pairs={{1,0},{2,1},{3,2},{4,3},{5,4},{6,5},{7,6},{0,7},{9,8},{10,9},{11,1... | collective-permute-start | bytes 331784 | tf_op jit(solution)/shard_map/ppermute | solution.py:26
  116.4 6.4 %collective-permute-start.26 = (bf16[3,1,3,32,192]{4,3,2,1,0:T(8,128)(2,1)S(1)}, bf16[3,1,3,32,192]{4,3,2,1,0:T(8,128)(2,1)S(1)}, u32[]{:S(2)}, u32[]{:S(2)}) collective-permute-start(bf16[3,1,3,32,192]{4,3,2,1,0:T(8,128)(2,1)S(1)} %pad_maximum_fusion.22), channel_id=1, source_target_pairs={{0,1},{1,2},{2,3},{3,4},{4,5},{5,6},{6,7},{7,0},{8,9},{9,10},{10,1... | collective-permute-start | bytes 331784 | tf_op jit(solution)/shard_map/ppermute | solution.py:24
  126.0 4.1 %collective-permute-start.29 = (bf16[1,1,3,32,192]{4,3,2,1,0:T(8,128)(2,1)S(1)}, bf16[1,1,3,32,192]{4,3,2,1,0:T(8,128)(2,1)S(1)}, u32[]{:S(2)}, u32[]{:S(2)}) collective-permute-start(bf16[1,1,3,32,192]{4,3,2,1,0:T(8,128)(2,1)S(1)} %convert_bitcast_fusion.6), channel_id=1, source_target_pairs={{8,0},{16,8},{24,16},{0,24},{9,1},{17,9},{25,17},{1,25},{10,2},{18... | collective-permute-start | bytes 110600 | tf_op jit(solution)/shard_map/ppermute | solution.py:26
  126.9 5.0 %collective-permute-start.28 = (bf16[1,1,3,32,192]{4,3,2,1,0:T(8,128)(2,1)S(1)}, bf16[1,1,3,32,192]{4,3,2,1,0:T(8,128)(2,1)S(1)}, u32[]{:S(2)}, u32[]{:S(2)}) collective-permute-start(bf16[1,1,3,32,192]{4,3,2,1,0:T(8,128)(2,1)S(1)} %convert_bitcast_fusion.6), channel_id=1, source_target_pairs={{0,8},{8,16},{16,24},{24,0},{1,9},{9,17},{17,25},{25,1},{2,10},{10... | collective-permute-start | bytes 110600 | tf_op jit(solution)/shard_map/ppermute | solution.py:24
  132.0 4.1 %collective-permute-start.31 = (bf16[3,1,3,32,192]{4,3,2,1,0:T(8,128)(2,1)S(1)}, bf16[3,1,3,32,192]{4,3,2,1,0:T(8,128)(2,1)S(1)}, u32[]{:S(2)}, u32[]{:S(2)}) collective-permute-start(bf16[3,1,3,32,192]{4,3,2,1,0:T(8,128)(2,1)S(1)} %pad_maximum_fusion.23), channel_id=1, source_target_pairs={{1,0},{2,1},{3,2},{4,3},{5,4},{6,5},{7,6},{0,7},{9,8},{10,9},{11,1... | collective-permute-start | bytes 331784 | tf_op jit(solution)/shard_map/ppermute | solution.py:26
  132.0 6.6 %collective-permute-start.30 = (bf16[3,1,3,32,192]{4,3,2,1,0:T(8,128)(2,1)S(1)}, bf16[3,1,3,32,192]{4,3,2,1,0:T(8,128)(2,1)S(1)}, u32[]{:S(2)}, u32[]{:S(2)}) collective-permute-start(bf16[3,1,3,32,192]{4,3,2,1,0:T(8,128)(2,1)S(1)} %pad_maximum_fusion.23), channel_id=1, source_target_pairs={{0,1},{1,2},{2,3},{3,4},{4,5},{5,6},{6,7},{7,0},{8,9},{9,10},{10,1... | collective-permute-start | bytes 331784 | tf_op jit(solution)/shard_map/ppermute | solution.py:24
  186.9 5.1 %collective-permute-start.33 = (bf16[1,1,3,32,192]{4,3,2,1,0:T(8,128)(2,1)S(1)}, bf16[1,1,3,32,192]{4,3,2,1,0:T(8,128)(2,1)S(1)}, u32[]{:S(2)}, u32[]{:S(2)}) collective-permute-start(bf16[1,1,3,32,192]{4,3,2,1,0:T(8,128)(2,1)S(1)} %fusion.218), channel_id=1, source_target_pairs={{8,0},{16,8},{24,16},{0,24},{9,1},{17,9},{25,17},{1,25},{10,2},{18... | collective-permute-start | bytes 110600 | tf_op jit(solution)/shard_map/ppermute | solution.py:26
  190.2 5.0 %collective-permute-start.32 = (bf16[1,1,3,32,192]{4,3,2,1,0:T(8,128)(2,1)S(1)}, bf16[1,1,3,32,192]{4,3,2,1,0:T(8,128)(2,1)S(1)}, u32[]{:S(2)}, u32[]{:S(2)}) collective-permute-start(bf16[1,1,3,32,192]{4,3,2,1,0:T(8,128)(2,1)S(1)} %fusion.218), channel_id=1, source_target_pairs={{0,8},{8,16},{16,24},{24,0},{1,9},{9,17},{17,25},{25,1},{2,10},{10... | collective-permute-start | bytes 110600 | tf_op jit(solution)/shard_map/ppermute | solution.py:24
  195.3 2.7 collective-permute-start.35
  195.3 6.6 %collective-permute-start.34 = (bf16[3,1,3,32,192]{4,3,2,1,0:T(8,128)(2,1)S(1)}, bf16[3,1,3,32,192]{4,3,2,1,0:T(8,128)(2,1)S(1)}, u32[]{:S(2)}, u32[]{:S(2)}) collective-permute-start(bf16[3,1,3,32,192]{4,3,2,1,0:T(8,128)(2,1)S(1)} %pad_maximum_fusion.24), channel_id=1, source_target_pairs={{0,1},{1,2},{2,3},{3,4},{4,5},{5,6},{6,7},{7,0},{8,9},{9,10},{10,1... | collective-permute-start | bytes 331784 | tf_op jit(solution)/shard_map/ppermute | solution.py:24
  207.3 4.4 %collective-permute-start.37 = (bf16[1,1,3,32,192]{4,3,2,1,0:T(8,128)(2,1)S(1)}, bf16[1,1,3,32,192]{4,3,2,1,0:T(8,128)(2,1)S(1)}, u32[]{:S(2)}, u32[]{:S(2)}) collective-permute-start(bf16[1,1,3,32,192]{4,3,2,1,0:T(8,128)(2,1)S(1)} %fusion.219), channel_id=1, source_target_pairs={{8,0},{16,8},{24,16},{0,24},{9,1},{17,9},{25,17},{1,25},{10,2},{18... | collective-permute-start | bytes 110600 | tf_op jit(solution)/shard_map/ppermute | solution.py:26
  207.4 5.0 %collective-permute-start.36 = (bf16[1,1,3,32,192]{4,3,2,1,0:T(8,128)(2,1)S(1)}, bf16[1,1,3,32,192]{4,3,2,1,0:T(8,128)(2,1)S(1)}, u32[]{:S(2)}, u32[]{:S(2)}) collective-permute-start(bf16[1,1,3,32,192]{4,3,2,1,0:T(8,128)(2,1)S(1)} %fusion.219), channel_id=1, source_target_pairs={{0,8},{8,16},{16,24},{24,0},{1,9},{9,17},{17,25},{25,1},{2,10},{10... | collective-permute-start | bytes 110600 | tf_op jit(solution)/shard_map/ppermute | solution.py:24
  212.5 4.0 %collective-permute-start.39 = (bf16[3,1,3,32,192]{4,3,2,1,0:T(8,128)(2,1)S(1)}, bf16[3,1,3,32,192]{4,3,2,1,0:T(8,128)(2,1)S(1)}, u32[]{:S(2)}, u32[]{:S(2)}) collective-permute-start(bf16[3,1,3,32,192]{4,3,2,1,0:T(8,128)(2,1)S(1)} %pad_maximum_fusion.25), channel_id=1, source_target_pairs={{1,0},{2,1},{3,2},{4,3},{5,4},{6,5},{7,6},{0,7},{9,8},{10,9},{11,1... | collective-permute-start | bytes 331784 | tf_op jit(solution)/shard_map/ppermute | solution.py:26
  212.5 6.5 %collective-permute-start.38 = (bf16[3,1,3,32,192]{4,3,2,1,0:T(8,128)(2,1)S(1)}, bf16[3,1,3,32,192]{4,3,2,1,0:T(8,128)(2,1)S(1)}, u32[]{:S(2)}, u32[]{:S(2)}) collective-permute-start(bf16[3,1,3,32,192]{4,3,2,1,0:T(8,128)(2,1)S(1)} %pad_maximum_fusion.25), channel_id=1, source_target_pairs={{0,1},{1,2},{2,3},{3,4},{4,5},{5,6},{6,7},{7,0},{8,9},{9,10},{10,1... | collective-permute-start | bytes 331784 | tf_op jit(solution)/shard_map/ppermute | solution.py:24
  224.5 4.1 %collective-permute-start.41 = (bf16[1,1,3,32,192]{4,3,2,1,0:T(8,128)(2,1)S(1)}, bf16[1,1,3,32,192]{4,3,2,1,0:T(8,128)(2,1)S(1)}, u32[]{:S(2)}, u32[]{:S(2)}) collective-permute-start(bf16[1,1,3,32,192]{4,3,2,1,0:T(8,128)(2,1)S(1)} %convert_bitcast_fusion.2), channel_id=1, source_target_pairs={{8,0},{16,8},{24,16},{0,24},{9,1},{17,9},{25,17},{1,25},{10,2},{18... | collective-permute-start | bytes 110600 | tf_op jit(solution)/shard_map/ppermute | solution.py:26
  225.5 5.0 %collective-permute-start.40 = (bf16[1,1,3,32,192]{4,3,2,1,0:T(8,128)(2,1)S(1)}, bf16[1,1,3,32,192]{4,3,2,1,0:T(8,128)(2,1)S(1)}, u32[]{:S(2)}, u32[]{:S(2)}) collective-permute-start(bf16[1,1,3,32,192]{4,3,2,1,0:T(8,128)(2,1)S(1)} %convert_bitcast_fusion.2), channel_id=1, source_target_pairs={{0,8},{8,16},{16,24},{24,0},{1,9},{9,17},{17,25},{25,1},{2,10},{10... | collective-permute-start | bytes 110600 | tf_op jit(solution)/shard_map/ppermute | solution.py:24
  230.5 4.1 %collective-permute-start.43 = (bf16[3,1,3,32,192]{4,3,2,1,0:T(8,128)(2,1)S(1)}, bf16[3,1,3,32,192]{4,3,2,1,0:T(8,128)(2,1)S(1)}, u32[]{:S(2)}, u32[]{:S(2)}) collective-permute-start(bf16[3,1,3,32,192]{4,3,2,1,0:T(8,128)(2,1)S(1)} %pad_maximum_fusion.26), channel_id=1, source_target_pairs={{1,0},{2,1},{3,2},{4,3},{5,4},{6,5},{7,6},{0,7},{9,8},{10,9},{11,1... | collective-permute-start | bytes 331784 | tf_op jit(solution)/shard_map/ppermute | solution.py:26
  230.6 6.4 %collective-permute-start.42 = (bf16[3,1,3,32,192]{4,3,2,1,0:T(8,128)(2,1)S(1)}, bf16[3,1,3,32,192]{4,3,2,1,0:T(8,128)(2,1)S(1)}, u32[]{:S(2)}, u32[]{:S(2)}) collective-permute-start(bf16[3,1,3,32,192]{4,3,2,1,0:T(8,128)(2,1)S(1)} %pad_maximum_fusion.26), channel_id=1, source_target_pairs={{0,1},{1,2},{2,3},{3,4},{4,5},{5,6},{6,7},{7,0},{8,9},{9,10},{10,1... | collective-permute-start | bytes 331784 | tf_op jit(solution)/shard_map/ppermute | solution.py:24
  240.2 4.1 %collective-permute-start.45 = (bf16[1,1,3,32,192]{4,3,2,1,0:T(8,128)(2,1)S(1)}, bf16[1,1,3,32,192]{4,3,2,1,0:T(8,128)(2,1)S(1)}, u32[]{:S(2)}, u32[]{:S(2)}) collective-permute-start(bf16[1,1,3,32,192]{4,3,2,1,0:T(8,128)(2,1)S(1)} %convert_bitcast_fusion.1), channel_id=1, source_target_pairs={{8,0},{16,8},{24,16},{0,24},{9,1},{17,9},{25,17},{1,25},{10,2},{18... | collective-permute-start | bytes 110600 | tf_op jit(solution)/shard_map/ppermute | solution.py:26
  242.2 5.0 %collective-permute-start.44 = (bf16[1,1,3,32,192]{4,3,2,1,0:T(8,128)(2,1)S(1)}, bf16[1,1,3,32,192]{4,3,2,1,0:T(8,128)(2,1)S(1)}, u32[]{:S(2)}, u32[]{:S(2)}) collective-permute-start(bf16[1,1,3,32,192]{4,3,2,1,0:T(8,128)(2,1)S(1)} %convert_bitcast_fusion.1), channel_id=1, source_target_pairs={{0,8},{8,16},{16,24},{24,0},{1,9},{9,17},{17,25},{25,1},{2,10},{10... | collective-permute-start | bytes 110600 | tf_op jit(solution)/shard_map/ppermute | solution.py:24
  247.2 4.1 %collective-permute-start.47 = (bf16[3,1,3,32,192]{4,3,2,1,0:T(8,128)(2,1)S(1)}, bf16[3,1,3,32,192]{4,3,2,1,0:T(8,128)(2,1)S(1)}, u32[]{:S(2)}, u32[]{:S(2)}) collective-permute-start(bf16[3,1,3,32,192]{4,3,2,1,0:T(8,128)(2,1)S(1)} %pad_maximum_fusion.27), channel_id=1, source_target_pairs={{1,0},{2,1},{3,2},{4,3},{5,4},{6,5},{7,6},{0,7},{9,8},{10,9},{11,1... | collective-permute-start | bytes 331784 | tf_op jit(solution)/shard_map/ppermute | solution.py:26
  247.3 6.4 %collective-permute-start.46 = (bf16[3,1,3,32,192]{4,3,2,1,0:T(8,128)(2,1)S(1)}, bf16[3,1,3,32,192]{4,3,2,1,0:T(8,128)(2,1)S(1)}, u32[]{:S(2)}, u32[]{:S(2)}) collective-permute-start(bf16[3,1,3,32,192]{4,3,2,1,0:T(8,128)(2,1)S(1)} %pad_maximum_fusion.27), channel_id=1, source_target_pairs={{0,1},{1,2},{2,3},{3,4},{4,5},{5,6},{6,7},{7,0},{8,9},{9,10},{10,1... | collective-permute-start | bytes 331784 | tf_op jit(solution)/shard_map/ppermute | solution.py:24
  256.9 4.1 %collective-permute-start.49 = (bf16[1,1,3,32,192]{4,3,2,1,0:T(8,128)(2,1)S(1)}, bf16[1,1,3,32,192]{4,3,2,1,0:T(8,128)(2,1)S(1)}, u32[]{:S(2)}, u32[]{:S(2)}) collective-permute-start(bf16[1,1,3,32,192]{4,3,2,1,0:T(8,128)(2,1)S(1)} %convert_bitcast_fusion), channel_id=1, source_target_pairs={{8,0},{16,8},{24,16},{0,24},{9,1},{17,9},{25,17},{1,25},{10,2},{18... | collective-permute-start | bytes 110600 | tf_op jit(solution)/shard_map/ppermute | solution.py:26
  257.5 5.0 %collective-permute-start.48 = (bf16[1,1,3,32,192]{4,3,2,1,0:T(8,128)(2,1)S(1)}, bf16[1,1,3,32,192]{4,3,2,1,0:T(8,128)(2,1)S(1)}, u32[]{:S(2)}, u32[]{:S(2)}) collective-permute-start(bf16[1,1,3,32,192]{4,3,2,1,0:T(8,128)(2,1)S(1)} %convert_bitcast_fusion), channel_id=1, source_target_pairs={{0,8},{8,16},{16,24},{24,0},{1,9},{9,17},{17,25},{25,1},{2,10},{10... | collective-permute-start | bytes 110600 | tf_op jit(solution)/shard_map/ppermute | solution.py:24
  262.5 4.1 %collective-permute-start.51 = (bf16[3,1,3,32,192]{4,3,2,1,0:T(8,128)(2,1)S(1)}, bf16[3,1,3,32,192]{4,3,2,1,0:T(8,128)(2,1)S(1)}, u32[]{:S(2)}, u32[]{:S(2)}) collective-permute-start(bf16[3,1,3,32,192]{4,3,2,1,0:T(8,128)(2,1)S(1)} %pad_maximum_fusion.28), channel_id=1, source_target_pairs={{1,0},{2,1},{3,2},{4,3},{5,4},{6,5},{7,6},{0,7},{9,8},{10,9},{11,1... | collective-permute-start | bytes 331784 | tf_op jit(solution)/shard_map/ppermute | solution.py:26
  262.5 6.4 %collective-permute-start.50 = (bf16[3,1,3,32,192]{4,3,2,1,0:T(8,128)(2,1)S(1)}, bf16[3,1,3,32,192]{4,3,2,1,0:T(8,128)(2,1)S(1)}, u32[]{:S(2)}, u32[]{:S(2)}) collective-permute-start(bf16[3,1,3,32,192]{4,3,2,1,0:T(8,128)(2,1)S(1)} %pad_maximum_fusion.28), channel_id=1, source_target_pairs={{0,1},{1,2},{2,3},{3,4},{4,5},{5,6},{6,7},{7,0},{8,9},{9,10},{10,1... | collective-permute-start | bytes 331784 | tf_op jit(solution)/shard_map/ppermute | solution.py:24
  272.2 4.1 %collective-permute-start.53 = (bf16[1,1,3,32,192]{4,3,2,1,0:T(8,128)(2,1)S(1)}, bf16[1,1,3,32,192]{4,3,2,1,0:T(8,128)(2,1)S(1)}, u32[]{:S(2)}, u32[]{:S(2)}) collective-permute-start(bf16[1,1,3,32,192]{4,3,2,1,0:T(8,128)(2,1)S(1)} %convert_bitcast_fusion.5), channel_id=1, source_target_pairs={{8,0},{16,8},{24,16},{0,24},{9,1},{17,9},{25,17},{1,25},{10,2},{18... | collective-permute-start | bytes 110600 | tf_op jit(solution)/shard_map/ppermute | solution.py:26
  272.7 5.0 %collective-permute-start.52 = (bf16[1,1,3,32,192]{4,3,2,1,0:T(8,128)(2,1)S(1)}, bf16[1,1,3,32,192]{4,3,2,1,0:T(8,128)(2,1)S(1)}, u32[]{:S(2)}, u32[]{:S(2)}) collective-permute-start(bf16[1,1,3,32,192]{4,3,2,1,0:T(8,128)(2,1)S(1)} %convert_bitcast_fusion.5), channel_id=1, source_target_pairs={{0,8},{8,16},{16,24},{24,0},{1,9},{9,17},{17,25},{25,1},{2,10},{10... | collective-permute-start | bytes 110600 | tf_op jit(solution)/shard_map/ppermute | solution.py:24
  277.7 4.1 %collective-permute-start.55 = (bf16[3,1,3,32,192]{4,3,2,1,0:T(8,128)(2,1)S(1)}, bf16[3,1,3,32,192]{4,3,2,1,0:T(8,128)(2,1)S(1)}, u32[]{:S(2)}, u32[]{:S(2)}) collective-permute-start(bf16[3,1,3,32,192]{4,3,2,1,0:T(8,128)(2,1)S(1)} %pad_maximum_fusion.29), channel_id=1, source_target_pairs={{1,0},{2,1},{3,2},{4,3},{5,4},{6,5},{7,6},{0,7},{9,8},{10,9},{11,1... | collective-permute-start | bytes 331784 | tf_op jit(solution)/shard_map/ppermute | solution.py:26
  277.8 6.4 %collective-permute-start.54 = (bf16[3,1,3,32,192]{4,3,2,1,0:T(8,128)(2,1)S(1)}, bf16[3,1,3,32,192]{4,3,2,1,0:T(8,128)(2,1)S(1)}, u32[]{:S(2)}, u32[]{:S(2)}) collective-permute-start(bf16[3,1,3,32,192]{4,3,2,1,0:T(8,128)(2,1)S(1)} %pad_maximum_fusion.29), channel_id=1, source_target_pairs={{0,1},{1,2},{2,3},{3,4},{4,5},{5,6},{6,7},{7,0},{8,9},{9,10},{10,1... | collective-permute-start | bytes 331784 | tf_op jit(solution)/shard_map/ppermute | solution.py:24
  287.4 4.1 %collective-permute-start.57 = (bf16[1,1,3,32,192]{4,3,2,1,0:T(8,128)(2,1)S(1)}, bf16[1,1,3,32,192]{4,3,2,1,0:T(8,128)(2,1)S(1)}, u32[]{:S(2)}, u32[]{:S(2)}) collective-permute-start(bf16[1,1,3,32,192]{4,3,2,1,0:T(8,128)(2,1)S(1)} %convert_bitcast_fusion.4), channel_id=1, source_target_pairs={{8,0},{16,8},{24,16},{0,24},{9,1},{17,9},{25,17},{1,25},{10,2},{18... | collective-permute-start | bytes 110600 | tf_op jit(solution)/shard_map/ppermute | solution.py:26
  288.3 5.0 %collective-permute-start.56 = (bf16[1,1,3,32,192]{4,3,2,1,0:T(8,128)(2,1)S(1)}, bf16[1,1,3,32,192]{4,3,2,1,0:T(8,128)(2,1)S(1)}, u32[]{:S(2)}, u32[]{:S(2)}) collective-permute-start(bf16[1,1,3,32,192]{4,3,2,1,0:T(8,128)(2,1)S(1)} %convert_bitcast_fusion.4), channel_id=1, source_target_pairs={{0,8},{8,16},{16,24},{24,0},{1,9},{9,17},{17,25},{25,1},{2,10},{10... | collective-permute-start | bytes 110600 | tf_op jit(solution)/shard_map/ppermute | solution.py:24
  293.3 4.1 %collective-permute-start.59 = (bf16[3,1,3,32,192]{4,3,2,1,0:T(8,128)(2,1)S(1)}, bf16[3,1,3,32,192]{4,3,2,1,0:T(8,128)(2,1)S(1)}, u32[]{:S(2)}, u32[]{:S(2)}) collective-permute-start(bf16[3,1,3,32,192]{4,3,2,1,0:T(8,128)(2,1)S(1)} %pad_maximum_fusion.30), channel_id=1, source_target_pairs={{1,0},{2,1},{3,2},{4,3},{5,4},{6,5},{7,6},{0,7},{9,8},{10,9},{11,1... | collective-permute-start | bytes 331784 | tf_op jit(solution)/shard_map/ppermute | solution.py:26
  293.6 6.4 %collective-permute-start.58 = (bf16[3,1,3,32,192]{4,3,2,1,0:T(8,128)(2,1)S(1)}, bf16[3,1,3,32,192]{4,3,2,1,0:T(8,128)(2,1)S(1)}, u32[]{:S(2)}, u32[]{:S(2)}) collective-permute-start(bf16[3,1,3,32,192]{4,3,2,1,0:T(8,128)(2,1)S(1)} %pad_maximum_fusion.30), channel_id=1, source_target_pairs={{0,1},{1,2},{2,3},{3,4},{4,5},{5,6},{6,7},{7,0},{8,9},{9,10},{10,1... | collective-permute-start | bytes 331784 | tf_op jit(solution)/shard_map/ppermute | solution.py:24
  303.2 4.1 %collective-permute-start.61 = (bf16[1,1,3,32,192]{4,3,2,1,0:T(8,128)(2,1)S(1)}, bf16[1,1,3,32,192]{4,3,2,1,0:T(8,128)(2,1)S(1)}, u32[]{:S(2)}, u32[]{:S(2)}) collective-permute-start(bf16[1,1,3,32,192]{4,3,2,1,0:T(8,128)(2,1)S(1)} %convert_bitcast_fusion.3), channel_id=1, source_target_pairs={{8,0},{16,8},{24,16},{0,24},{9,1},{17,9},{25,17},{1,25},{10,2},{18... | collective-permute-start | bytes 110600 | tf_op jit(solution)/shard_map/ppermute | solution.py:26
  304.6 5.0 %collective-permute-start.60 = (bf16[1,1,3,32,192]{4,3,2,1,0:T(8,128)(2,1)S(1)}, bf16[1,1,3,32,192]{4,3,2,1,0:T(8,128)(2,1)S(1)}, u32[]{:S(2)}, u32[]{:S(2)}) collective-permute-start(bf16[1,1,3,32,192]{4,3,2,1,0:T(8,128)(2,1)S(1)} %convert_bitcast_fusion.3), channel_id=1, source_target_pairs={{0,8},{8,16},{16,24},{24,0},{1,9},{9,17},{17,25},{25,1},{2,10},{10... | collective-permute-start | bytes 110600 | tf_op jit(solution)/shard_map/ppermute | solution.py:24
  309.6 4.1 %collective-permute-start.63 = (bf16[3,1,3,32,192]{4,3,2,1,0:T(8,128)(2,1)S(1)}, bf16[3,1,3,32,192]{4,3,2,1,0:T(8,128)(2,1)S(1)}, u32[]{:S(2)}, u32[]{:S(2)}) collective-permute-start(bf16[3,1,3,32,192]{4,3,2,1,0:T(8,128)(2,1)S(1)} %pad_maximum_fusion.31), channel_id=1, source_target_pairs={{1,0},{2,1},{3,2},{4,3},{5,4},{6,5},{7,6},{0,7},{9,8},{10,9},{11,1... | collective-permute-start | bytes 331784 | tf_op jit(solution)/shard_map/ppermute | solution.py:26
  309.7 6.6 %collective-permute-start.62 = (bf16[3,1,3,32,192]{4,3,2,1,0:T(8,128)(2,1)S(1)}, bf16[3,1,3,32,192]{4,3,2,1,0:T(8,128)(2,1)S(1)}, u32[]{:S(2)}, u32[]{:S(2)}) collective-permute-start(bf16[3,1,3,32,192]{4,3,2,1,0:T(8,128)(2,1)S(1)} %pad_maximum_fusion.31), channel_id=1, source_target_pairs={{0,1},{1,2},{2,3},{3,4},{4,5},{5,6},{6,7},{7,0},{8,9},{9,10},{10,1... | collective-permute-start | bytes 331784 | tf_op jit(solution)/shard_map/ppermute | solution.py:24
  (5 other events, 112.0 us)

commit v3 on v2

--- a/solution.py
+++ b/solution.py
@@ -45,11 +45,24 @@
     return jnp.transpose(blocks, (0, 2, 1, 3))
 
 
+def all_sum(value, axes):
+    for axis in axes:
+        count = lax.axis_size(axis)
+        if count & (count - 1):
+            value = lax.psum(value, axis)
+            continue
+        stride = 1
+        while stride < count:
+            value = value + lax.ppermute(value, axis, [(i, i ^ stride) for i in range(count)])
+            stride *= 2
+    return value
+
+
 def orthonormal(filtered, rows_total):
     partial_gram = jnp.einsum(
         "zvd,zwd->vw", filtered, filtered, precision=lax.Precision.HIGHEST
     )
-    gram_matrix = lax.psum(partial_gram, ("gx", "gy"))
+    gram_matrix = all_sum(partial_gram, ("gx", "gy"))
     factor = jnp.linalg.cholesky(gram_matrix)
     identity = jnp.eye(filtered.shape[1], dtype=jnp.float32)
     inverse = jax.scipy.linalg.solve_triangular(factor, identity, lower=True)

time: 366 us -> 321 us (0.88)
  blocking collectives: 75.1 us -> 0 us
  waiting for transfers between devices: 155 us -> 183 us
    psum x2 -> x0, blocking collectives: 75.1 us -> none  [orthonormal(): gram_matrix = lax.psum(partial_gram, ('gx', 'gy'))]
    ppermute x0 -> x10, waiting for transfers between devices: none -> 30.5 us  [all_sum(): lax.ppermute(value, axis, [(i, i ^ stride) for i in range(count)])]
    ppermute x32, waiting for transfers between devices: 69.7 us -> 65.7 us  [with_halo(): lax.ppermute(tail, axis, [(i, (i + 1) % count) for i in range(count)])]
  transfers between devices with their start and end apart: 64 -> 74, of which waited for: 62 -> 72; matrix products, arithmetic and copies ran while one was open for 3% -> 4% of each run, Pallas kernels for 0% -> 0%
where the time goes in v3:
time: 321 us
  waiting for transfers between devices  183 us (57%)
  matrix products  57.8 us (18%)
  starting transfers between devices  50.5 us (16%)
  other arithmetic  18.4 us (6%)
  local copies, waits for them, and re-layouts  10.6 us (3%)
    ppermute x32, waiting for transfers between devices, with_halo(): lax.ppermute(head, axis, [((i + 1) % count, i) for i in range(count)])  86.5 us
    ppermute x32, waiting for transfers between devices, with_halo(): lax.ppermute(tail, axis, [(i, (i + 1) % count) for i in range(count)])  65.7 us
    dot_general x16, matrix products, apply_operator(): jnp.einsum('kvj,tikj->tvi', window_cells, dense, preferred_element_type=j...  55.7 us
    ppermute x10, waiting for transfers between devices, all_sum(): lax.ppermute(value, axis, [(i, i ^ stride) for i in range(count)])  30.5 us
    ppermute x32, starting transfers between devices, with_halo(): lax.ppermute(tail, axis, [(i, (i + 1) % count) for i in range(count)])  25.1 us
    ppermute x32, starting transfers between devices, with_halo(): lax.ppermute(head, axis, [((i + 1) % count, i) for i in range(count)])  21.8 us
    gather x1, local copies, waits for them, and re-layouts, dense_coupling(): jnp.take(matrices, index.reshape(-1), axis=0)  10.3 us
    another operation x6, other arithmetic, orthonormal(): factor = jnp.linalg.cholesky(gram_matrix)  7.19 us
  transfers between devices with their start and end apart: 74, of which 72 were waited for; matrix products, arithmetic and copies ran while one was open for 4% of the time, Pallas kernels for 0%

profile of v3, /device:TPU:0, one launch (start us, length us, event | category | flops | bytes accessed | tf_op | source)
XLA Modules:
  0.0 320.7 jit_solution(12511227188803382971)
XLA Ops:
  0.9 3.9 %collective-permute-start.1 = (bf16[1,1,3,32,192]{4,3,2,1,0:T(8,128)(2,1)S(1)}, bf16[1,1,3,32,192]{4,3,2,1,0:T(8,128)(2,1)S(1)}, u32[]{:S(2)}, u32[]{:S(2)}) collective-permute-start(bf16[1,1,3,32,192]{4,3,2,1,0:T(8,128)(2,1)S(1)} %convert_element_type.61), channel_id=1, source_target_pairs={{8,0},{16,8},{24,16},{0,24},{9,1},{17,9},{25,17},{1,25},{10,2},{18... | collective-permute-start | bytes 110600 | tf_op jit(solution)/shard_map/ppermute | solution.py:26
  6.4 10.3 %gather_fusion = bf16[81,192,192]{2,1,0:T(8,128)(2,1)} fusion(bf16[81,192,192]{2,1,0:T(8,128)(2,1)} %bitcast.481, s32[1024]{0:T(1024)S(1)} %pad_clamp_fusion), kind=kCustom, calls=%fused_computation | custom fusion | bytes 11944260 | tf_op jit(solution)/shard_map/jit(_take)/gather | solution.py:41
  16.8 2.8 collective-permute-start.3
  19.7 2.5 collective-permute-done.3
  22.3 3.7 %collective-permute-done.2 = bf16[3,1,3,32,192]{4,3,2,1,0:T(8,128)(2,1)S(1)} collective-permute-done((bf16[3,1,3,32,192]{4,3,2,1,0:T(8,128)(2,1)S(1)}, bf16[3,1,3,32,192]{4,3,2,1,0:T(8,128)(2,1)S(1)}, u32[]{:S(2)}, u32[]{:S(2)}) %collective-permute-start.2) | collective-permute-done | bytes 110624 | tf_op jit(solution)/shard_map/ppermute | solution.py:24
  26.1 5.3 %fusion.171 = f32[3,32,192]{2,1,0:T(8,128)S(1)} fusion(bf16[27,32,192,1]{2,1,0,3:T(8,128)(2,1)S(1)} %bitcast.515, f32[1,1,3,32,192]{4,3,2,1,0:T(8,128)S(1)} %copy-done, bf16[3,27,192,192]{3,2,1,0:T(8,128)(2,1)} %bitcast.482, pred[3,27]{1,0:T(4,128)(4,1)S(1)} %compare_and_fusion, pred[3,27]{1,0:T(4,128)(4,1)S(1)} %and_reduce_fusion), kind=kOutput, calls=%fused_computation.82 | convolution fusion | flops 197111808 | bytes 6451362 | tf_op jit(solution)/shard_map/kvj,tikj->tvi/dot_general | solution.py:84
  31.4 2.7 collective-permute-start.5
  35.8 3.2 %collective-permute-done.4 = bf16[1,1,3,32,192]{4,3,2,1,0:T(8,128)(2,1)S(1)} collective-permute-done((bf16[1,1,3,32,192]{4,3,2,1,0:T(8,128)(2,1)S(1)}, bf16[1,1,3,32,192]{4,3,2,1,0:T(8,128)(2,1)S(1)}, u32[]{:S(2)}, u32[]{:S(2)}) %collective-permute-start.4) | collective-permute-done | bytes 36896 | tf_op jit(solution)/shard_map/ppermute | solution.py:24
  39.6 3.6 %collective-permute-done.7 = bf16[3,1,3,32,192]{4,3,2,1,0:T(8,128)(2,1)S(1)} collective-permute-done((bf16[3,1,3,32,192]{4,3,2,1,0:T(8,128)(2,1)S(1)}, bf16[3,1,3,32,192]{4,3,2,1,0:T(8,128)(2,1)S(1)}, u32[]{:S(2)}, u32[]{:S(2)}) %collective-permute-start.7) | collective-permute-done | bytes 110624 | tf_op jit(solution)/shard_map/ppermute | solution.py:26
  43.2 2.4 collective-permute-done.6
  45.7 3.1 fusion.174
  54.5 3.6 %collective-permute-done.11 = bf16[3,1,3,32,192]{4,3,2,1,0:T(8,128)(2,1)S(1)} collective-permute-done((bf16[3,1,3,32,192]{4,3,2,1,0:T(8,128)(2,1)S(1)}, bf16[3,1,3,32,192]{4,3,2,1,0:T(8,128)(2,1)S(1)}, u32[]{:S(2)}, u32[]{:S(2)}) %collective-permute-start.11) | collective-permute-done | bytes 110624 | tf_op jit(solution)/shard_map/ppermute | solution.py:26
  58.1 2.5 collective-permute-done.10
  60.7 3.1 fusion.177
  70.3 3.6 %collective-permute-done.15 = bf16[3,1,3,32,192]{4,3,2,1,0:T(8,128)(2,1)S(1)} collective-permute-done((bf16[3,1,3,32,192]{4,3,2,1,0:T(8,128)(2,1)S(1)}, bf16[3,1,3,32,192]{4,3,2,1,0:T(8,128)(2,1)S(1)}, u32[]{:S(2)}, u32[]{:S(2)}) %collective-permute-start.15) | collective-permute-done | bytes 110624 | tf_op jit(solution)/shard_map/ppermute | solution.py:26
  73.9 2.4 collective-permute-done.14
  76.3 3.1 fusion.180
  85.8 3.6 %collective-permute-done.19 = bf16[3,1,3,32,192]{4,3,2,1,0:T(8,128)(2,1)S(1)} collective-permute-done((bf16[3,1,3,32,192]{4,3,2,1,0:T(8,128)(2,1)S(1)}, bf16[3,1,3,32,192]{4,3,2,1,0:T(8,128)(2,1)S(1)}, u32[]{:S(2)}, u32[]{:S(2)}) %collective-permute-start.19) | collective-permute-done | bytes 110624 | tf_op jit(solution)/shard_map/ppermute | solution.py:26
  89.3 2.4 collective-permute-done.18
  91.8 3.1 fusion.183
  99.1 2.3 collective-permute-done.20
  101.9 3.6 %collective-permute-done.23 = bf16[3,1,3,32,192]{4,3,2,1,0:T(8,128)(2,1)S(1)} collective-permute-done((bf16[3,1,3,32,192]{4,3,2,1,0:T(8,128)(2,1)S(1)}, bf16[3,1,3,32,192]{4,3,2,1,0:T(8,128)(2,1)S(1)}, u32[]{:S(2)}, u32[]{:S(2)}) %collective-permute-start.23) | collective-permute-done | bytes 110624 | tf_op jit(solution)/shard_map/ppermute | solution.py:26
  105.5 2.4 collective-permute-done.22
  108.0 3.1 fusion.186
  116.9 3.6 %collective-permute-done.27 = bf16[3,1,3,32,192]{4,3,2,1,0:T(8,128)(2,1)S(1)} collective-permute-done((bf16[3,1,3,32,192]{4,3,2,1,0:T(8,128)(2,1)S(1)}, bf16[3,1,3,32,192]{4,3,2,1,0:T(8,128)(2,1)S(1)}, u32[]{:S(2)}, u32[]{:S(2)}) %collective-permute-start.27) | collective-permute-done | bytes 110624 | tf_op jit(solution)/shard_map/ppermute | solution.py:26
  120.5 2.4 collective-permute-done.26
  122.9 3.1 fusion.189
  132.6 3.6 %collective-permute-done.31 = bf16[3,1,3,32,192]{4,3,2,1,0:T(8,128)(2,1)S(1)} collective-permute-done((bf16[3,1,3,32,192]{4,3,2,1,0:T(8,128)(2,1)S(1)}, bf16[3,1,3,32,192]{4,3,2,1,0:T(8,128)(2,1)S(1)}, u32[]{:S(2)}, u32[]{:S(2)}) %collective-permute-start.31) | collective-permute-done | bytes 110624 | tf_op jit(solution)/shard_map/ppermute | solution.py:26
  136.1 2.5 collective-permute-done.30
  138.8 3.1 fusion.192
  142.4 3.5 %collective-permute-done.32 = f32[32,32]{0,1:T(8,128)S(1)} collective-permute-done((f32[32,32]{0,1:T(8,128)S(1)}, f32[32,32]{0,1:T(8,128)S(1)}, u32[]{:S(2)}, u32[]{:S(2)}) %collective-permute-start.32) | collective-permute-done | bytes 4128 | tf_op jit(solution)/shard_map/ppermute | solution.py:56
  150.9 3.7 %collective-permute-done.35 = f32[32,32]{0,1:T(8,128)S(1)} collective-permute-done((f32[32,32]{0,1:T(8,128)S(1)}, f32[32,32]{0,1:T(8,128)S(1)}, u32[]{:S(2)}, u32[]{:S(2)}) %collective-permute-start.35) | collective-permute-done | bytes 4128 | tf_op jit(solution)/shard_map/ppermute | solution.py:56
  154.6 4.6 %collective-permute-done.36 = f32[32,32]{0,1:T(8,128)S(1)} collective-permute-done((f32[32,32]{0,1:T(8,128)S(1)}, f32[32,32]{0,1:T(8,128)S(1)}, u32[]{:S(2)}, u32[]{:S(2)}) %collective-permute-start.36) | collective-permute-done | bytes 4128 | tf_op jit(solution)/shard_map/ppermute | solution.py:56
  159.3 2.9 cholesky.44
  163.6 2.4 custom-call.6
  173.1 3.6 %collective-permute-done.40 = bf16[3,1,3,32,192]{4,3,2,1,0:T(8,128)(2,1)S(1)} collective-permute-done((bf16[3,1,3,32,192]{4,3,2,1,0:T(8,128)(2,1)S(1)}, bf16[3,1,3,32,192]{4,3,2,1,0:T(8,128)(2,1)S(1)}, u32[]{:S(2)}, u32[]{:S(2)}) %collective-permute-start.40) | collective-permute-done | bytes 110624 | tf_op jit(solution)/shard_map/ppermute | solution.py:26
  176.7 2.4 collective-permute-done.39
  179.1 5.3 %fusion.126 = f32[3,192,32]{1,2,0:T(8,128)S(1)} fusion(bf16[27,32,192,1]{2,1,0,3:T(8,128)(2,1)S(1)} %bitcast.517, f32[3,192,32]{1,2,0:T(8,128)S(1)} %fusion.229, bf16[3,27,192,192]{3,2,1,0:T(8,128)(2,1)} %bitcast.483, pred[3,27]{1,0:T(4,128)(4,1)S(1)} %compare_and_fusion, pred[3,27]{1,0:T(4,128)(4,1)S(1)} %and_reduce_fusion), kind=kOutput, calls=%fused_computation.67 | convolution fusion | flops 197111808 | bytes 6451362 | tf_op jit(solution)/shard_map/kvj,tikj->tvi/dot_general | solution.py:84
  191.2 3.6 %collective-permute-done.44 = bf16[3,1,3,32,192]{4,3,2,1,0:T(8,128)(2,1)S(1)} collective-permute-done((bf16[3,1,3,32,192]{4,3,2,1,0:T(8,128)(2,1)S(1)}, bf16[3,1,3,32,192]{4,3,2,1,0:T(8,128)(2,1)S(1)}, u32[]{:S(2)}, u32[]{:S(2)}) %collective-permute-start.44) | collective-permute-done | bytes 110624 | tf_op jit(solution)/shard_map/ppermute | solution.py:26
  194.8 2.4 collective-permute-done.43
  197.2 5.3 %fusion.195 = f32[3,192,32]{1,2,0:T(8,128)S(1)} fusion(bf16[27,32,192,1]{2,1,0,3:T(8,128)(2,1)S(1)} %bitcast.509, f32[3,192,32]{1,2,0:T(8,128)S(1)} %fusion.229, f32[3,192,32]{1,2,0:T(8,128)S(1)} %fusion.126, bf16[3,27,192,192]{3,2,1,0:T(8,128)(2,1)} %bitcast.484, pred[3,27]{1,0:T(4,128)(4,1)S(1)} %compare_and_fusion, pred[3,27]{1,0:T(4,128)(4,1)S(1)} %and_reduce_fusion), kind=kOutput, calls=%fused_computation.90 | convolution fusion | flops 197167104 | bytes 6525090 | tf_op jit(solution)/shard_map/kvj,tikj->tvi/dot_general | solution.py:84
  208.4 3.6 %collective-permute-done.48 = bf16[3,1,3,32,192]{4,3,2,1,0:T(8,128)(2,1)S(1)} collective-permute-done((bf16[3,1,3,32,192]{4,3,2,1,0:T(8,128)(2,1)S(1)}, bf16[3,1,3,32,192]{4,3,2,1,0:T(8,128)(2,1)S(1)}, u32[]{:S(2)}, u32[]{:S(2)}) %collective-permute-start.48) | collective-permute-done | bytes 110624 | tf_op jit(solution)/shard_map/ppermute | solution.py:26
  212.0 2.4 collective-permute-done.47
  214.5 3.1 fusion.198
  224.1 3.6 %collective-permute-done.52 = bf16[3,1,3,32,192]{4,3,2,1,0:T(8,128)(2,1)S(1)} collective-permute-done((bf16[3,1,3,32,192]{4,3,2,1,0:T(8,128)(2,1)S(1)}, bf16[3,1,3,32,192]{4,3,2,1,0:T(8,128)(2,1)S(1)}, u32[]{:S(2)}, u32[]{:S(2)}) %collective-permute-start.52) | collective-permute-done | bytes 110624 | tf_op jit(solution)/shard_map/ppermute | solution.py:26
  227.6 2.4 collective-permute-done.51
  230.1 3.1 fusion.201
  239.8 3.6 %collective-permute-done.56 = bf16[3,1,3,32,192]{4,3,2,1,0:T(8,128)(2,1)S(1)} collective-permute-done((bf16[3,1,3,32,192]{4,3,2,1,0:T(8,128)(2,1)S(1)}, bf16[3,1,3,32,192]{4,3,2,1,0:T(8,128)(2,1)S(1)}, u32[]{:S(2)}, u32[]{:S(2)}) %collective-permute-start.56) | collective-permute-done | bytes 110624 | tf_op jit(solution)/shard_map/ppermute | solution.py:26
  243.4 2.4 collective-permute-done.55
  245.8 3.1 fusion.204
  255.7 3.6 %collective-permute-done.60 = bf16[3,1,3,32,192]{4,3,2,1,0:T(8,128)(2,1)S(1)} collective-permute-done((bf16[3,1,3,32,192]{4,3,2,1,0:T(8,128)(2,1)S(1)}, bf16[3,1,3,32,192]{4,3,2,1,0:T(8,128)(2,1)S(1)}, u32[]{:S(2)}, u32[]{:S(2)}) %collective-permute-start.60) | collective-permute-done | bytes 110624 | tf_op jit(solution)/shard_map/ppermute | solution.py:26
  259.3 2.4 collective-permute-done.59
  261.7 3.1 fusion.207
  270.7 3.6 %collective-permute-done.64 = bf16[3,1,3,32,192]{4,3,2,1,0:T(8,128)(2,1)S(1)} collective-permute-done((bf16[3,1,3,32,192]{4,3,2,1,0:T(8,128)(2,1)S(1)}, bf16[3,1,3,32,192]{4,3,2,1,0:T(8,128)(2,1)S(1)}, u32[]{:S(2)}, u32[]{:S(2)}) %collective-permute-start.64) | collective-permute-done | bytes 110624 | tf_op jit(solution)/shard_map/ppermute | solution.py:26
  274.2 2.4 collective-permute-done.63
  276.7 3.1 fusion.210
  286.4 3.6 %collective-permute-done.68 = bf16[3,1,3,32,192]{4,3,2,1,0:T(8,128)(2,1)S(1)} collective-permute-done((bf16[3,1,3,32,192]{4,3,2,1,0:T(8,128)(2,1)S(1)}, bf16[3,1,3,32,192]{4,3,2,1,0:T(8,128)(2,1)S(1)}, u32[]{:S(2)}, u32[]{:S(2)}) %collective-permute-start.68) | collective-permute-done | bytes 110624 | tf_op jit(solution)/shard_map/ppermute | solution.py:26
  289.9 2.4 collective-permute-done.67
  292.4 3.1 fusion.213
  296.0 3.5 %collective-permute-done.69 = f32[32,32]{0,1:T(8,128)S(1)} collective-permute-done((f32[32,32]{0,1:T(8,128)S(1)}, f32[32,32]{0,1:T(8,128)S(1)}, u32[]{:S(2)}, u32[]{:S(2)}) %collective-permute-start.69) | collective-permute-done | bytes 4128 | tf_op jit(solution)/shard_map/ppermute | solution.py:56
  304.5 3.7 %collective-permute-done.72 = f32[32,32]{0,1:T(8,128)S(1)} collective-permute-done((f32[32,32]{0,1:T(8,128)S(1)}, f32[32,32]{0,1:T(8,128)S(1)}, u32[]{:S(2)}, u32[]{:S(2)}) %collective-permute-start.72) | collective-permute-done | bytes 4128 | tf_op jit(solution)/shard_map/ppermute | solution.py:56
  308.2 4.6 %collective-permute-done.73 = f32[32,32]{0,1:T(8,128)S(1)} collective-permute-done((f32[32,32]{0,1:T(8,128)S(1)}, f32[32,32]{0,1:T(8,128)S(1)}, u32[]{:S(2)}, u32[]{:S(2)}) %collective-permute-start.73) | collective-permute-done | bytes 4128 | tf_op jit(solution)/shard_map/ppermute | solution.py:56
  312.9 2.9 cholesky.55
  317.2 2.4 custom-call.7
  (199 shorter events, 109.3 us)
Async XLA Ops:
  0.9 15.8 %collective-permute-start.1 = (bf16[1,1,3,32,192]{4,3,2,1,0:T(8,128)(2,1)S(1)}, bf16[1,1,3,32,192]{4,3,2,1,0:T(8,128)(2,1)S(1)}, u32[]{:S(2)}, u32[]{:S(2)}) collective-permute-start(bf16[1,1,3,32,192]{4,3,2,1,0:T(8,128)(2,1)S(1)} %convert_element_type.61), channel_id=1, source_target_pairs={{8,0},{16,8},{24,16},{0,24},{9,1},{17,9},{25,17},{1,25},{10,2},{18... | collective-permute-start | bytes 110600 | tf_op jit(solution)/shard_map/ppermute | solution.py:26
  4.8 11.9 %collective-permute-start = (bf16[1,1,3,32,192]{4,3,2,1,0:T(8,128)(2,1)S(1)}, bf16[1,1,3,32,192]{4,3,2,1,0:T(8,128)(2,1)S(1)}, u32[]{:S(2)}, u32[]{:S(2)}) collective-permute-start(bf16[1,1,3,32,192]{4,3,2,1,0:T(8,128)(2,1)S(1)} %convert_element_type.61), channel_id=1, source_target_pairs={{0,8},{8,16},{16,24},{24,0},{1,9},{9,17},{17,25},{25,1},{2,10},{10... | collective-permute-start | bytes 110600 | tf_op jit(solution)/shard_map/ppermute | solution.py:24
  16.8 5.5 %collective-permute-start.3 = (bf16[3,1,3,32,192]{4,3,2,1,0:T(8,128)(2,1)S(1)}, bf16[3,1,3,32,192]{4,3,2,1,0:T(8,128)(2,1)S(1)}, u32[]{:S(2)}, u32[]{:S(2)}) collective-permute-start(bf16[3,1,3,32,192]{4,3,2,1,0:T(8,128)(2,1)S(1)} %pad_maximum_fusion.16), channel_id=1, source_target_pairs={{1,0},{2,1},{3,2},{4,3},{5,4},{6,5},{7,6},{0,7},{9,8},{10,9},{11,1... | collective-permute-start | bytes 331784 | tf_op jit(solution)/shard_map/ppermute | solution.py:26
  19.6 6.4 %collective-permute-start.2 = (bf16[3,1,3,32,192]{4,3,2,1,0:T(8,128)(2,1)S(1)}, bf16[3,1,3,32,192]{4,3,2,1,0:T(8,128)(2,1)S(1)}, u32[]{:S(2)}, u32[]{:S(2)}) collective-permute-start(bf16[3,1,3,32,192]{4,3,2,1,0:T(8,128)(2,1)S(1)} %pad_maximum_fusion.16), channel_id=1, source_target_pairs={{0,1},{1,2},{2,3},{3,4},{4,5},{5,6},{6,7},{7,0},{8,9},{9,10},{10,1... | collective-permute-start | bytes 331784 | tf_op jit(solution)/shard_map/ppermute | solution.py:24
  31.4 4.4 %collective-permute-start.5 = (bf16[1,1,3,32,192]{4,3,2,1,0:T(8,128)(2,1)S(1)}, bf16[1,1,3,32,192]{4,3,2,1,0:T(8,128)(2,1)S(1)}, u32[]{:S(2)}, u32[]{:S(2)}) collective-permute-start(bf16[1,1,3,32,192]{4,3,2,1,0:T(8,128)(2,1)S(1)} %fusion.217), channel_id=1, source_target_pairs={{8,0},{16,8},{24,16},{0,24},{9,1},{17,9},{25,17},{1,25},{10,2},{18... | collective-permute-start | bytes 110600 | tf_op jit(solution)/shard_map/ppermute | solution.py:26
  34.0 5.0 %collective-permute-start.4 = (bf16[1,1,3,32,192]{4,3,2,1,0:T(8,128)(2,1)S(1)}, bf16[1,1,3,32,192]{4,3,2,1,0:T(8,128)(2,1)S(1)}, u32[]{:S(2)}, u32[]{:S(2)}) collective-permute-start(bf16[1,1,3,32,192]{4,3,2,1,0:T(8,128)(2,1)S(1)} %fusion.217), channel_id=1, source_target_pairs={{0,8},{8,16},{16,24},{24,0},{1,9},{9,17},{17,25},{25,1},{2,10},{10... | collective-permute-start | bytes 110600 | tf_op jit(solution)/shard_map/ppermute | solution.py:24
  39.1 4.1 %collective-permute-start.7 = (bf16[3,1,3,32,192]{4,3,2,1,0:T(8,128)(2,1)S(1)}, bf16[3,1,3,32,192]{4,3,2,1,0:T(8,128)(2,1)S(1)}, u32[]{:S(2)}, u32[]{:S(2)}) collective-permute-start(bf16[3,1,3,32,192]{4,3,2,1,0:T(8,128)(2,1)S(1)} %pad_maximum_fusion.17), channel_id=1, source_target_pairs={{1,0},{2,1},{3,2},{4,3},{5,4},{6,5},{7,6},{0,7},{9,8},{10,9},{11,1... | collective-permute-start | bytes 331784 | tf_op jit(solution)/shard_map/ppermute | solution.py:26
  39.1 6.4 %collective-permute-start.6 = (bf16[3,1,3,32,192]{4,3,2,1,0:T(8,128)(2,1)S(1)}, bf16[3,1,3,32,192]{4,3,2,1,0:T(8,128)(2,1)S(1)}, u32[]{:S(2)}, u32[]{:S(2)}) collective-permute-start(bf16[3,1,3,32,192]{4,3,2,1,0:T(8,128)(2,1)S(1)} %pad_maximum_fusion.17), channel_id=1, source_target_pairs={{0,1},{1,2},{2,3},{3,4},{4,5},{5,6},{6,7},{7,0},{8,9},{9,10},{10,1... | collective-permute-start | bytes 331784 | tf_op jit(solution)/shard_map/ppermute | solution.py:24
  48.8 4.1 %collective-permute-start.9 = (bf16[1,1,3,32,192]{4,3,2,1,0:T(8,128)(2,1)S(1)}, bf16[1,1,3,32,192]{4,3,2,1,0:T(8,128)(2,1)S(1)}, u32[]{:S(2)}, u32[]{:S(2)}) collective-permute-start(bf16[1,1,3,32,192]{4,3,2,1,0:T(8,128)(2,1)S(1)} %convert_bitcast_fusion.11), channel_id=1, source_target_pairs={{8,0},{16,8},{24,16},{0,24},{9,1},{17,9},{25,17},{1,25},{10,2},{18... | collective-permute-start | bytes 110600 | tf_op jit(solution)/shard_map/ppermute | solution.py:26
  48.9 5.0 %collective-permute-start.8 = (bf16[1,1,3,32,192]{4,3,2,1,0:T(8,128)(2,1)S(1)}, bf16[1,1,3,32,192]{4,3,2,1,0:T(8,128)(2,1)S(1)}, u32[]{:S(2)}, u32[]{:S(2)}) collective-permute-start(bf16[1,1,3,32,192]{4,3,2,1,0:T(8,128)(2,1)S(1)} %convert_bitcast_fusion.11), channel_id=1, source_target_pairs={{0,8},{8,16},{16,24},{24,0},{1,9},{9,17},{17,25},{25,1},{2,10},{10... | collective-permute-start | bytes 110600 | tf_op jit(solution)/shard_map/ppermute | solution.py:24
  53.9 4.1 %collective-permute-start.11 = (bf16[3,1,3,32,192]{4,3,2,1,0:T(8,128)(2,1)S(1)}, bf16[3,1,3,32,192]{4,3,2,1,0:T(8,128)(2,1)S(1)}, u32[]{:S(2)}, u32[]{:S(2)}) collective-permute-start(bf16[3,1,3,32,192]{4,3,2,1,0:T(8,128)(2,1)S(1)} %pad_maximum_fusion.18), channel_id=1, source_target_pairs={{1,0},{2,1},{3,2},{4,3},{5,4},{6,5},{7,6},{0,7},{9,8},{10,9},{11,1... | collective-permute-start | bytes 331784 | tf_op jit(solution)/shard_map/ppermute | solution.py:26
  54.2 6.4 %collective-permute-start.10 = (bf16[3,1,3,32,192]{4,3,2,1,0:T(8,128)(2,1)S(1)}, bf16[3,1,3,32,192]{4,3,2,1,0:T(8,128)(2,1)S(1)}, u32[]{:S(2)}, u32[]{:S(2)}) collective-permute-start(bf16[3,1,3,32,192]{4,3,2,1,0:T(8,128)(2,1)S(1)} %pad_maximum_fusion.18), channel_id=1, source_target_pairs={{0,1},{1,2},{2,3},{3,4},{4,5},{5,6},{6,7},{7,0},{8,9},{9,10},{10,1... | collective-permute-start | bytes 331784 | tf_op jit(solution)/shard_map/ppermute | solution.py:24
  63.8 4.1 %collective-permute-start.13 = (bf16[1,1,3,32,192]{4,3,2,1,0:T(8,128)(2,1)S(1)}, bf16[1,1,3,32,192]{4,3,2,1,0:T(8,128)(2,1)S(1)}, u32[]{:S(2)}, u32[]{:S(2)}) collective-permute-start(bf16[1,1,3,32,192]{4,3,2,1,0:T(8,128)(2,1)S(1)} %convert_bitcast_fusion.10), channel_id=1, source_target_pairs={{8,0},{16,8},{24,16},{0,24},{9,1},{17,9},{25,17},{1,25},{10,2},{18... | collective-permute-start | bytes 110600 | tf_op jit(solution)/shard_map/ppermute | solution.py:26
  64.7 5.0 %collective-permute-start.12 = (bf16[1,1,3,32,192]{4,3,2,1,0:T(8,128)(2,1)S(1)}, bf16[1,1,3,32,192]{4,3,2,1,0:T(8,128)(2,1)S(1)}, u32[]{:S(2)}, u32[]{:S(2)}) collective-permute-start(bf16[1,1,3,32,192]{4,3,2,1,0:T(8,128)(2,1)S(1)} %convert_bitcast_fusion.10), channel_id=1, source_target_pairs={{0,8},{8,16},{16,24},{24,0},{1,9},{9,17},{17,25},{25,1},{2,10},{10... | collective-permute-start | bytes 110600 | tf_op jit(solution)/shard_map/ppermute | solution.py:24
  69.7 4.1 %collective-permute-start.15 = (bf16[3,1,3,32,192]{4,3,2,1,0:T(8,128)(2,1)S(1)}, bf16[3,1,3,32,192]{4,3,2,1,0:T(8,128)(2,1)S(1)}, u32[]{:S(2)}, u32[]{:S(2)}) collective-permute-start(bf16[3,1,3,32,192]{4,3,2,1,0:T(8,128)(2,1)S(1)} %pad_maximum_fusion.19), channel_id=1, source_target_pairs={{1,0},{2,1},{3,2},{4,3},{5,4},{6,5},{7,6},{0,7},{9,8},{10,9},{11,1... | collective-permute-start | bytes 331784 | tf_op jit(solution)/shard_map/ppermute | solution.py:26
  69.8 6.4 %collective-permute-start.14 = (bf16[3,1,3,32,192]{4,3,2,1,0:T(8,128)(2,1)S(1)}, bf16[3,1,3,32,192]{4,3,2,1,0:T(8,128)(2,1)S(1)}, u32[]{:S(2)}, u32[]{:S(2)}) collective-permute-start(bf16[3,1,3,32,192]{4,3,2,1,0:T(8,128)(2,1)S(1)} %pad_maximum_fusion.19), channel_id=1, source_target_pairs={{0,1},{1,2},{2,3},{3,4},{4,5},{5,6},{6,7},{7,0},{8,9},{9,10},{10,1... | collective-permute-start | bytes 331784 | tf_op jit(solution)/shard_map/ppermute | solution.py:24
  79.4 4.1 %collective-permute-start.17 = (bf16[1,1,3,32,192]{4,3,2,1,0:T(8,128)(2,1)S(1)}, bf16[1,1,3,32,192]{4,3,2,1,0:T(8,128)(2,1)S(1)}, u32[]{:S(2)}, u32[]{:S(2)}) collective-permute-start(bf16[1,1,3,32,192]{4,3,2,1,0:T(8,128)(2,1)S(1)} %convert_bitcast_fusion.9), channel_id=1, source_target_pairs={{8,0},{16,8},{24,16},{0,24},{9,1},{17,9},{25,17},{1,25},{10,2},{18... | collective-permute-start | bytes 110600 | tf_op jit(solution)/shard_map/ppermute | solution.py:26
  80.2 5.0 %collective-permute-start.16 = (bf16[1,1,3,32,192]{4,3,2,1,0:T(8,128)(2,1)S(1)}, bf16[1,1,3,32,192]{4,3,2,1,0:T(8,128)(2,1)S(1)}, u32[]{:S(2)}, u32[]{:S(2)}) collective-permute-start(bf16[1,1,3,32,192]{4,3,2,1,0:T(8,128)(2,1)S(1)} %convert_bitcast_fusion.9), channel_id=1, source_target_pairs={{0,8},{8,16},{16,24},{24,0},{1,9},{9,17},{17,25},{25,1},{2,10},{10... | collective-permute-start | bytes 110600 | tf_op jit(solution)/shard_map/ppermute | solution.py:24
  85.2 4.1 %collective-permute-start.19 = (bf16[3,1,3,32,192]{4,3,2,1,0:T(8,128)(2,1)S(1)}, bf16[3,1,3,32,192]{4,3,2,1,0:T(8,128)(2,1)S(1)}, u32[]{:S(2)}, u32[]{:S(2)}) collective-permute-start(bf16[3,1,3,32,192]{4,3,2,1,0:T(8,128)(2,1)S(1)} %pad_maximum_fusion.20), channel_id=1, source_target_pairs={{1,0},{2,1},{3,2},{4,3},{5,4},{6,5},{7,6},{0,7},{9,8},{10,9},{11,1... | collective-permute-start | bytes 331784 | tf_op jit(solution)/shard_map/ppermute | solution.py:26
  85.3 6.4 %collective-permute-start.18 = (bf16[3,1,3,32,192]{4,3,2,1,0:T(8,128)(2,1)S(1)}, bf16[3,1,3,32,192]{4,3,2,1,0:T(8,128)(2,1)S(1)}, u32[]{:S(2)}, u32[]{:S(2)}) collective-permute-start(bf16[3,1,3,32,192]{4,3,2,1,0:T(8,128)(2,1)S(1)} %pad_maximum_fusion.20), channel_id=1, source_target_pairs={{0,1},{1,2},{2,3},{3,4},{4,5},{5,6},{6,7},{7,0},{8,9},{9,10},{10,1... | collective-permute-start | bytes 331784 | tf_op jit(solution)/shard_map/ppermute | solution.py:24
  94.9 4.1 %collective-permute-start.21 = (bf16[1,1,3,32,192]{4,3,2,1,0:T(8,128)(2,1)S(1)}, bf16[1,1,3,32,192]{4,3,2,1,0:T(8,128)(2,1)S(1)}, u32[]{:S(2)}, u32[]{:S(2)}) collective-permute-start(bf16[1,1,3,32,192]{4,3,2,1,0:T(8,128)(2,1)S(1)} %convert_bitcast_fusion.8), channel_id=1, source_target_pairs={{8,0},{16,8},{24,16},{0,24},{9,1},{17,9},{25,17},{1,25},{10,2},{18... | collective-permute-start | bytes 110600 | tf_op jit(solution)/shard_map/ppermute | solution.py:26
  96.3 5.0 %collective-permute-start.20 = (bf16[1,1,3,32,192]{4,3,2,1,0:T(8,128)(2,1)S(1)}, bf16[1,1,3,32,192]{4,3,2,1,0:T(8,128)(2,1)S(1)}, u32[]{:S(2)}, u32[]{:S(2)}) collective-permute-start(bf16[1,1,3,32,192]{4,3,2,1,0:T(8,128)(2,1)S(1)} %convert_bitcast_fusion.8), channel_id=1, source_target_pairs={{0,8},{8,16},{16,24},{24,0},{1,9},{9,17},{17,25},{25,1},{2,10},{10... | collective-permute-start | bytes 110600 | tf_op jit(solution)/shard_map/ppermute | solution.py:24
  101.4 4.1 %collective-permute-start.23 = (bf16[3,1,3,32,192]{4,3,2,1,0:T(8,128)(2,1)S(1)}, bf16[3,1,3,32,192]{4,3,2,1,0:T(8,128)(2,1)S(1)}, u32[]{:S(2)}, u32[]{:S(2)}) collective-permute-start(bf16[3,1,3,32,192]{4,3,2,1,0:T(8,128)(2,1)S(1)} %pad_maximum_fusion.21), channel_id=1, source_target_pairs={{1,0},{2,1},{3,2},{4,3},{5,4},{6,5},{7,6},{0,7},{9,8},{10,9},{11,1... | collective-permute-start | bytes 331784 | tf_op jit(solution)/shard_map/ppermute | solution.py:26
  101.4 6.4 %collective-permute-start.22 = (bf16[3,1,3,32,192]{4,3,2,1,0:T(8,128)(2,1)S(1)}, bf16[3,1,3,32,192]{4,3,2,1,0:T(8,128)(2,1)S(1)}, u32[]{:S(2)}, u32[]{:S(2)}) collective-permute-start(bf16[3,1,3,32,192]{4,3,2,1,0:T(8,128)(2,1)S(1)} %pad_maximum_fusion.21), channel_id=1, source_target_pairs={{0,1},{1,2},{2,3},{3,4},{4,5},{5,6},{6,7},{7,0},{8,9},{9,10},{10,1... | collective-permute-start | bytes 331784 | tf_op jit(solution)/shard_map/ppermute | solution.py:24
  111.1 4.1 %collective-permute-start.25 = (bf16[1,1,3,32,192]{4,3,2,1,0:T(8,128)(2,1)S(1)}, bf16[1,1,3,32,192]{4,3,2,1,0:T(8,128)(2,1)S(1)}, u32[]{:S(2)}, u32[]{:S(2)}) collective-permute-start(bf16[1,1,3,32,192]{4,3,2,1,0:T(8,128)(2,1)S(1)} %convert_bitcast_fusion.7), channel_id=1, source_target_pairs={{8,0},{16,8},{24,16},{0,24},{9,1},{17,9},{25,17},{1,25},{10,2},{18... | collective-permute-start | bytes 110600 | tf_op jit(solution)/shard_map/ppermute | solution.py:26
  111.3 5.0 %collective-permute-start.24 = (bf16[1,1,3,32,192]{4,3,2,1,0:T(8,128)(2,1)S(1)}, bf16[1,1,3,32,192]{4,3,2,1,0:T(8,128)(2,1)S(1)}, u32[]{:S(2)}, u32[]{:S(2)}) collective-permute-start(bf16[1,1,3,32,192]{4,3,2,1,0:T(8,128)(2,1)S(1)} %convert_bitcast_fusion.7), channel_id=1, source_target_pairs={{0,8},{8,16},{16,24},{24,0},{1,9},{9,17},{17,25},{25,1},{2,10},{10... | collective-permute-start | bytes 110600 | tf_op jit(solution)/shard_map/ppermute | solution.py:24
  116.3 4.1 %collective-permute-start.27 = (bf16[3,1,3,32,192]{4,3,2,1,0:T(8,128)(2,1)S(1)}, bf16[3,1,3,32,192]{4,3,2,1,0:T(8,128)(2,1)S(1)}, u32[]{:S(2)}, u32[]{:S(2)}) collective-permute-start(bf16[3,1,3,32,192]{4,3,2,1,0:T(8,128)(2,1)S(1)} %pad_maximum_fusion.22), channel_id=1, source_target_pairs={{1,0},{2,1},{3,2},{4,3},{5,4},{6,5},{7,6},{0,7},{9,8},{10,9},{11,1... | collective-permute-start | bytes 331784 | tf_op jit(solution)/shard_map/ppermute | solution.py:26
  116.5 6.4 %collective-permute-start.26 = (bf16[3,1,3,32,192]{4,3,2,1,0:T(8,128)(2,1)S(1)}, bf16[3,1,3,32,192]{4,3,2,1,0:T(8,128)(2,1)S(1)}, u32[]{:S(2)}, u32[]{:S(2)}) collective-permute-start(bf16[3,1,3,32,192]{4,3,2,1,0:T(8,128)(2,1)S(1)} %pad_maximum_fusion.22), channel_id=1, source_target_pairs={{0,1},{1,2},{2,3},{3,4},{4,5},{5,6},{6,7},{7,0},{8,9},{9,10},{10,1... | collective-permute-start | bytes 331784 | tf_op jit(solution)/shard_map/ppermute | solution.py:24
  126.0 4.1 %collective-permute-start.29 = (bf16[1,1,3,32,192]{4,3,2,1,0:T(8,128)(2,1)S(1)}, bf16[1,1,3,32,192]{4,3,2,1,0:T(8,128)(2,1)S(1)}, u32[]{:S(2)}, u32[]{:S(2)}) collective-permute-start(bf16[1,1,3,32,192]{4,3,2,1,0:T(8,128)(2,1)S(1)} %convert_bitcast_fusion.6), channel_id=1, source_target_pairs={{8,0},{16,8},{24,16},{0,24},{9,1},{17,9},{25,17},{1,25},{10,2},{18... | collective-permute-start | bytes 110600 | tf_op jit(solution)/shard_map/ppermute | solution.py:26
  127.0 5.0 %collective-permute-start.28 = (bf16[1,1,3,32,192]{4,3,2,1,0:T(8,128)(2,1)S(1)}, bf16[1,1,3,32,192]{4,3,2,1,0:T(8,128)(2,1)S(1)}, u32[]{:S(2)}, u32[]{:S(2)}) collective-permute-start(bf16[1,1,3,32,192]{4,3,2,1,0:T(8,128)(2,1)S(1)} %convert_bitcast_fusion.6), channel_id=1, source_target_pairs={{0,8},{8,16},{16,24},{24,0},{1,9},{9,17},{17,25},{25,1},{2,10},{10... | collective-permute-start | bytes 110600 | tf_op jit(solution)/shard_map/ppermute | solution.py:24
  132.0 4.1 %collective-permute-start.31 = (bf16[3,1,3,32,192]{4,3,2,1,0:T(8,128)(2,1)S(1)}, bf16[3,1,3,32,192]{4,3,2,1,0:T(8,128)(2,1)S(1)}, u32[]{:S(2)}, u32[]{:S(2)}) collective-permute-start(bf16[3,1,3,32,192]{4,3,2,1,0:T(8,128)(2,1)S(1)} %pad_maximum_fusion.23), channel_id=1, source_target_pairs={{1,0},{2,1},{3,2},{4,3},{5,4},{6,5},{7,6},{0,7},{9,8},{10,9},{11,1... | collective-permute-start | bytes 331784 | tf_op jit(solution)/shard_map/ppermute | solution.py:26
  132.1 6.6 %collective-permute-start.30 = (bf16[3,1,3,32,192]{4,3,2,1,0:T(8,128)(2,1)S(1)}, bf16[3,1,3,32,192]{4,3,2,1,0:T(8,128)(2,1)S(1)}, u32[]{:S(2)}, u32[]{:S(2)}) collective-permute-start(bf16[3,1,3,32,192]{4,3,2,1,0:T(8,128)(2,1)S(1)} %pad_maximum_fusion.23), channel_id=1, source_target_pairs={{0,1},{1,2},{2,3},{3,4},{4,5},{5,6},{6,7},{7,0},{8,9},{9,10},{10,1... | collective-permute-start | bytes 331784 | tf_op jit(solution)/shard_map/ppermute | solution.py:24
  154.6 4.6 %collective-permute-start.36 = (f32[32,32]{0,1:T(8,128)S(1)}, f32[32,32]{0,1:T(8,128)S(1)}, u32[]{:S(2)}, u32[]{:S(2)}) collective-permute-start(f32[32,32]{0,1:T(8,128)S(1)} %add.68), channel_id=1, source_target_pairs={{0,4},{1,5},{2,6},{3,7},{4,0},{5,1},{6,2},{7,3},{8,12},{9,13},{10,... | collective-permute-start | bytes 12296 | tf_op jit(solution)/shard_map/ppermute | solution.py:56
  166.5 4.1 %collective-permute-start.38 = (bf16[1,1,3,32,192]{4,3,2,1,0:T(8,128)(2,1)S(1)}, bf16[1,1,3,32,192]{4,3,2,1,0:T(8,128)(2,1)S(1)}, u32[]{:S(2)}, u32[]{:S(2)}) collective-permute-start(bf16[1,1,3,32,192]{4,3,2,1,0:T(8,128)(2,1)S(1)} %fusion.218), channel_id=1, source_target_pairs={{8,0},{16,8},{24,16},{0,24},{9,1},{17,9},{25,17},{1,25},{10,2},{18... | collective-permute-start | bytes 110600 | tf_op jit(solution)/shard_map/ppermute | solution.py:26
  167.5 5.0 %collective-permute-start.37 = (bf16[1,1,3,32,192]{4,3,2,1,0:T(8,128)(2,1)S(1)}, bf16[1,1,3,32,192]{4,3,2,1,0:T(8,128)(2,1)S(1)}, u32[]{:S(2)}, u32[]{:S(2)}) collective-permute-start(bf16[1,1,3,32,192]{4,3,2,1,0:T(8,128)(2,1)S(1)} %fusion.218), channel_id=1, source_target_pairs={{0,8},{8,16},{16,24},{24,0},{1,9},{9,17},{17,25},{25,1},{2,10},{10... | collective-permute-start | bytes 110600 | tf_op jit(solution)/shard_map/ppermute | solution.py:24
  172.5 4.1 %collective-permute-start.40 = (bf16[3,1,3,32,192]{4,3,2,1,0:T(8,128)(2,1)S(1)}, bf16[3,1,3,32,192]{4,3,2,1,0:T(8,128)(2,1)S(1)}, u32[]{:S(2)}, u32[]{:S(2)}) collective-permute-start(bf16[3,1,3,32,192]{4,3,2,1,0:T(8,128)(2,1)S(1)} %pad_maximum_fusion.24), channel_id=1, source_target_pairs={{1,0},{2,1},{3,2},{4,3},{5,4},{6,5},{7,6},{0,7},{9,8},{10,9},{11,1... | collective-permute-start | bytes 331784 | tf_op jit(solution)/shard_map/ppermute | solution.py:26
  172.6 6.4 %collective-permute-start.39 = (bf16[3,1,3,32,192]{4,3,2,1,0:T(8,128)(2,1)S(1)}, bf16[3,1,3,32,192]{4,3,2,1,0:T(8,128)(2,1)S(1)}, u32[]{:S(2)}, u32[]{:S(2)}) collective-permute-start(bf16[3,1,3,32,192]{4,3,2,1,0:T(8,128)(2,1)S(1)} %pad_maximum_fusion.24), channel_id=1, source_target_pairs={{0,1},{1,2},{2,3},{3,4},{4,5},{5,6},{6,7},{7,0},{8,9},{9,10},{10,1... | collective-permute-start | bytes 331784 | tf_op jit(solution)/shard_map/ppermute | solution.py:24
  184.5 4.1 %collective-permute-start.42 = (bf16[1,1,3,32,192]{4,3,2,1,0:T(8,128)(2,1)S(1)}, bf16[1,1,3,32,192]{4,3,2,1,0:T(8,128)(2,1)S(1)}, u32[]{:S(2)}, u32[]{:S(2)}) collective-permute-start(bf16[1,1,3,32,192]{4,3,2,1,0:T(8,128)(2,1)S(1)} %fusion.219), channel_id=1, source_target_pairs={{8,0},{16,8},{24,16},{0,24},{9,1},{17,9},{25,17},{1,25},{10,2},{18... | collective-permute-start | bytes 110600 | tf_op jit(solution)/shard_map/ppermute | solution.py:26
  185.6 5.0 %collective-permute-start.41 = (bf16[1,1,3,32,192]{4,3,2,1,0:T(8,128)(2,1)S(1)}, bf16[1,1,3,32,192]{4,3,2,1,0:T(8,128)(2,1)S(1)}, u32[]{:S(2)}, u32[]{:S(2)}) collective-permute-start(bf16[1,1,3,32,192]{4,3,2,1,0:T(8,128)(2,1)S(1)} %fusion.219), channel_id=1, source_target_pairs={{0,8},{8,16},{16,24},{24,0},{1,9},{9,17},{17,25},{25,1},{2,10},{10... | collective-permute-start | bytes 110600 | tf_op jit(solution)/shard_map/ppermute | solution.py:24
  190.6 4.1 %collective-permute-start.44 = (bf16[3,1,3,32,192]{4,3,2,1,0:T(8,128)(2,1)S(1)}, bf16[3,1,3,32,192]{4,3,2,1,0:T(8,128)(2,1)S(1)}, u32[]{:S(2)}, u32[]{:S(2)}) collective-permute-start(bf16[3,1,3,32,192]{4,3,2,1,0:T(8,128)(2,1)S(1)} %pad_maximum_fusion.25), channel_id=1, source_target_pairs={{1,0},{2,1},{3,2},{4,3},{5,4},{6,5},{7,6},{0,7},{9,8},{10,9},{11,1... | collective-permute-start | bytes 331784 | tf_op jit(solution)/shard_map/ppermute | solution.py:26
  190.7 6.4 %collective-permute-start.43 = (bf16[3,1,3,32,192]{4,3,2,1,0:T(8,128)(2,1)S(1)}, bf16[3,1,3,32,192]{4,3,2,1,0:T(8,128)(2,1)S(1)}, u32[]{:S(2)}, u32[]{:S(2)}) collective-permute-start(bf16[3,1,3,32,192]{4,3,2,1,0:T(8,128)(2,1)S(1)} %pad_maximum_fusion.25), channel_id=1, source_target_pairs={{0,1},{1,2},{2,3},{3,4},{4,5},{5,6},{6,7},{7,0},{8,9},{9,10},{10,1... | collective-permute-start | bytes 331784 | tf_op jit(solution)/shard_map/ppermute | solution.py:24
  202.6 4.1 %collective-permute-start.46 = (bf16[1,1,3,32,192]{4,3,2,1,0:T(8,128)(2,1)S(1)}, bf16[1,1,3,32,192]{4,3,2,1,0:T(8,128)(2,1)S(1)}, u32[]{:S(2)}, u32[]{:S(2)}) collective-permute-start(bf16[1,1,3,32,192]{4,3,2,1,0:T(8,128)(2,1)S(1)} %convert_bitcast_fusion.2), channel_id=1, source_target_pairs={{8,0},{16,8},{24,16},{0,24},{9,1},{17,9},{25,17},{1,25},{10,2},{18... | collective-permute-start | bytes 110600 | tf_op jit(solution)/shard_map/ppermute | solution.py:26
  202.8 5.0 %collective-permute-start.45 = (bf16[1,1,3,32,192]{4,3,2,1,0:T(8,128)(2,1)S(1)}, bf16[1,1,3,32,192]{4,3,2,1,0:T(8,128)(2,1)S(1)}, u32[]{:S(2)}, u32[]{:S(2)}) collective-permute-start(bf16[1,1,3,32,192]{4,3,2,1,0:T(8,128)(2,1)S(1)} %convert_bitcast_fusion.2), channel_id=1, source_target_pairs={{0,8},{8,16},{16,24},{24,0},{1,9},{9,17},{17,25},{25,1},{2,10},{10... | collective-permute-start | bytes 110600 | tf_op jit(solution)/shard_map/ppermute | solution.py:24
  207.8 4.1 %collective-permute-start.48 = (bf16[3,1,3,32,192]{4,3,2,1,0:T(8,128)(2,1)S(1)}, bf16[3,1,3,32,192]{4,3,2,1,0:T(8,128)(2,1)S(1)}, u32[]{:S(2)}, u32[]{:S(2)}) collective-permute-start(bf16[3,1,3,32,192]{4,3,2,1,0:T(8,128)(2,1)S(1)} %pad_maximum_fusion.26), channel_id=1, source_target_pairs={{1,0},{2,1},{3,2},{4,3},{5,4},{6,5},{7,6},{0,7},{9,8},{10,9},{11,1... | collective-permute-start | bytes 331784 | tf_op jit(solution)/shard_map/ppermute | solution.py:26
  208.0 6.4 %collective-permute-start.47 = (bf16[3,1,3,32,192]{4,3,2,1,0:T(8,128)(2,1)S(1)}, bf16[3,1,3,32,192]{4,3,2,1,0:T(8,128)(2,1)S(1)}, u32[]{:S(2)}, u32[]{:S(2)}) collective-permute-start(bf16[3,1,3,32,192]{4,3,2,1,0:T(8,128)(2,1)S(1)} %pad_maximum_fusion.26), channel_id=1, source_target_pairs={{0,1},{1,2},{2,3},{3,4},{4,5},{5,6},{6,7},{7,0},{8,9},{9,10},{10,1... | collective-permute-start | bytes 331784 | tf_op jit(solution)/shard_map/ppermute | solution.py:24
  217.6 4.1 %collective-permute-start.50 = (bf16[1,1,3,32,192]{4,3,2,1,0:T(8,128)(2,1)S(1)}, bf16[1,1,3,32,192]{4,3,2,1,0:T(8,128)(2,1)S(1)}, u32[]{:S(2)}, u32[]{:S(2)}) collective-permute-start(bf16[1,1,3,32,192]{4,3,2,1,0:T(8,128)(2,1)S(1)} %convert_bitcast_fusion.1), channel_id=1, source_target_pairs={{8,0},{16,8},{24,16},{0,24},{9,1},{17,9},{25,17},{1,25},{10,2},{18... | collective-permute-start | bytes 110600 | tf_op jit(solution)/shard_map/ppermute | solution.py:26
  218.5 5.0 %collective-permute-start.49 = (bf16[1,1,3,32,192]{4,3,2,1,0:T(8,128)(2,1)S(1)}, bf16[1,1,3,32,192]{4,3,2,1,0:T(8,128)(2,1)S(1)}, u32[]{:S(2)}, u32[]{:S(2)}) collective-permute-start(bf16[1,1,3,32,192]{4,3,2,1,0:T(8,128)(2,1)S(1)} %convert_bitcast_fusion.1), channel_id=1, source_target_pairs={{0,8},{8,16},{16,24},{24,0},{1,9},{9,17},{17,25},{25,1},{2,10},{10... | collective-permute-start | bytes 110600 | tf_op jit(solution)/shard_map/ppermute | solution.py:24
  223.6 6.4 %collective-permute-start.51 = (bf16[3,1,3,32,192]{4,3,2,1,0:T(8,128)(2,1)S(1)}, bf16[3,1,3,32,192]{4,3,2,1,0:T(8,128)(2,1)S(1)}, u32[]{:S(2)}, u32[]{:S(2)}) collective-permute-start(bf16[3,1,3,32,192]{4,3,2,1,0:T(8,128)(2,1)S(1)} %pad_maximum_fusion.27), channel_id=1, source_target_pairs={{0,1},{1,2},{2,3},{3,4},{4,5},{5,6},{6,7},{7,0},{8,9},{9,10},{10,1... | collective-permute-start | bytes 331784 | tf_op jit(solution)/shard_map/ppermute | solution.py:24
  233.2 4.1 %collective-permute-start.54 = (bf16[1,1,3,32,192]{4,3,2,1,0:T(8,128)(2,1)S(1)}, bf16[1,1,3,32,192]{4,3,2,1,0:T(8,128)(2,1)S(1)}, u32[]{:S(2)}, u32[]{:S(2)}) collective-permute-start(bf16[1,1,3,32,192]{4,3,2,1,0:T(8,128)(2,1)S(1)} %convert_bitcast_fusion), channel_id=1, source_target_pairs={{8,0},{16,8},{24,16},{0,24},{9,1},{17,9},{25,17},{1,25},{10,2},{18... | collective-permute-start | bytes 110600 | tf_op jit(solution)/shard_map/ppermute | solution.py:26
  234.2 5.0 %collective-permute-start.53 = (bf16[1,1,3,32,192]{4,3,2,1,0:T(8,128)(2,1)S(1)}, bf16[1,1,3,32,192]{4,3,2,1,0:T(8,128)(2,1)S(1)}, u32[]{:S(2)}, u32[]{:S(2)}) collective-permute-start(bf16[1,1,3,32,192]{4,3,2,1,0:T(8,128)(2,1)S(1)} %convert_bitcast_fusion), channel_id=1, source_target_pairs={{0,8},{8,16},{16,24},{24,0},{1,9},{9,17},{17,25},{25,1},{2,10},{10... | collective-permute-start | bytes 110600 | tf_op jit(solution)/shard_map/ppermute | solution.py:24
  239.3 4.1 %collective-permute-start.56 = (bf16[3,1,3,32,192]{4,3,2,1,0:T(8,128)(2,1)S(1)}, bf16[3,1,3,32,192]{4,3,2,1,0:T(8,128)(2,1)S(1)}, u32[]{:S(2)}, u32[]{:S(2)}) collective-permute-start(bf16[3,1,3,32,192]{4,3,2,1,0:T(8,128)(2,1)S(1)} %pad_maximum_fusion.28), channel_id=1, source_target_pairs={{1,0},{2,1},{3,2},{4,3},{5,4},{6,5},{7,6},{0,7},{9,8},{10,9},{11,1... | collective-permute-start | bytes 331784 | tf_op jit(solution)/shard_map/ppermute | solution.py:26
  239.3 6.4 %collective-permute-start.55 = (bf16[3,1,3,32,192]{4,3,2,1,0:T(8,128)(2,1)S(1)}, bf16[3,1,3,32,192]{4,3,2,1,0:T(8,128)(2,1)S(1)}, u32[]{:S(2)}, u32[]{:S(2)}) collective-permute-start(bf16[3,1,3,32,192]{4,3,2,1,0:T(8,128)(2,1)S(1)} %pad_maximum_fusion.28), channel_id=1, source_target_pairs={{0,1},{1,2},{2,3},{3,4},{4,5},{5,6},{6,7},{7,0},{8,9},{9,10},{10,1... | collective-permute-start | bytes 331784 | tf_op jit(solution)/shard_map/ppermute | solution.py:24
  249.0 4.1 %collective-permute-start.58 = (bf16[1,1,3,32,192]{4,3,2,1,0:T(8,128)(2,1)S(1)}, bf16[1,1,3,32,192]{4,3,2,1,0:T(8,128)(2,1)S(1)}, u32[]{:S(2)}, u32[]{:S(2)}) collective-permute-start(bf16[1,1,3,32,192]{4,3,2,1,0:T(8,128)(2,1)S(1)} %convert_bitcast_fusion.5), channel_id=1, source_target_pairs={{8,0},{16,8},{24,16},{0,24},{9,1},{17,9},{25,17},{1,25},{10,2},{18... | collective-permute-start | bytes 110600 | tf_op jit(solution)/shard_map/ppermute | solution.py:26
  250.1 5.0 %collective-permute-start.57 = (bf16[1,1,3,32,192]{4,3,2,1,0:T(8,128)(2,1)S(1)}, bf16[1,1,3,32,192]{4,3,2,1,0:T(8,128)(2,1)S(1)}, u32[]{:S(2)}, u32[]{:S(2)}) collective-permute-start(bf16[1,1,3,32,192]{4,3,2,1,0:T(8,128)(2,1)S(1)} %convert_bitcast_fusion.5), channel_id=1, source_target_pairs={{0,8},{8,16},{16,24},{24,0},{1,9},{9,17},{17,25},{25,1},{2,10},{10... | collective-permute-start | bytes 110600 | tf_op jit(solution)/shard_map/ppermute | solution.py:24
  255.2 6.4 %collective-permute-start.59 = (bf16[3,1,3,32,192]{4,3,2,1,0:T(8,128)(2,1)S(1)}, bf16[3,1,3,32,192]{4,3,2,1,0:T(8,128)(2,1)S(1)}, u32[]{:S(2)}, u32[]{:S(2)}) collective-permute-start(bf16[3,1,3,32,192]{4,3,2,1,0:T(8,128)(2,1)S(1)} %pad_maximum_fusion.29), channel_id=1, source_target_pairs={{0,1},{1,2},{2,3},{3,4},{4,5},{5,6},{6,7},{7,0},{8,9},{9,10},{10,1... | collective-permute-start | bytes 331784 | tf_op jit(solution)/shard_map/ppermute | solution.py:24
  264.9 4.1 %collective-permute-start.62 = (bf16[1,1,3,32,192]{4,3,2,1,0:T(8,128)(2,1)S(1)}, bf16[1,1,3,32,192]{4,3,2,1,0:T(8,128)(2,1)S(1)}, u32[]{:S(2)}, u32[]{:S(2)}) collective-permute-start(bf16[1,1,3,32,192]{4,3,2,1,0:T(8,128)(2,1)S(1)} %convert_bitcast_fusion.4), channel_id=1, source_target_pairs={{8,0},{16,8},{24,16},{0,24},{9,1},{17,9},{25,17},{1,25},{10,2},{18... | collective-permute-start | bytes 110600 | tf_op jit(solution)/shard_map/ppermute | solution.py:26
  265.1 5.0 %collective-permute-start.61 = (bf16[1,1,3,32,192]{4,3,2,1,0:T(8,128)(2,1)S(1)}, bf16[1,1,3,32,192]{4,3,2,1,0:T(8,128)(2,1)S(1)}, u32[]{:S(2)}, u32[]{:S(2)}) collective-permute-start(bf16[1,1,3,32,192]{4,3,2,1,0:T(8,128)(2,1)S(1)} %convert_bitcast_fusion.4), channel_id=1, source_target_pairs={{0,8},{8,16},{16,24},{24,0},{1,9},{9,17},{17,25},{25,1},{2,10},{10... | collective-permute-start | bytes 110600 | tf_op jit(solution)/shard_map/ppermute | solution.py:24
  270.1 4.1 %collective-permute-start.64 = (bf16[3,1,3,32,192]{4,3,2,1,0:T(8,128)(2,1)S(1)}, bf16[3,1,3,32,192]{4,3,2,1,0:T(8,128)(2,1)S(1)}, u32[]{:S(2)}, u32[]{:S(2)}) collective-permute-start(bf16[3,1,3,32,192]{4,3,2,1,0:T(8,128)(2,1)S(1)} %pad_maximum_fusion.30), channel_id=1, source_target_pairs={{1,0},{2,1},{3,2},{4,3},{5,4},{6,5},{7,6},{0,7},{9,8},{10,9},{11,1... | collective-permute-start | bytes 331784 | tf_op jit(solution)/shard_map/ppermute | solution.py:26
  270.2 6.4 %collective-permute-start.63 = (bf16[3,1,3,32,192]{4,3,2,1,0:T(8,128)(2,1)S(1)}, bf16[3,1,3,32,192]{4,3,2,1,0:T(8,128)(2,1)S(1)}, u32[]{:S(2)}, u32[]{:S(2)}) collective-permute-start(bf16[3,1,3,32,192]{4,3,2,1,0:T(8,128)(2,1)S(1)} %pad_maximum_fusion.30), channel_id=1, source_target_pairs={{0,1},{1,2},{2,3},{3,4},{4,5},{5,6},{6,7},{7,0},{8,9},{9,10},{10,1... | collective-permute-start | bytes 331784 | tf_op jit(solution)/shard_map/ppermute | solution.py:24
  279.8 4.1 %collective-permute-start.66 = (bf16[1,1,3,32,192]{4,3,2,1,0:T(8,128)(2,1)S(1)}, bf16[1,1,3,32,192]{4,3,2,1,0:T(8,128)(2,1)S(1)}, u32[]{:S(2)}, u32[]{:S(2)}) collective-permute-start(bf16[1,1,3,32,192]{4,3,2,1,0:T(8,128)(2,1)S(1)} %convert_bitcast_fusion.3), channel_id=1, source_target_pairs={{8,0},{16,8},{24,16},{0,24},{9,1},{17,9},{25,17},{1,25},{10,2},{18... | collective-permute-start | bytes 110600 | tf_op jit(solution)/shard_map/ppermute | solution.py:26
  280.8 5.0 %collective-permute-start.65 = (bf16[1,1,3,32,192]{4,3,2,1,0:T(8,128)(2,1)S(1)}, bf16[1,1,3,32,192]{4,3,2,1,0:T(8,128)(2,1)S(1)}, u32[]{:S(2)}, u32[]{:S(2)}) collective-permute-start(bf16[1,1,3,32,192]{4,3,2,1,0:T(8,128)(2,1)S(1)} %convert_bitcast_fusion.3), channel_id=1, source_target_pairs={{0,8},{8,16},{16,24},{24,0},{1,9},{9,17},{17,25},{25,1},{2,10},{10... | collective-permute-start | bytes 110600 | tf_op jit(solution)/shard_map/ppermute | solution.py:24
  285.8 4.1 %collective-permute-start.68 = (bf16[3,1,3,32,192]{4,3,2,1,0:T(8,128)(2,1)S(1)}, bf16[3,1,3,32,192]{4,3,2,1,0:T(8,128)(2,1)S(1)}, u32[]{:S(2)}, u32[]{:S(2)}) collective-permute-start(bf16[3,1,3,32,192]{4,3,2,1,0:T(8,128)(2,1)S(1)} %pad_maximum_fusion.31), channel_id=1, source_target_pairs={{1,0},{2,1},{3,2},{4,3},{5,4},{6,5},{7,6},{0,7},{9,8},{10,9},{11,1... | collective-permute-start | bytes 331784 | tf_op jit(solution)/shard_map/ppermute | solution.py:26
  285.9 6.4 %collective-permute-start.67 = (bf16[3,1,3,32,192]{4,3,2,1,0:T(8,128)(2,1)S(1)}, bf16[3,1,3,32,192]{4,3,2,1,0:T(8,128)(2,1)S(1)}, u32[]{:S(2)}, u32[]{:S(2)}) collective-permute-start(bf16[3,1,3,32,192]{4,3,2,1,0:T(8,128)(2,1)S(1)} %pad_maximum_fusion.31), channel_id=1, source_target_pairs={{0,1},{1,2},{2,3},{3,4},{4,5},{5,6},{6,7},{7,0},{8,9},{9,10},{10,1... | collective-permute-start | bytes 331784 | tf_op jit(solution)/shard_map/ppermute | solution.py:24
  308.2 4.6 %collective-permute-start.73 = (f32[32,32]{0,1:T(8,128)S(1)}, f32[32,32]{0,1:T(8,128)S(1)}, u32[]{:S(2)}, u32[]{:S(2)}) collective-permute-start(f32[32,32]{0,1:T(8,128)S(1)} %add.73), channel_id=1, source_target_pairs={{0,4},{1,5},{2,6},{3,7},{4,0},{5,1},{6,2},{7,3},{8,12},{9,13},{10,... | collective-permute-start | bytes 12296 | tf_op jit(solution)/shard_map/ppermute | solution.py:56
  (15 other events, 144.7 us)
